TPU v7x, 256 devices: a whole 4x4x8 slice. The times are simulated.
256 devices in a mesh: blk: 32 (over x_lo, z, core), tp: 8 (over y, x_hi).
Axes of the slice: x: 4 (x_hi: 2, x_lo: 2; x = x_hi * 2 + x_lo), y: 4, z: 8, core: 2. Of those that a mesh axis runs over, the one named last changes fastest.
Arguments:
- hidden_in: bfloat16 [12288, 4096], P('blk'), may hold values from -6 to 6
- w_query: bfloat16 [4096, 4096], P('blk', 'tp'), may hold values from -0.09375 to 0.09375
- w_key: bfloat16 [4096, 1024], P('blk', 'tp'), may hold values from -0.09375 to 0.09375
- w_value: bfloat16 [4096, 1024], P('blk', 'tp'), may hold values from -0.09375 to 0.09375
- starts: int32 [32], P('blk'), may hold values from 0 to 1152, as said below
- key_cache: bfloat16 [32, 1152, 1024], P('blk', None, 'tp'), may hold values from -400 to 400
- value_cache: bfloat16 [32, 1152, 1024], P('blk', None, 'tp'), may hold values from -6 to 6
- grad_out: bfloat16 [12288, 4096], P('blk', 'tp'), may hold values from -6 to 6
Outputs:
- attended: bfloat16 [12288, 4096], P('blk', 'tp')
- grad_in: bfloat16 [12288, 4096], P('blk', 'tp')
- grad_wq: float32 [4096, 4096], P('blk', 'tp')
- grad_wk: float32 [4096, 1024], P('blk', 'tp')
- grad_wv: float32 [4096, 1024], P('blk', 'tp')
Inputs may be any that keep to these rules, and one draw needn't show every extreme that they name: `starts`: every entry is a multiple of 384; both 0 and 1152 occur.
All inputs are finite; a program needn't handle non-finite values.
Results may differ from a plain program's by a relative error of at most 0.025.
The roundings to bfloat16 on the way count: a program that leaves them out, or rounds other values in their place, can miss the bound.
Values may be sent and summed in bfloat16 or wider, within the bound.
No kernel may reach another device: no remote copies, remote signals or barrier semaphores. Data moves between devices by JAX's collectives and lax.ppermute only.
A program may use at most 128 MiB of HBM per device.

v0:
```python
import jax
import jax.numpy as jnp
from jax import lax
from jax.sharding import PartitionSpec as P

H = 32
KV = 8
HD = 128


def contract_last(left, right):
    return lax.dot_general(
        left, right, (((1,), (1,)), ((), ())), preferred_element_type=jnp.float32
    )


def contract_first(left, right):
    return lax.dot_general(
        left, right, (((0,), (0,)), ((), ())), preferred_element_type=jnp.float32
    )


def head_pass(queries, cache_keys, cache_values, fresh_keys, fresh_values, grad_heads, offset):
    groups, row_count, head_width = queries.shape
    cached = cache_keys.shape[0]
    factor = head_width ** (-0.5)
    key_list = jnp.concatenate([cache_keys, fresh_keys], 0)
    value_list = jnp.concatenate([cache_values, fresh_values], 0)
    flat_query = queries.reshape(groups * row_count, head_width)
    flat_grad = grad_heads.reshape(groups * row_count, head_width)
    scores = contract_last(flat_query, key_list) * factor
    scores = scores.reshape(groups, row_count, cached + row_count)
    row_pos = lax.iota(jnp.int32, row_count)
    cache_ok = jnp.broadcast_to(lax.iota(jnp.int32, cached)[None, :] < offset, (row_count, cached))
    own_ok = row_pos[None, :] <= row_pos[:, None]
    allowed = jnp.concatenate([cache_ok, own_ok], 1)
    scores = jnp.where(allowed[None], scores, -jnp.inf)
    row_max = jnp.max(scores, axis=-1, keepdims=True)
    expo = jnp.exp(scores - row_max)
    probs = (expo / jnp.sum(expo, axis=-1, keepdims=True)).astype(jnp.bfloat16)
    probs = probs.reshape(groups * row_count, cached + row_count)
    attended = jnp.dot(probs, value_list, preferred_element_type=jnp.float32).astype(jnp.bfloat16)
    grad_probs = contract_last(flat_grad, value_list)
    probs_wide = probs.astype(jnp.float32)
    row_dot = jnp.sum(probs_wide * grad_probs, axis=-1, keepdims=True)
    grad_scores = (probs_wide * (grad_probs - row_dot) * factor).astype(jnp.bfloat16)
    grad_query = jnp.dot(grad_scores, key_list, preferred_element_type=jnp.float32).astype(
        jnp.bfloat16
    )
    grad_keys = contract_first(grad_scores[:, cached:], flat_query).astype(jnp.bfloat16)
    grad_values = contract_first(probs[:, cached:], flat_grad).astype(jnp.bfloat16)
    return (
        attended.reshape(groups, row_count, head_width),
        grad_query.reshape(groups, row_count, head_width),
        grad_keys,
        grad_values,
    )


def local(hidden_in, w_query, w_key, w_value, starts, key_cache, value_cache, grad_out):
    tokens_dev = hidden_in.shape[0]
    kv_local = w_key.shape[1] // HD
    group = H // KV
    cached = key_cache.shape[1]
    full_query, full_key, full_value = (
        lax.all_gather(w_query, "blk", axis=0, tiled=True),
        lax.all_gather(w_key, "blk", axis=0, tiled=True),
        lax.all_gather(w_value, "blk", axis=0, tiled=True),
    )
    proj_query = jnp.dot(hidden_in, full_query, preferred_element_type=jnp.float32)
    proj_key = jnp.dot(hidden_in, full_key, preferred_element_type=jnp.float32)
    proj_value = jnp.dot(hidden_in, full_value, preferred_element_type=jnp.float32)
    queries = proj_query.astype(jnp.bfloat16)
    new_keys = proj_key.astype(jnp.bfloat16)
    new_values = proj_value.astype(jnp.bfloat16)
    per_query = queries.reshape(tokens_dev, kv_local, group, HD).transpose(1, 2, 0, 3)
    per_grad = grad_out.reshape(tokens_dev, kv_local, group, HD).transpose(1, 2, 0, 3)
    cache_k = key_cache[0].reshape(cached, kv_local, HD).transpose(1, 0, 2)
    cache_v = value_cache[0].reshape(cached, kv_local, HD).transpose(1, 0, 2)
    fresh_k = new_keys.reshape(tokens_dev, kv_local, HD).transpose(1, 0, 2)
    fresh_v = new_values.reshape(tokens_dev, kv_local, HD).transpose(1, 0, 2)
    offset = starts[0]
    results = lax.map(
        lambda packed: head_pass(*packed, offset),
        (per_query, cache_k, cache_v, fresh_k, fresh_v, per_grad),
    )
    attended = results[0].transpose(2, 0, 1, 3).reshape(tokens_dev, kv_local * group * HD)
    grad_query = results[1].transpose(2, 0, 1, 3).reshape(tokens_dev, kv_local * group * HD)
    grad_keys = results[2].transpose(1, 0, 2).reshape(tokens_dev, kv_local * HD)
    grad_values = results[3].transpose(1, 0, 2).reshape(tokens_dev, kv_local * HD)
    input_term = (
        contract_last(grad_query, full_query)
        + contract_last(grad_keys, full_key)
        + contract_last(grad_values, full_value)
    )
    grad_in = lax.psum_scatter(input_term, "tp", scatter_dimension=1, tiled=True).astype(
        jnp.bfloat16
    )
    grads_cat = jnp.concatenate([grad_query, grad_keys, grad_values], 1)
    blk_count = lax.axis_size("blk")
    summed = lax.psum_scatter(
        contract_first(hidden_in, grads_cat), "blk", scatter_dimension=0, tiled=True
    )
    summed = summed * (tokens_dev * blk_count) ** (-0.5)
    query_cols = w_query.shape[1]
    kv_cols = w_key.shape[1]
    grad_wq = summed[:, :query_cols]
    grad_wk = summed[:, query_cols : query_cols + kv_cols]
    grad_wv = summed[:, query_cols + kv_cols :]
    return (attended, grad_in, grad_wq, grad_wk, grad_wv)


def solution(mesh):
    in_specs = (
        P("blk", None),
        P("blk", "tp"),
        P("blk", "tp"),
        P("blk", "tp"),
        P("blk"),
        P("blk", None, "tp"),
        P("blk", None, "tp"),
        P("blk", "tp"),
    )
    out_specs = (P("blk", "tp"), P("blk", "tp"), P("blk", "tp"), P("blk", "tp"), P("blk", "tp"))
    return jax.shard_map(local, mesh=mesh, in_specs=in_specs, out_specs=out_specs, check_vma=False)
```

profile of v0, /device:TPU:1, one launch (start us, length us, event | category | flops | bytes accessed | tf_op | source)
XLA Modules:
  0.0 501.1 jit_solution(6510871509543316294)
XLA Ops:
  7.2 0.0 copy-start
  7.2 0.0 all-gather.8.cloned.1.call-start
  7.2 0.7 all-gather.8.cloned.1.call-update
  7.9 0.0 all-gather.6.cloned.1.call-start
  8.0 0.7 all-gather.6.cloned.1.call-update
  8.7 0.0 all-gather.4.cloned.1.call-start
  8.7 0.7 all-gather.4.cloned.1.call-update
  9.4 0.0 reduce-scatter.3.cloned.1.call-start
  10.1 1.2 copy.27
  11.3 0.9 copy.28
  12.3 0.3 pad_add_fusion
  12.6 2.2 broadcast_in_dim.55
  14.8 2.6 copy.33
  17.4 60.1 %all-gather.8.cloned.1.call-done = bf16[4096,128]{1,0:T(8,128)(2,1)} async-done(((bf16[128,128]{1,0:T(8,128)(2,1)}), bf16[4096,128]{1,0:T(8,128)(2,1)}) %all-gather.8.cloned.1.call-update) | async-done | bytes 1048592 | tf_op jit(solution)/shard_map/all_gather | solution.py:68
  77.6 0.0 copy-done
  77.6 2.8 convolution_convert_fusion.3
  80.4 62.3 %all-gather.6.cloned.1.call-done = bf16[4096,128]{1,0:T(8,128)(2,1)} async-done(((bf16[128,128]{1,0:T(8,128)(2,1)}), bf16[4096,128]{1,0:T(8,128)(2,1)}) %all-gather.6.cloned.1.call-update) | async-done | bytes 1048592 | tf_op jit(solution)/shard_map/all_gather | solution.py:67
  142.7 2.8 convolution_convert_fusion.4
  145.6 65.3 %all-gather.4.cloned.1.call-done = bf16[4096,512]{1,0:T(8,128)(2,1)} async-done(((bf16[128,512]{1,0:T(8,128)(2,1)}), bf16[4096,512]{1,0:T(8,128)(2,1)}) %all-gather.4.cloned.1.call-update) | async-done | bytes 4194320 | tf_op jit(solution)/shard_map/all_gather | solution.py:66
  210.9 4.7 convolution_convert_fusion.2
  215.6 1.1 reshape.70
  216.7 0.1 copy.25
  216.7 3.6 fusion.27
  220.3 0.0 copy-start.6
  220.3 0.0 copy-start.7
  220.3 0.0 copy-start.11
  220.4 1.3 fusion.4
  221.7 0.0 copy-done.6
  221.7 0.0 copy-done.7
  221.7 0.0 copy-done.11
  221.7 5.0 %fusion.1 = (f32[1536]{0:T(1024)S(1)}, bf16[1536,1536]{0,1:T(8,128)(2,1)S(1)}, f32[1536,1536]{1,0:T(8,128)}) fusion(f32[1536]{0:T(1024)S(1)} %fusion.4, f32[1536,1536]{0,1:T(8,128)S(1)} %get-tuple-element.61, f32[1536]{0:T(1024)S(1)} %get-tuple-element.60, bf16[1536,128]{1,0:T(8,128)(2,1)S(1)} %bitcast.60, bf16[384,128]{1,0:T(8,128)(2,1)S(1)} %copy-done.7, ...), kind=kOutput, calls=%fused_computation.4 | convolution fusion | flops 618920448 | bytes 24397824 | tf_op jit(solution)/shard_map/while/body/eval_jaxpr/dot_general | solution.py:12
  226.8 1.5 fusion.12
  228.3 8.0 %fusion.3 = bf16[1536,1536]{0,1:T(8,128)(2,1)} fusion(bf16[1536,1536]{0,1:T(8,128)(2,1)S(1)} %get-tuple-element.57, f32[1536,1536]{1,0:T(8,128)} %get-tuple-element.62, f32[1536]{0:T(1024)S(1)} %get-tuple-element.56), kind=kLoop, calls=%fused_computation.6 | loop fusion | flops 11796480 | bytes 18880512 | tf_op jit(solution)/shard_map/while/body/eval_jaxpr/convert_element_type | solution.py:46
  236.3 0.0 copy-done.1
  236.3 2.4 fusion.9
  238.7 0.0 copy-done.9
  238.7 0.0 copy-done.10
  238.7 4.5 convolution_convert_fusion
  243.2 1.2 copy.29
  244.5 0.0 copy-start.3
  244.5 0.0 copy-start.4
  244.5 4.1 fusion.28
  248.6 0.0 copy-done.3
  248.6 0.0 copy-done.4
  248.6 0.0 copy-start.2
  248.6 1.0 fusion.29
  249.7 0.2 copy-done.2
  249.9 3.7 add_add_fusion
  253.6 0.0 reduce-scatter.3.cloned.1.call-update
  253.6 0.0 reduce-scatter.5.cloned.1.call-start
  253.6 7.3 %convolution_bitcast_fusion = f32[4096,768]{0,1:T(8,128)} fusion(bf16[384,4096]{1,0:T(8,128)(2,1)S(1)} %copy-done, bf16[384,128]{0,1:T(8,128)(2,1)} %fusion.12, bf16[384,128]{0,1:T(8,128)(2,1)} %fusion.9, bf16[384,512]{0,1:T(8,128)(2,1)S(1)} %bitcast.56), kind=kOutput, calls=%fused_computation.11 | convolution fusion | flops 2417688576 | bytes 16318464 | tf_op jit(solution)/shard_map/dot_general | solution.py:18
  261.0 0.0 reduce-scatter.5.cloned.1.call-update
  261.0 0.9 copy-done.8
  261.9 0.1 copy-done.12
  262.0 3.8 convolution_convert_fusion.1
  265.7 0.3 copy.26
  266.1 0.8 copy.36
  266.9 89.1 %reduce-scatter.3.cloned.1.call-done = f32[384,512]{1,0:T(8,128)} async-done(((f32[384,4096]{1,0:T(8,128)}), f32[384,512]{1,0:T(8,128)}) %reduce-scatter.3.cloned.1.call-update) | async-done | bytes 786448 | tf_op jit(solution)/shard_map/reduce_scatter | solution.py:96
  355.9 1.9 convert_element_type.51
  357.8 133.4 %reduce-scatter.5.cloned.1.call-done = f32[128,768]{0,1:T(8,128)} async-done(((f32[4096,768]{0,1:T(8,128)}), f32[128,768]{0,1:T(8,128)}) %reduce-scatter.5.cloned.1.call-update) | async-done | bytes 393232 | tf_op jit(solution)/shard_map/reduce_scatter | solution.py:101
  491.2 1.0 broadcast_multiply_fusion
  492.3 0.8 copy.30
  493.1 0.7 copy.32
  493.9 0.7 copy.31
  (12 shorter events, 0.1 us)
Async XLA Ops:
  7.2 70.4 %copy-start = (bf16[384,4096]{1,0:T(8,128)(2,1)S(1)}, bf16[384,4096]{1,0:T(8,128)(2,1)}, u32[]{:S(2)}) copy-start(bf16[384,4096]{1,0:T(8,128)(2,1)} %param.8) | copy-start | bytes 9437188
  7.2 70.4 %all-gather.8.cloned.1.call-start = ((), (), s32[]{:S(2)}) async-start(), calls=%async_computation.4 | async-start | bytes 1081344 | tf_op jit(solution)/shard_map/all_gather | solution.py:68
  7.9 134.8 %all-gather.6.cloned.1.call-start = ((), (), s32[]{:S(2)}) async-start(), calls=%async_computation.3 | async-start | bytes 1081344 | tf_op jit(solution)/shard_map/all_gather | solution.py:67
  8.7 202.2 %all-gather.4.cloned.1.call-start = ((), (), s32[]{:S(2)}) async-start(), calls=%async_computation.2 | async-start | bytes 4325376 | tf_op jit(solution)/shard_map/all_gather | solution.py:66
  9.4 346.5 %reduce-scatter.3.cloned.1.call-start = ((), (), s32[]{:S(2)}) async-start(), calls=%async_computation.5 | async-start | bytes 7077888 | tf_op jit(solution)/shard_map/reduce_scatter | solution.py:96
  220.3 1.4 copy-start.6
  220.3 1.4 copy-start.7
  220.3 1.4 copy-start.11
  226.8 9.6 %copy-start.1 = (bf16[1536,1536]{0,1:T(8,128)(2,1)}, bf16[1536,1536]{0,1:T(8,128)(2,1)S(1)}, u32[]{:S(2)}) copy-start(bf16[1536,1536]{0,1:T(8,128)(2,1)S(1)} %get-tuple-element.57) | copy-start | bytes 14155780
  228.3 10.4 %copy-start.9 = (bf16[384,128]{1,0:T(8,128)(2,1)S(1)}, bf16[384,128]{1,0:T(8,128)(2,1)}, u32[]{:S(2)}) copy-start(bf16[384,128]{1,0:T(8,128)(2,1)} %convolution_convert_fusion.4) | copy-start | bytes 294916
  228.3 10.4 %copy-start.10 = (bf16[1,1152,128]{2,1,0:T(8,128)(2,1)S(1)}, bf16[1,1152,128]{2,1,0:T(8,128)(2,1)}, u32[]{:S(2)}) copy-start(bf16[1,1152,128]{2,1,0:T(8,128)(2,1)} %param.13) | copy-start | bytes 884740
  244.5 4.2 copy-start.3
  244.5 4.2 copy-start.4
  248.6 1.2 copy-start.2
  248.6 1.2 copy-start.5
  253.6 237.6 %reduce-scatter.5.cloned.1.call-start = ((), (), s32[]{:S(2)}) async-start(), calls=%async_computation.6 | async-start | bytes 12976128 | tf_op jit(solution)/shard_map/reduce_scatter | solution.py:101
  261.0 0.9 copy-start.8
  261.0 1.0 copy-start.12
Sparse Core Ops, SparseCore 0:
  9.8 67.6 all-gather.7
  79.4 63.2 all-gather.5
  144.6 66.2 all-gather.3
  253.7 102.1 reduce-scatter.2
  358.3 132.8 reduce-scatter.4
where the time goes:
time: 505 us; the launch traced here: 501 us
  waiting for transfers between devices  412 us (82%)
  matrix products  47.4 us (9%)
  between operations  14.6 us (3%)
  local copies, waits for them, and re-layouts  14 us (3%)
  other arithmetic  12.6 us (2%)
    reduce_scatter x1, waiting for transfers between devices, local(): lax.psum_scatter(contract_first(hidden_in, grads_cat), 'blk', scatter_dim...  133 us
    reduce_scatter x1, waiting for transfers between devices, local(): lax.psum_scatter(input_term, 'tp', scatter_dimension=1, tiled=True)  89.1 us
    all_gather x1, waiting for transfers between devices, local(): lax.all_gather(w_query, 'blk', axis=0, tiled=True)  65.3 us
    all_gather x1, waiting for transfers between devices, local(): lax.all_gather(w_key, 'blk', axis=0, tiled=True)  62.3 us
    all_gather x1, waiting for transfers between devices, local(): lax.all_gather(w_value, 'blk', axis=0, tiled=True)  60.1 us
    dot_general x5, matrix products, contract_last(): lax.dot_general(left, right, (((1,), (1,)), ((), ())), preferred_element_...  17.5 us
    dot_general x3, matrix products, contract_first(): lax.dot_general(left, right, (((0,), (0,)), ((), ())), preferred_element_...  11.3 us
  transfers between devices with their start and end apart: 5, of which 5 were waited for; matrix products, arithmetic and copies ran while one was open for 5% of the time, Pallas kernels for 0%

commit v1 on v0

--- a/solution.py
+++ b/solution.py
@@ -62,17 +62,14 @@
     kv_local = w_key.shape[1] // HD
     group = H // KV
     cached = key_cache.shape[1]
-    full_query, full_key, full_value = (
-        lax.all_gather(w_query, "blk", axis=0, tiled=True),
-        lax.all_gather(w_key, "blk", axis=0, tiled=True),
-        lax.all_gather(w_value, "blk", axis=0, tiled=True),
-    )
-    proj_query = jnp.dot(hidden_in, full_query, preferred_element_type=jnp.float32)
-    proj_key = jnp.dot(hidden_in, full_key, preferred_element_type=jnp.float32)
-    proj_value = jnp.dot(hidden_in, full_value, preferred_element_type=jnp.float32)
-    queries = proj_query.astype(jnp.bfloat16)
-    new_keys = proj_key.astype(jnp.bfloat16)
-    new_values = proj_value.astype(jnp.bfloat16)
+    query_cols = w_query.shape[1]
+    kv_cols = w_key.shape[1]
+    local_w = jnp.concatenate([w_query, w_key, w_value], 1)
+    full_w = lax.all_gather(local_w, "blk", axis=0, tiled=True)
+    proj = jnp.dot(hidden_in, full_w, preferred_element_type=jnp.float32)
+    queries = proj[:, :query_cols].astype(jnp.bfloat16)
+    new_keys = proj[:, query_cols : query_cols + kv_cols].astype(jnp.bfloat16)
+    new_values = proj[:, query_cols + kv_cols :].astype(jnp.bfloat16)
     per_query = queries.reshape(tokens_dev, kv_local, group, HD).transpose(1, 2, 0, 3)
     per_grad = grad_out.reshape(tokens_dev, kv_local, group, HD).transpose(1, 2, 0, 3)
     cache_k = key_cache[0].reshape(cached, kv_local, HD).transpose(1, 0, 2)
@@ -88,22 +85,16 @@
     grad_query = results[1].transpose(2, 0, 1, 3).reshape(tokens_dev, kv_local * group * HD)
     grad_keys = results[2].transpose(1, 0, 2).reshape(tokens_dev, kv_local * HD)
     grad_values = results[3].transpose(1, 0, 2).reshape(tokens_dev, kv_local * HD)
-    input_term = (
-        contract_last(grad_query, full_query)
-        + contract_last(grad_keys, full_key)
-        + contract_last(grad_values, full_value)
-    )
+    grads_cat = jnp.concatenate([grad_query, grad_keys, grad_values], 1)
+    input_term = contract_last(grads_cat, full_w)
     grad_in = lax.psum_scatter(input_term, "tp", scatter_dimension=1, tiled=True).astype(
         jnp.bfloat16
     )
-    grads_cat = jnp.concatenate([grad_query, grad_keys, grad_values], 1)
     blk_count = lax.axis_size("blk")
     summed = lax.psum_scatter(
         contract_first(hidden_in, grads_cat), "blk", scatter_dimension=0, tiled=True
     )
     summed = summed * (tokens_dev * blk_count) ** (-0.5)
-    query_cols = w_query.shape[1]
-    kv_cols = w_key.shape[1]
     grad_wq = summed[:, :query_cols]
     grad_wk = summed[:, query_cols : query_cols + kv_cols]
     grad_wv = summed[:, query_cols + kv_cols :]

time: 505 us -> 381 us (0.75)
  waiting for transfers between devices: 412 us -> 290 us
  matrix products: 47.4 us -> 42.1 us
    all_gather x3 -> x1, waiting for transfers between devices: 188 us -> 66.7 us  [local(): full_w = lax.all_gather(local_w, 'blk', axis=0, tiled=True)]
    dot_general x3 -> x1, matrix products: 10.4 us -> 5.65 us  [local(): proj = jnp.dot(hidden_in, full_w, preferred_element_type=jnp.float32)]
    dot_general x5 -> x3, matrix products: 17.5 us -> 16.9 us  [contract_last(): lax.dot_general(left, right, (((1,), (1,)), ((), ())), preferred_element_...]
  transfers between devices with their start and end apart: 5 -> 3, of which waited for: 5 -> 3; matrix products, arithmetic and copies ran while one was open for 5% -> 6% of each run, Pallas kernels for 0% -> 0%
where the time goes in v1:
time: 381 us; the launch traced here: 377 us
  waiting for transfers between devices  290 us (76%)
  matrix products  42.1 us (11%)
  local copies, waits for them, and re-layouts  16.3 us (4%)
  between operations  14.5 us (4%)
  other arithmetic  14.3 us (4%)
    reduce_scatter x1, waiting for transfers between devices, local(): lax.psum_scatter(contract_first(hidden_in, grads_cat), 'blk', scatter_dim...  134 us
    reduce_scatter x1, waiting for transfers between devices, local(): lax.psum_scatter(input_term, 'tp', scatter_dimension=1, tiled=True)  89.2 us
    all_gather x1, waiting for transfers between devices, local(): full_w = lax.all_gather(local_w, 'blk', axis=0, tiled=True)  66.7 us
    dot_general x3, matrix products, contract_last(): lax.dot_general(left, right, (((1,), (1,)), ((), ())), preferred_element_...  16.9 us
    dot_general x3, matrix products, contract_first(): lax.dot_general(left, right, (((0,), (0,)), ((), ())), preferred_element_...  11.2 us
    convert_element_type x1, other arithmetic, head_pass(): (probs_wide * (grad_probs - row_dot) * factor).astype(jnp.bfloat16)  7.93 us
    unnamed x24, local copies, waits for them, and re-layouts  7.92 us
  transfers between devices with their start and end apart: 3, of which 3 were waited for; matrix products, arithmetic and copies ran while one was open for 6% of the time, Pallas kernels for 0%

profile of v1, /device:TPU:1, one launch (start us, length us, event | category | flops | bytes accessed | tf_op | source)
XLA Modules:
  0.0 377.2 jit_solution(8844071087340533991)
XLA Ops:
  7.2 0.0 copy-start
  7.2 0.0 all-gather.2.cloned.1.call-start
  7.2 1.8 pad_maximum_fusion.9
  9.0 0.0 all-gather.2.cloned.1.call-update
  9.0 0.0 reduce-scatter.3.cloned.1.call-start
  9.7 1.2 copy.33
  10.9 0.9 copy.34
  11.9 0.3 pad_add_fusion
  12.2 2.2 broadcast_in_dim.55
  14.5 2.6 copy.39
  17.0 66.7 %all-gather.2.cloned.1.call-done = bf16[4096,768]{1,0:T(8,128)(2,1)} async-done(((bf16[128,768]{1,0:T(8,128)(2,1)}), bf16[4096,768]{1,0:T(8,128)(2,1)}) %all-gather.2.cloned.1.call-update) | async-done | bytes 6291472 | tf_op jit(solution)/shard_map/all_gather | solution.py:68
  83.7 0.0 copy-done
  83.7 5.6 %fusion.5 = bf16[384,768]{0,1:T(8,128)(2,1)S(1)} fusion(bf16[4096,768]{1,0:T(8,128)(2,1)} %all-gather.2.cloned.1.call-done, bf16[384,4096]{1,0:T(8,128)(2,1)S(1)} %copy-done), kind=kOutput, calls=%fused_computation.16 | convolution fusion | flops 2416214016 | bytes 10027008 | tf_op jit(solution)/shard_map/dot_general | solution.py:69
  89.4 0.7 fusion.24
  90.1 0.9 copy.29
  91.0 1.0 copy.30
  92.0 1.0 copy.31
  93.1 0.0 copy-start.4
  93.1 3.7 fusion.26
  96.7 0.0 copy-start.2
  96.7 0.0 copy-start.7
  96.8 1.3 fusion.4
  98.1 0.0 copy-done.4
  98.1 0.0 copy-done.2
  98.1 0.0 copy-done.7
  98.1 5.1 %fusion.1 = (f32[1536]{0:T(1024)S(1)}, bf16[1536,1536]{0,1:T(8,128)(2,1)S(1)}, f32[1536,1536]{1,0:T(8,128)}) fusion(f32[1536]{0:T(1024)S(1)} %fusion.4, f32[1536,1536]{0,1:T(8,128)S(1)} %get-tuple-element.63, f32[1536]{0:T(1024)S(1)} %get-tuple-element.62, bf16[1536,128]{1,0:T(8,128)(2,1)S(1)} %bitcast.55, bf16[384,128]{1,0:T(8,128)(2,1)S(1)} %copy.31, ...), kind=kOutput, calls=%fused_computation.4 | convolution fusion | flops 618920448 | bytes 24397824 | tf_op jit(solution)/shard_map/while/body/eval_jaxpr/dot_general | solution.py:12
  103.2 0.0 copy-start.1
  103.2 1.5 fusion.13
  104.7 0.0 copy-start.3
  104.7 0.0 copy-start.6
  104.7 7.9 %fusion.3 = bf16[1536,1536]{0,1:T(8,128)(2,1)} fusion(bf16[1536,1536]{0,1:T(8,128)(2,1)S(1)} %get-tuple-element.57, f32[1536,1536]{1,0:T(8,128)} %get-tuple-element.64, f32[1536]{0:T(1024)S(1)} %get-tuple-element.56), kind=kLoop, calls=%fused_computation.6 | loop fusion | flops 11796480 | bytes 18880512 | tf_op jit(solution)/shard_map/while/body/eval_jaxpr/convert_element_type | solution.py:46
  112.7 0.0 copy-done.1
  112.7 0.0 copy-done.3
  112.7 2.4 fusion.10
  115.1 0.0 copy-done.6
  115.1 4.5 %convolution_convert_fusion = bf16[1536,128]{1,0:T(8,128)(2,1)} fusion(bf16[1536,1536]{0,1:T(8,128)(2,1)} %fusion.3, bf16[384,128]{1,0:T(8,128)(2,1)S(1)} %copy.30, bf16[1152,128]{1,0:T(8,128)(2,1)S(1)} %bitcast.63), kind=kOutput, calls=%fused_computation.12 | convolution fusion | flops 604962816 | bytes 5505024 | tf_op jit(solution)/shard_map/while/body/eval_jaxpr/dot_general | solution.py:47
  119.6 1.2 copy.35
  120.8 8.2 %fusion.17 = f32[384,4096]{1,0:T(8,128)} fusion(bf16[4096,768]{1,0:T(8,128)(2,1)} %all-gather.2.cloned.1.call-done, bf16[384,128]{0,1:T(8,128)(2,1)} %fusion.13, bf16[384,128]{0,1:T(8,128)(2,1)} %fusion.10, bf16[384,512]{0,1:T(8,128)(2,1)S(1)} %bitcast.53), kind=kOutput, calls=%fused_computation.29 | convolution fusion | flops 2417688576 | bytes 13172736 | tf_op jit(solution)/shard_map/dot_general | solution.py:12
  129.0 0.0 reduce-scatter.3.cloned.1.call-update
  129.0 0.0 reduce-scatter.5.cloned.1.call-start
  129.1 7.3 %convolution_bitcast_fusion = f32[4096,768]{0,1:T(8,128)} fusion(bf16[384,4096]{1,0:T(8,128)(2,1)S(1)} %copy-done, bf16[384,128]{0,1:T(8,128)(2,1)} %fusion.13, bf16[384,128]{0,1:T(8,128)(2,1)} %fusion.10, bf16[384,512]{0,1:T(8,128)(2,1)S(1)} %bitcast.54), kind=kOutput, calls=%fused_computation.11 | convolution fusion | flops 2417688576 | bytes 16318464 | tf_op jit(solution)/shard_map/dot_general | solution.py:18
  136.4 0.0 copy-start.5
  136.4 0.0 copy-start.8
  136.4 0.0 reduce-scatter.5.cloned.1.call-update
  136.4 0.9 copy-done.5
  137.2 0.1 copy-done.8
  137.4 3.8 convolution_convert_fusion.1
  141.1 0.3 copy.32
  141.5 0.8 copy.42
  142.3 89.2 %reduce-scatter.3.cloned.1.call-done = f32[384,512]{1,0:T(8,128)} async-done(((f32[384,4096]{1,0:T(8,128)}), f32[384,512]{1,0:T(8,128)}) %reduce-scatter.3.cloned.1.call-update) | async-done | bytes 786448 | tf_op jit(solution)/shard_map/reduce_scatter | solution.py:90
  231.5 1.9 convert_element_type.42
  233.4 133.9 %reduce-scatter.5.cloned.1.call-done = f32[128,768]{0,1:T(8,128)} async-done(((f32[4096,768]{0,1:T(8,128)}), f32[128,768]{0,1:T(8,128)}) %reduce-scatter.5.cloned.1.call-update) | async-done | bytes 393232 | tf_op jit(solution)/shard_map/reduce_scatter | solution.py:94
  367.3 1.0 broadcast_multiply_fusion
  368.3 0.8 copy.36
  369.2 0.7 copy.38
  369.9 0.7 copy.37
  (6 shorter events, 0.1 us)
Async XLA Ops:
  7.2 76.5 %copy-start = (bf16[384,4096]{1,0:T(8,128)(2,1)S(1)}, bf16[384,4096]{1,0:T(8,128)(2,1)}, u32[]{:S(2)}) copy-start(bf16[384,4096]{1,0:T(8,128)(2,1)} %param.8) | copy-start | bytes 9437188
  7.2 76.5 %all-gather.2.cloned.1.call-start = ((), (), s32[]{:S(2)}) async-start(), calls=%async_computation.2 | async-start | bytes 6488064 | tf_op jit(solution)/shard_map/all_gather | solution.py:68
  9.0 222.5 %reduce-scatter.3.cloned.1.call-start = ((), (), s32[]{:S(2)}) async-start(), calls=%async_computation.3 | async-start | bytes 7077888 | tf_op jit(solution)/shard_map/reduce_scatter | solution.py:90
  93.1 5.0 %copy-start.4 = (bf16[384,128]{1,0:T(8,128)(2,1)}, bf16[384,128]{1,0:T(8,128)(2,1)S(1)}, u32[]{:S(2)}) copy-start(bf16[384,128]{1,0:T(8,128)(2,1)S(1)} %copy.31) | copy-start | bytes 294916
  96.7 1.4 copy-start.2
  96.7 1.4 copy-start.7
  103.2 9.5 %copy-start.1 = (bf16[1536,1536]{0,1:T(8,128)(2,1)}, bf16[1536,1536]{0,1:T(8,128)(2,1)S(1)}, u32[]{:S(2)}) copy-start(bf16[1536,1536]{0,1:T(8,128)(2,1)S(1)} %get-tuple-element.57) | copy-start | bytes 14155780
  104.7 7.9 %copy-start.3 = (bf16[384,1,4,128]{3,0,2,1:T(8,128)(2,1)S(1)}, bf16[384,1,4,128]{3,0,2,1:T(8,128)(2,1)}, u32[]{:S(2)}) copy-start(bf16[384,1,4,128]{3,0,2,1:T(8,128)(2,1)} %copy.29) | copy-start | bytes 1179652
  104.7 10.3 %copy-start.6 = (bf16[1,1152,128]{2,1,0:T(8,128)(2,1)S(1)}, bf16[1,1152,128]{2,1,0:T(8,128)(2,1)}, u32[]{:S(2)}) copy-start(bf16[1,1152,128]{2,1,0:T(8,128)(2,1)} %param.13) | copy-start | bytes 884740
  129.0 238.2 %reduce-scatter.5.cloned.1.call-start = ((), (), s32[]{:S(2)}) async-start(), calls=%async_computation.4 | async-start | bytes 12976128 | tf_op jit(solution)/shard_map/reduce_scatter | solution.py:94
  136.4 0.9 copy-start.5
  136.4 1.0 copy-start.8
Sparse Core Ops, SparseCore 0:
  10.4 73.2 all-gather.1
  129.1 102.2 reduce-scatter.2
  234.0 133.1 reduce-scatter.4

commit v2 on v1

--- a/solution.py
+++ b/solution.py
@@ -86,14 +86,15 @@
     grad_keys = results[2].transpose(1, 0, 2).reshape(tokens_dev, kv_local * HD)
     grad_values = results[3].transpose(1, 0, 2).reshape(tokens_dev, kv_local * HD)
     grads_cat = jnp.concatenate([grad_query, grad_keys, grad_values], 1)
-    input_term = contract_last(grads_cat, full_w)
-    grad_in = lax.psum_scatter(input_term, "tp", scatter_dimension=1, tiled=True).astype(
-        jnp.bfloat16
-    )
     blk_count = lax.axis_size("blk")
-    summed = lax.psum_scatter(
-        contract_first(hidden_in, grads_cat), "blk", scatter_dimension=0, tiled=True
-    )
+    tp_count = lax.axis_size("tp")
+    weight_term = contract_first(hidden_in, grads_cat).astype(jnp.bfloat16)
+    summed = lax.psum_scatter(weight_term, "blk", scatter_dimension=0, tiled=True)
+    summed = summed.astype(jnp.float32)
+    input_term = contract_last(grads_cat, full_w).astype(jnp.bfloat16)
+    input_term = input_term.reshape(tokens_dev, tp_count, -1).transpose(1, 0, 2)
+    gathered = lax.all_to_all(input_term, "tp", 0, 0, tiled=True)
+    grad_in = jnp.sum(gathered.astype(jnp.float32), axis=0).astype(jnp.bfloat16)
     summed = summed * (tokens_dev * blk_count) ** (-0.5)
     grad_wq = summed[:, :query_cols]
     grad_wk = summed[:, query_cols : query_cols + kv_cols]

time: 381 us -> 275 us (0.72)
  waiting for transfers between devices: 290 us -> 170 us
  local copies, waits for them, and re-layouts: 16.3 us -> 27.1 us
  starting transfers between devices: 0.12 us -> 6.44 us
    reduce_scatter x2 -> x0, waiting for transfers between devices: 223 us -> none  [the longest x1 134 us: local(): lax.psum_scatter(contract_first(hidden_in, grads_cat), 'blk', scatter_dim...]
    unnamed x3, waiting for transfers between devices: 0.05 us -> 57.1 us
    all_to_all x0 -> x1, waiting for transfers between devices: none -> 45.9 us  [local(): gathered = lax.all_to_all(input_term, 'tp', 0, 0, tiled=True)]
    unnamed x24 -> x26, local copies, waits for them, and re-layouts: 7.92 us -> 16.7 us
    all_to_all x0 -> x1, starting transfers between devices: none -> 6.36 us  [local(): gathered = lax.all_to_all(input_term, 'tp', 0, 0, tiled=True)]
  transfers between devices with their start and end apart: 3 -> 3, of which waited for: 3 -> 3; matrix products, arithmetic and copies ran while one was open for 6% -> 9% of each run, Pallas kernels for 0% -> 0%
where the time goes in v2:
time: 275 us; the launch traced here: 271 us
  waiting for transfers between devices  170 us (62%)
  matrix products  38.6 us (14%)
  local copies, waits for them, and re-layouts  27.1 us (10%)
  between operations  14.9 us (5%)
  other arithmetic  14.6 us (5%)
  starting transfers between devices  6.44 us (2%)
    all_gather x1, waiting for transfers between devices, local(): full_w = lax.all_gather(local_w, 'blk', axis=0, tiled=True)  66.6 us
    unnamed x3, waiting for transfers between devices  57.1 us
    all_to_all x1, waiting for transfers between devices, local(): gathered = lax.all_to_all(input_term, 'tp', 0, 0, tiled=True)  45.9 us
    unnamed x26, local copies, waits for them, and re-layouts  16.7 us
    dot_general x3, matrix products, contract_last(): lax.dot_general(left, right, (((1,), (1,)), ((), ())), preferred_element_...  14.3 us
    dot_general x3, matrix products, contract_first(): lax.dot_general(left, right, (((0,), (0,)), ((), ())), preferred_element_...  10.3 us
    convert_element_type x1, other arithmetic, head_pass(): (probs_wide * (grad_probs - row_dot) * factor).astype(jnp.bfloat16)  7.93 us
    all_to_all x1, starting transfers between devices, local(): gathered = lax.all_to_all(input_term, 'tp', 0, 0, tiled=True)  6.36 us
  transfers between devices with their start and end apart: 3, of which 3 were waited for; matrix products, arithmetic and copies ran while one was open for 9% of the time, Pallas kernels for 0%

profile of v2, /device:TPU:1, one launch (start us, length us, event | category | flops | bytes accessed | tf_op | source)
XLA Modules:
  0.0 271.2 jit_solution(3518373715141281989)
XLA Ops:
  7.2 0.0 copy-start
  7.2 0.0 all-gather.2.cloned.1.call-start
  7.2 1.8 pad_maximum_fusion.9
  9.0 0.0 all-gather.2.cloned.1.call-update
  9.0 0.0 reduce-scatter.4.cloned.1.call-start
  9.7 1.2 copy.43
  10.9 0.9 copy.44
  11.9 0.3 pad_add_fusion
  12.2 2.2 broadcast_in_dim.55
  14.5 2.6 copy.53
  17.1 66.6 %all-gather.2.cloned.1.call-done = bf16[4096,768]{1,0:T(8,128)(2,1)} async-done(((bf16[128,768]{1,0:T(8,128)(2,1)}), bf16[4096,768]{1,0:T(8,128)(2,1)}) %all-gather.2.cloned.1.call-update) | async-done | bytes 6291472 | tf_op jit(solution)/shard_map/all_gather | solution.py:68
  83.7 0.0 copy-done
  83.7 5.6 %fusion.6 = bf16[384,768]{0,1:T(8,128)(2,1)S(1)} fusion(bf16[4096,768]{1,0:T(8,128)(2,1)} %all-gather.2.cloned.1.call-done, bf16[384,4096]{1,0:T(8,128)(2,1)S(1)} %copy-done), kind=kOutput, calls=%fused_computation.19 | convolution fusion | flops 2416214016 | bytes 10027008 | tf_op jit(solution)/shard_map/dot_general | solution.py:69
  89.4 0.7 fusion.24
  90.1 0.9 copy.39
  91.0 1.0 copy.40
  92.0 1.0 copy.41
  93.1 0.0 copy-start.4
  93.1 3.7 %fusion.26 = (f32[1536]{0:T(1024)S(1)}, f32[1536,1536]{0,1:T(8,128)S(1)}) fusion(pred[1536,1536]{0,1:T(8,128)(4,1)} %bitcast.59, bf16[1536,128]{1,0:T(8,128)(2,1)} %bitcast.66, bf16[384,128]{1,0:T(8,128)(2,1)S(1)} %copy.40, bf16[1152,128]{1,0:T(8,128)(2,1)} %bitcast.72), kind=kOutput, calls=%fused_computation.43 | convolution fusion | flops 611842560 | bytes 12589056 | tf_op jit(solution)/shard_map/while/body/eval_jaxpr/dot_general | solution.py:12
  96.7 0.0 copy-start.2
  96.8 0.0 copy-start.7
  96.8 1.3 fusion.4
  98.1 0.0 copy-done.4
  98.1 0.0 copy-done.2
  98.1 0.0 copy-done.7
  98.1 5.0 %fusion.1 = (f32[1536]{0:T(1024)S(1)}, bf16[1536,1536]{0,1:T(8,128)(2,1)S(1)}, f32[1536,1536]{1,0:T(8,128)}) fusion(f32[1536]{0:T(1024)S(1)} %fusion.4, f32[1536,1536]{0,1:T(8,128)S(1)} %get-tuple-element.68, f32[1536]{0:T(1024)S(1)} %get-tuple-element.67, bf16[1536,128]{1,0:T(8,128)(2,1)S(1)} %bitcast.63, bf16[384,128]{1,0:T(8,128)(2,1)S(1)} %copy.41, ...), kind=kOutput, calls=%fused_computation.4 | convolution fusion | flops 618920448 | bytes 24397824 | tf_op jit(solution)/shard_map/while/body/eval_jaxpr/dot_general | solution.py:12
  103.2 0.0 copy-start.1
  103.2 1.6 fusion.14
  104.7 0.0 copy-start.3
  104.7 0.0 copy-start.6
  104.7 7.9 %fusion.3 = bf16[1536,1536]{0,1:T(8,128)(2,1)} fusion(bf16[1536,1536]{0,1:T(8,128)(2,1)S(1)} %get-tuple-element.62, f32[1536,1536]{1,0:T(8,128)} %get-tuple-element.69, f32[1536]{0:T(1024)S(1)} %get-tuple-element.61), kind=kLoop, calls=%fused_computation.6 | loop fusion | flops 11796480 | bytes 18880512 | tf_op jit(solution)/shard_map/while/body/eval_jaxpr/convert_element_type | solution.py:46
  112.7 0.0 copy-done.1
  112.7 0.0 copy-done.3
  112.7 2.4 fusion.11
  115.1 0.0 copy-done.6
  115.1 4.5 %convolution_convert_fusion.2 = bf16[1536,128]{1,0:T(8,128)(2,1)} fusion(bf16[1536,1536]{0,1:T(8,128)(2,1)} %fusion.3, bf16[384,128]{1,0:T(8,128)(2,1)S(1)} %copy.40, bf16[1152,128]{1,0:T(8,128)(2,1)S(1)} %bitcast.73), kind=kOutput, calls=%fused_computation.15 | convolution fusion | flops 604962816 | bytes 5505024 | tf_op jit(solution)/shard_map/while/body/eval_jaxpr/dot_general | solution.py:47
  119.6 1.2 copy.45
  120.8 6.3 %fusion.5 = bf16[4096,768]{0,1:T(8,128)(2,1)} fusion(bf16[384,4096]{1,0:T(8,128)(2,1)S(1)} %copy-done, bf16[384,128]{0,1:T(8,128)(2,1)} %fusion.14, bf16[384,128]{0,1:T(8,128)(2,1)} %fusion.11, bf16[384,512]{0,1:T(8,128)(2,1)S(1)} %bitcast.68), kind=kOutput, calls=%fused_computation.12 | convolution fusion | flops 2420834304 | bytes 10027008 | tf_op jit(solution)/shard_map/dot_general | solution.py:18
  127.2 8.6 %copy.50 = bf16[4096,768]{1,0:T(8,128)(2,1)} copy(bf16[4096,768]{0,1:T(8,128)(2,1)} %fusion.5) | data formatting | bytes 12582912
  135.8 0.0 reduce-scatter.4.cloned.1.call-update
  135.8 5.6 %convolution_convert_fusion.1 = bf16[384,4096]{1,0:T(8,128)(2,1)S(1)} fusion(bf16[4096,768]{1,0:T(8,128)(2,1)} %all-gather.2.cloned.1.call-done, bf16[384,128]{0,1:T(8,128)(2,1)} %fusion.14, bf16[384,128]{0,1:T(8,128)(2,1)} %fusion.11, bf16[384,512]{0,1:T(8,128)(2,1)S(1)} %bitcast.69), kind=kOutput, calls=%fused_computation.13 | convolution fusion | flops 2419261440 | bytes 10027008 | tf_op jit(solution)/shard_map/dot_general | solution.py:12
  141.4 2.0 copy.57
  143.4 0.0 copy-start.5
  143.4 0.0 copy-start.8
  143.4 6.4 %all-to-all-start = ((bf16[8,384,512]{2,1,0:T(8,128)(2,1)}), bf16[8,384,512]{2,1,0:T(8,128)(2,1)}, u32[]{:S(2)}, u32[]{:S(2)}) async-start(bf16[8,384,512]{2,1,0:T(8,128)(2,1)} %bitcast.56), calls=%async_computation | async-start | bytes 6291456 | tf_op jit(solution)/shard_map/all_to_all | solution.py:96
  149.7 0.0 copy-done.5
  149.7 0.0 copy-done.8
  149.8 3.8 %convolution_convert_fusion.3 = bf16[1536,128]{1,0:T(8,128)(2,1)S(1)} fusion(bf16[1536,1536]{0,1:T(8,128)(2,1)} %copy-done.1, bf16[384,128]{1,0:T(8,128)(2,1)S(1)} %copy-done.5, bf16[1152,128]{1,0:T(8,128)(2,1)S(1)} %bitcast.75), kind=kOutput, calls=%fused_computation.16 | convolution fusion | flops 604962816 | bytes 5505024 | tf_op jit(solution)/shard_map/while/body/eval_jaxpr/dot_general | solution.py:42
  153.6 0.3 copy.42
  153.9 0.8 copy.58
  154.7 45.9 %all-to-all-done = bf16[8,384,512]{2,1,0:T(8,128)(2,1)} async-done(((bf16[8,384,512]{2,1,0:T(8,128)(2,1)}), bf16[8,384,512]{2,1,0:T(8,128)(2,1)}, u32[]{:S(2)}, u32[]{:S(2)}) %all-to-all-start) | async-done | bytes 3145760 | tf_op jit(solution)/shard_map/all_to_all | solution.py:96
  200.6 3.2 %reduce_sum.34 = bf16[384,512]{1,0:T(8,128)(2,1)} reduce(bf16[8,384,512]{2,1,0:T(8,128)(2,1)} %all-to-all-done, bf16[]{:T(256)} %constant.34.clone.1), dimensions={0}, to_apply=%region_3.4 | reduce | flops 1376256 | bytes 3538946 | tf_op jit(solution)/shard_map/reduce_sum | solution.py:97
  203.9 57.0 %reduce-scatter.4.cloned.1.call-done = bf16[128,768]{1,0:T(8,128)(2,1)} async-done(((bf16[4096,768]{1,0:T(8,128)(2,1)}), bf16[128,768]{1,0:T(8,128)(2,1)}) %reduce-scatter.4.cloned.1.call-update) | async-done | bytes 196624
  260.9 1.1 copy.51
  262.1 0.8 copy.47
  262.9 0.7 copy.49
  263.7 0.7 copy.48
  (7 shorter events, 0.2 us)
Async XLA Ops:
  7.2 76.5 %copy-start = (bf16[384,4096]{1,0:T(8,128)(2,1)S(1)}, bf16[384,4096]{1,0:T(8,128)(2,1)}, u32[]{:S(2)}) copy-start(bf16[384,4096]{1,0:T(8,128)(2,1)} %param.8) | copy-start | bytes 9437188
  7.2 76.5 %all-gather.2.cloned.1.call-start = ((), (), s32[]{:S(2)}) async-start(), calls=%async_computation.2 | async-start | bytes 6488064 | tf_op jit(solution)/shard_map/all_gather | solution.py:68
  9.0 251.9 %reduce-scatter.4.cloned.1.call-start = ((), (), s32[]{:S(2)}) async-start(), calls=%async_computation.3 | async-start | bytes 6488064
  93.1 5.0 %copy-start.4 = (bf16[384,128]{1,0:T(8,128)(2,1)}, bf16[384,128]{1,0:T(8,128)(2,1)S(1)}, u32[]{:S(2)}) copy-start(bf16[384,128]{1,0:T(8,128)(2,1)S(1)} %copy.41) | copy-start | bytes 294916
  96.7 1.4 copy-start.2
  96.8 1.4 copy-start.7
  103.2 9.5 %copy-start.1 = (bf16[1536,1536]{0,1:T(8,128)(2,1)}, bf16[1536,1536]{0,1:T(8,128)(2,1)S(1)}, u32[]{:S(2)}) copy-start(bf16[1536,1536]{0,1:T(8,128)(2,1)S(1)} %get-tuple-element.62) | copy-start | bytes 14155780
  104.7 7.9 %copy-start.3 = (bf16[384,1,4,128]{3,0,2,1:T(8,128)(2,1)S(1)}, bf16[384,1,4,128]{3,0,2,1:T(8,128)(2,1)}, u32[]{:S(2)}) copy-start(bf16[384,1,4,128]{3,0,2,1:T(8,128)(2,1)} %copy.39) | copy-start | bytes 1179652
  104.7 10.4 %copy-start.6 = (bf16[1,1152,128]{2,1,0:T(8,128)(2,1)S(1)}, bf16[1,1152,128]{2,1,0:T(8,128)(2,1)}, u32[]{:S(2)}) copy-start(bf16[1,1152,128]{2,1,0:T(8,128)(2,1)} %param.13) | copy-start | bytes 884740
  143.4 6.4 %copy-start.5 = (bf16[384,128]{1,0:T(8,128)(2,1)S(1)}, bf16[384,128]{1,0:T(8,128)(2,1)}, u32[]{:S(2)}) copy-start(bf16[384,128]{1,0:T(8,128)(2,1)} %copy-done.4) | copy-start | bytes 294916
  143.4 6.4 %copy-start.8 = (bf16[1,1152,128]{2,1,0:T(8,128)(2,1)S(1)}, bf16[1,1152,128]{2,1,0:T(8,128)(2,1)}, u32[]{:S(2)}) copy-start(bf16[1,1152,128]{2,1,0:T(8,128)(2,1)} %param.14) | copy-start | bytes 884740
  143.4 57.3 %all-to-all-start = ((bf16[8,384,512]{2,1,0:T(8,128)(2,1)}), bf16[8,384,512]{2,1,0:T(8,128)(2,1)}, u32[]{:S(2)}, u32[]{:S(2)}) async-start(bf16[8,384,512]{2,1,0:T(8,128)(2,1)} %bitcast.56), calls=%async_computation | async-start | bytes 6291456 | tf_op jit(solution)/shard_map/all_to_all | solution.py:96
Sparse Core Ops, SparseCore 0:
  10.4 73.2 all-gather.1
  135.9 124.9 reduce-scatter.3

commit v3 on v2

--- a/solution.py
+++ b/solution.py
@@ -1,11 +1,13 @@
 import jax
 import jax.numpy as jnp
 from jax import lax
-from jax.sharding import PartitionSpec as P
+from jax.sharding import Mesh, PartitionSpec as P
 
 H = 32
 KV = 8
 HD = 128
+SWAP = [(0, 1), (1, 0)]
+BLK = ("xl", "z", "c")
 
 
 def contract_last(left, right):
@@ -65,7 +67,7 @@
     query_cols = w_query.shape[1]
     kv_cols = w_key.shape[1]
     local_w = jnp.concatenate([w_query, w_key, w_value], 1)
-    full_w = lax.all_gather(local_w, "blk", axis=0, tiled=True)
+    full_w = lax.all_gather(local_w, BLK, axis=0, tiled=True)
     proj = jnp.dot(hidden_in, full_w, preferred_element_type=jnp.float32)
     queries = proj[:, :query_cols].astype(jnp.bfloat16)
     new_keys = proj[:, query_cols : query_cols + kv_cols].astype(jnp.bfloat16)
@@ -86,16 +88,28 @@
     grad_keys = results[2].transpose(1, 0, 2).reshape(tokens_dev, kv_local * HD)
     grad_values = results[3].transpose(1, 0, 2).reshape(tokens_dev, kv_local * HD)
     grads_cat = jnp.concatenate([grad_query, grad_keys, grad_values], 1)
-    blk_count = lax.axis_size("blk")
     tp_count = lax.axis_size("tp")
-    weight_term = contract_first(hidden_in, grads_cat).astype(jnp.bfloat16)
-    summed = lax.psum_scatter(weight_term, "blk", scatter_dimension=0, tiled=True)
-    summed = summed.astype(jnp.float32)
+    z_count = lax.axis_size("z")
+    rows = w_query.shape[0]
+    chip_core = lax.axis_index("c")
+    x_pos = lax.axis_index("xl")
+    by_place = hidden_in.reshape(tokens_dev, 2, z_count, 2, rows).transpose(0, 2, 1, 3, 4)
+    cols_other = lax.dynamic_index_in_dim(by_place, 1 - chip_core, 3, False)
+    cols_own = lax.dynamic_index_in_dim(by_place, chip_core, 3, False)
+    part_other = contract_first(cols_other.reshape(tokens_dev, -1), grads_cat)
+    from_peer = lax.ppermute(part_other, "c", SWAP)
+    part_own = contract_first(cols_own.reshape(tokens_dev, -1), grads_cat)
+    chip_sum = (part_own + from_peer).astype(jnp.bfloat16)
+    ring_sum = lax.psum_scatter(chip_sum, "z", scatter_dimension=0, tiled=True)
+    ring_sum = ring_sum.reshape(2, rows, -1)
+    keep = lax.dynamic_index_in_dim(ring_sum, x_pos, 0, False)
+    give = lax.dynamic_index_in_dim(ring_sum, 1 - x_pos, 0, False)
+    summed = keep.astype(jnp.float32) + lax.ppermute(give, "xl", SWAP).astype(jnp.float32)
     input_term = contract_last(grads_cat, full_w).astype(jnp.bfloat16)
     input_term = input_term.reshape(tokens_dev, tp_count, -1).transpose(1, 0, 2)
     gathered = lax.all_to_all(input_term, "tp", 0, 0, tiled=True)
     grad_in = jnp.sum(gathered.astype(jnp.float32), axis=0).astype(jnp.bfloat16)
-    summed = summed * (tokens_dev * blk_count) ** (-0.5)
+    summed = summed * (tokens_dev * lax.axis_size(BLK)) ** (-0.5)
     grad_wq = summed[:, :query_cols]
     grad_wk = summed[:, query_cols : query_cols + kv_cols]
     grad_wv = summed[:, query_cols + kv_cols :]
@@ -103,15 +117,18 @@
 
 
 def solution(mesh):
+    blk = mesh.shape["blk"]
+    devices = mesh.devices.reshape(2, blk // 4, 2, mesh.shape["tp"])
+    split = Mesh(devices, BLK + ("tp",))
     in_specs = (
-        P("blk", None),
-        P("blk", "tp"),
-        P("blk", "tp"),
-        P("blk", "tp"),
-        P("blk"),
-        P("blk", None, "tp"),
-        P("blk", None, "tp"),
-        P("blk", "tp"),
+        P(BLK, None),
+        P(BLK, "tp"),
+        P(BLK, "tp"),
+        P(BLK, "tp"),
+        P(BLK),
+        P(BLK, None, "tp"),
+        P(BLK, None, "tp"),
+        P(BLK, "tp"),
     )
-    out_specs = (P("blk", "tp"), P("blk", "tp"), P("blk", "tp"), P("blk", "tp"), P("blk", "tp"))
-    return jax.shard_map(local, mesh=mesh, in_specs=in_specs, out_specs=out_specs, check_vma=False)
+    out_specs = (P(BLK, "tp"),) * 5
+    return jax.shard_map(local, mesh=split, in_specs=in_specs, out_specs=out_specs, check_vma=False)

time: 275 us -> 198 us (0.72)
  waiting for transfers between devices: 170 us -> 103 us
  local copies, waits for them, and re-layouts: 27.1 us -> 21.4 us
    unnamed x3 -> x2, waiting for transfers between devices: 57.1 us -> 0.03 us
    all_to_all x1, waiting for transfers between devices: 45.9 us -> 1.42 us  [local(): gathered = lax.all_to_all(input_term, 'tp', 0, 0, tiled=True)]
    reduce_scatter x0 -> x1, waiting for transfers between devices: none -> 30 us  [local(): ring_sum = lax.psum_scatter(chip_sum, 'z', scatter_dimension=0, tiled=True)]
    ppermute x0 -> x2, waiting for transfers between devices: none -> 9.7 us  [the longest x1 9.7 us: local(): from_peer = lax.ppermute(part_other, 'c', SWAP)]
    unnamed x26 -> x22, local copies, waits for them, and re-layouts: 16.7 us -> 7.12 us
    all_gather x1, waiting for transfers between devices: 66.6 us -> 62.1 us  [local(): full_w = lax.all_gather(local_w, BLK, axis=0, tiled=True)]
    dynamic_slice x0 -> x3, local copies, waits for them, and re-layouts: none -> 3 us  [the longest x2 1.65 us: local(): cols_own = lax.dynamic_index_in_dim(by_place, chip_core, 3, False)]
    dot_general x3 -> x4, matrix products: 10.3 us -> 8.93 us  [contract_first(): lax.dot_general(left, right, (((0,), (0,)), ((), ())), preferred_element_...]
  transfers between devices with their start and end apart: 3 -> 5, of which waited for: 3 -> 4; matrix products, arithmetic and copies ran while one was open for 9% -> 14% of each run, Pallas kernels for 0% -> 0%
where the time goes in v3:
time: 198 us; the launch traced here: 196 us
  waiting for transfers between devices  103 us (52%)
  matrix products  36.6 us (18%)
  local copies, waits for them, and re-layouts  21.4 us (11%)
  between operations  14.9 us (8%)
  other arithmetic  12.1 us (6%)
  starting transfers between devices  7.85 us (4%)
    all_gather x1, waiting for transfers between devices, local(): full_w = lax.all_gather(local_w, BLK, axis=0, tiled=True)  62.1 us
    reduce_scatter x1, waiting for transfers between devices, local(): ring_sum = lax.psum_scatter(chip_sum, 'z', scatter_dimension=0, tiled=True)  30 us
    dot_general x3, matrix products, contract_last(): lax.dot_general(left, right, (((1,), (1,)), ((), ())), preferred_element_...  12.7 us
    ppermute x1, waiting for transfers between devices, local(): from_peer = lax.ppermute(part_other, 'c', SWAP)  9.7 us
    dot_general x4, matrix products, contract_first(): lax.dot_general(left, right, (((0,), (0,)), ((), ())), preferred_element_...  8.93 us
    dot_general x1, matrix products, local(): proj = jnp.dot(hidden_in, full_w, preferred_element_type=jnp.float32)  7.15 us
    unnamed x22, local copies, waits for them, and re-layouts  7.12 us
    convert_element_type x1, other arithmetic, head_pass(): (probs_wide * (grad_probs - row_dot) * factor).astype(jnp.bfloat16)  6.52 us
  transfers between devices with their start and end apart: 5, of which 4 were waited for; matrix products, arithmetic and copies ran while one was open for 14% of the time, Pallas kernels for 0%

profile of v3, /device:TPU:1, one launch (start us, length us, event | category | flops | bytes accessed | tf_op | source)
XLA Modules:
  0.0 196.2 jit_solution(956832347037213325)
XLA Ops:
  7.2 0.0 copy-start.3
  7.2 0.0 all-gather.2.cloned.1.call-start
  7.2 1.7 pad_maximum_fusion.7
  8.9 0.0 all-gather.2.cloned.1.call-update
  8.9 0.0 reduce-scatter.2.cloned.1.call-start
  9.7 0.3 pad_add_fusion
  10.0 2.2 %broadcast_in_dim.55 = pred[4,384,1536]{1,0,2:T(4,128)(4,1)S(1)} broadcast(pred[384,1536]{0,1:T(8,128)(4,1)S(1)} %pad_add_fusion), dimensions={1,2} | broadcast | bytes 2949120 | tf_op jit(solution)/shard_map/while/body/eval_jaxpr/jit(_where)/broadcast_in_dim | solution.py:39
  12.2 2.6 %copy.45 = pred[192,8,4,384]{3,1,2,0:T(8,128)(4,1)} copy(pred[192,8,4,384]{3,2,1,0:T(4,128)(4,1)S(1)} %bitcast.68) | data formatting | bytes 4718592
  14.9 0.0 copy-done.3
  14.9 0.2 copy.37
  15.1 0.2 copy.38
  15.3 3.4 %copy.41 = bf16[384,4096]{0,1:T(8,128)(2,1)S(1)} copy(bf16[384,4096]{1,0:T(8,128)(2,1)} %param.8) | data formatting | bytes 6291456 | tf_op args[0]
  18.8 1.5 dynamic-slice_bitcast_fusion.1
  20.2 1.4 copy.43
  21.6 0.0 copy-start.2
  21.6 62.1 %all-gather.2.cloned.1.call-done = bf16[4096,768]{1,0:T(8,128)(2,1)} async-done(((bf16[128,768]{1,0:T(8,128)(2,1)}), bf16[4096,768]{1,0:T(8,128)(2,1)}) %all-gather.2.cloned.1.call-update) | async-done | bytes 6291472 | tf_op jit(solution)/shard_map/all_gather | solution.py:70
  83.7 7.2 %fusion.5 = bf16[384,768]{0,1:T(8,128)(2,1)S(1)} fusion(bf16[4096,768]{1,0:T(8,128)(2,1)} %all-gather.2.cloned.1.call-done, bf16[384,4096]{1,0:T(8,128)(2,1)} %param.8), kind=kOutput, calls=%fused_computation.20 | convolution fusion | flops 2416214016 | bytes 10027008 | tf_op jit(solution)/shard_map/dot_general | solution.py:71
  90.9 0.7 fusion.23
  91.6 0.8 copy.34
  92.3 0.2 copy.33
  92.6 0.0 copy-start.4
  92.6 1.7 copy.35
  94.3 0.0 copy-done.2
  94.3 2.8 %fusion.25 = (f32[1536]{0:T(1024)S(1)}, f32[1536,1536]{0,1:T(8,128)S(1)}) fusion(pred[1536,1536]{0,1:T(8,128)(4,1)S(1)} %bitcast.75, bf16[1536,128]{1,0:T(8,128)(2,1)S(1)} %bitcast.82, bf16[384,128]{1,0:T(8,128)(2,1)} %copy.34, bf16[1152,128]{1,0:T(8,128)(2,1)} %bitcast.88), kind=kOutput, calls=%fused_computation.45 | convolution fusion | flops 611842560 | bytes 12589056 | tf_op jit(solution)/shard_map/while/body/eval_jaxpr/dot_general | solution.py:14
  97.1 0.0 copy-done.4
  97.1 0.0 copy-start.7
  97.1 0.0 copy-start.8
  97.1 1.3 fusion.4
  98.4 0.0 copy-done.7
  98.4 0.0 copy-done.8
  98.4 4.5 %fusion.1 = (f32[1536]{0:T(1024)S(1)}, bf16[1536,1536]{0,1:T(8,128)(2,1)}, f32[1536,1536]{1,0:T(8,128)S(1)}) fusion(f32[1536]{0:T(1024)S(1)} %fusion.4, f32[1536,1536]{0,1:T(8,128)S(1)} %get-tuple-element.50, f32[1536]{0:T(1024)S(1)} %get-tuple-element.49, bf16[1536,128]{1,0:T(8,128)(2,1)S(1)} %bitcast.79, bf16[384,128]{1,0:T(8,128)(2,1)S(1)} %copy-done.7, ...), kind=kOutput, calls=%fused_computation.4 | convolution fusion | flops 618920448 | bytes 24397824 | tf_op jit(solution)/shard_map/while/body/eval_jaxpr/dot_general | solution.py:14
  102.9 6.5 %fusion.3 = bf16[1536,1536]{0,1:T(8,128)(2,1)} fusion(bf16[1536,1536]{0,1:T(8,128)(2,1)} %get-tuple-element.30, f32[1536,1536]{1,0:T(8,128)S(1)} %get-tuple-element.51, f32[1536]{0:T(1024)S(1)} %get-tuple-element.29), kind=kLoop, calls=%fused_computation.6 | loop fusion | flops 11796480 | bytes 18880512 | tf_op jit(solution)/shard_map/while/body/eval_jaxpr/convert_element_type | solution.py:48
  109.4 0.0 copy-start.5
  109.4 0.0 copy-start
  109.4 4.0 %convolution_convert_fusion.1 = bf16[1536,128]{1,0:T(8,128)(2,1)S(1)} fusion(bf16[1536,1536]{0,1:T(8,128)(2,1)} %fusion.3, bf16[384,128]{1,0:T(8,128)(2,1)} %copy.34, bf16[1152,128]{1,0:T(8,128)(2,1)} %bitcast.89), kind=kOutput, calls=%fused_computation.14 | convolution fusion | flops 604962816 | bytes 5505024 | tf_op jit(solution)/shard_map/while/body/eval_jaxpr/dot_general | solution.py:49
  113.4 0.0 copy-done.5
  113.4 1.8 fusion.10
  115.2 1.8 fusion.13
  117.0 0.2 copy.39
  117.2 0.0 copy-done
  117.2 0.0 copy-start.1
  117.2 1.8 fusion.22
  119.0 0.4 collective-permute-start
  119.4 0.0 copy-done.1
  119.4 0.2 copy.42
  119.6 9.7 %collective-permute-done = f32[2048,768]{1,0:T(8,128)S(1)} collective-permute-done((f32[2048,768]{1,0:T(8,128)S(1)}, f32[2048,768]{1,0:T(8,128)S(1)}, u32[]{:S(2)}, u32[]{:S(2)}) %collective-permute-start) | collective-permute-done | bytes 6291488 | tf_op jit(solution)/shard_map/ppermute | solution.py:100
  129.3 3.6 %add_convert_fusion = bf16[2048,768]{1,0:T(8,128)(2,1)} fusion(f32[2048,768]{1,0:T(8,128)S(1)} %collective-permute-done, bf16[384,2048]{0,1:T(8,128)(2,1)S(1)} %bitcast.70, bf16[384,128]{0,1:T(8,128)(2,1)S(1)} %fusion.13, bf16[384,128]{0,1:T(8,128)(2,1)S(1)} %fusion.10, bf16[384,512]{0,1:T(8,128)(2,1)S(1)} %bitcast.72), kind=kOutput, calls=%fused_computation.11 | convolution fusion | flops 1212874752 | bytes 11599872 | tf_op jit(solution)/shard_map/dot_general | solution.py:20
  132.9 0.0 reduce-scatter.2.cloned.1.call-update
  132.9 5.4 %convolution_convert_fusion = bf16[384,4096]{1,0:T(8,128)(2,1)S(1)} fusion(bf16[4096,768]{1,0:T(8,128)(2,1)} %all-gather.2.cloned.1.call-done, bf16[384,128]{0,1:T(8,128)(2,1)S(1)} %fusion.13, bf16[384,128]{0,1:T(8,128)(2,1)S(1)} %fusion.10, bf16[384,512]{0,1:T(8,128)(2,1)S(1)} %bitcast.73), kind=kOutput, calls=%fused_computation.12 | convolution fusion | flops 2419261440 | bytes 10027008 | tf_op jit(solution)/shard_map/dot_general | solution.py:14
  138.3 1.9 copy.49
  140.3 6.2 %all-to-all-start = ((bf16[8,384,512]{2,1,0:T(8,128)(2,1)}), bf16[8,384,512]{2,1,0:T(8,128)(2,1)S(1)}, u32[]{:S(2)}, u32[]{:S(2)}) async-start(bf16[8,384,512]{2,1,0:T(8,128)(2,1)} %bitcast.64), calls=%async_computation | async-start | bytes 6291456 | tf_op jit(solution)/shard_map/all_to_all | solution.py:110
  146.5 30.0 %reduce-scatter.2.cloned.1.call-done = bf16[256,768]{1,0:T(8,128)(2,1)} async-done(((bf16[2048,768]{1,0:T(8,128)(2,1)}), bf16[256,768]{1,0:T(8,128)(2,1)}) %reduce-scatter.2.cloned.1.call-update) | async-done | bytes 393232 | tf_op jit(solution)/shard_map/reduce_scatter | solution.py:103
  176.6 1.6 dynamic-slice_bitcast_fusion.2
  178.2 1.2 collective-permute-start.1
  179.3 3.8 %convolution_convert_fusion.2 = bf16[1536,128]{1,0:T(8,128)(2,1)S(1)} fusion(bf16[1536,1536]{0,1:T(8,128)(2,1)} %get-tuple-element.30, bf16[384,128]{1,0:T(8,128)(2,1)} %copy.35, bf16[1152,128]{1,0:T(8,128)(2,1)} %bitcast.90), kind=kOutput, calls=%fused_computation.15 | convolution fusion | flops 604962816 | bytes 5505024 | tf_op jit(solution)/shard_map/while/body/eval_jaxpr/dot_general | solution.py:44
  183.2 0.3 copy.36
  183.5 0.8 copy.50
  184.3 1.4 all-to-all-done
  185.7 1.3 reduce_sum.34
  187.0 0.0 collective-permute-done.1
  187.0 0.0 copy-done.6
  187.0 1.0 fusion.16
  188.0 0.7 slice.42
  188.7 0.7 fusion.24
  (5 shorter events, 0.1 us)
Async XLA Ops:
  7.2 7.7 %copy-start.3 = (bf16[384,512]{1,0:T(8,128)(2,1)S(1)}, bf16[384,512]{1,0:T(8,128)(2,1)}, u32[]{:S(2)}) copy-start(bf16[384,512]{1,0:T(8,128)(2,1)} %param.15) | copy-start | bytes 1179652
  7.2 76.5 %all-gather.2.cloned.1.call-start = ((), (), s32[]{:S(2)}) async-start(), calls=%async_computation.2 | async-start | bytes 6488064 | tf_op jit(solution)/shard_map/all_gather | solution.py:70
  8.9 167.6 %reduce-scatter.2.cloned.1.call-start = ((), (), s32[]{:S(2)}) async-start(), calls=%async_computation.3 | async-start | bytes 3538944 | tf_op jit(solution)/shard_map/reduce_scatter | solution.py:103
  21.6 72.7 %copy-start.2 = (pred[192,8,4,384]{3,1,2,0:T(8,128)(4,1)S(1)}, pred[192,8,4,384]{3,1,2,0:T(8,128)(4,1)}, u32[]{:S(2)}) copy-start(pred[192,8,4,384]{3,1,2,0:T(8,128)(4,1)} %copy.45) | copy-start | bytes 7077892
  92.6 4.5 %copy-start.4 = (bf16[384,1,4,128]{3,0,2,1:T(8,128)(2,1)}, bf16[384,1,4,128]{3,0,2,1:T(8,128)(2,1)S(1)}, u32[]{:S(2)}) copy-start(bf16[384,1,4,128]{3,0,2,1:T(8,128)(2,1)S(1)} %copy.33) | copy-start | bytes 1179652
  97.1 1.3 copy-start.7
  97.1 1.3 copy-start.8
  109.4 4.0 %copy-start.5 = (bf16[384,1,4,128]{3,0,2,1:T(8,128)(2,1)S(1)}, bf16[384,1,4,128]{3,0,2,1:T(8,128)(2,1)}, u32[]{:S(2)}) copy-start(bf16[384,1,4,128]{3,0,2,1:T(8,128)(2,1)} %copy-done.4) | copy-start | bytes 1179652
  109.4 7.8 %copy-start = (bf16[384,8,2,1,128]{0,4,2,1,3:T(8,128)(2,1)S(1)}, bf16[384,8,2,1,128]{0,4,2,1,3:T(8,128)(2,1)}, u32[]{:S(2)}) copy-start(bf16[384,8,2,1,128]{0,4,2,1,3:T(8,128)(2,1)} %copy.43) | copy-start | bytes 4718596
  117.2 2.2 %copy-start.1 = (bf16[384,8,2,1,128]{0,4,3,1,2:T(8,128)(2,1)S(1)}, bf16[384,8,2,1,128]{0,4,3,1,2:T(8,128)(2,1)}, u32[]{:S(2)}) copy-start(bf16[384,8,2,1,128]{0,4,3,1,2:T(8,128)(2,1)} %get-tuple-element.31) | copy-start | bytes 4718596
  119.0 10.2 %collective-permute-start = (f32[2048,768]{1,0:T(8,128)S(1)}, f32[2048,768]{1,0:T(8,128)S(1)}, u32[]{:S(2)}, u32[]{:S(2)}) collective-permute-start(f32[2048,768]{1,0:T(8,128)S(1)} %fusion.22), channel_id=1, source_target_pairs={{0,8},{8,0},{1,9},{9,1},{2,10},{10,2},{3,11},{11,3},{4,12},{12,4},... | collective-permute-start | bytes 18874376 | tf_op jit(solution)/shard_map/ppermute | solution.py:100
  140.3 45.4 %all-to-all-start = ((bf16[8,384,512]{2,1,0:T(8,128)(2,1)}), bf16[8,384,512]{2,1,0:T(8,128)(2,1)S(1)}, u32[]{:S(2)}, u32[]{:S(2)}) async-start(bf16[8,384,512]{2,1,0:T(8,128)(2,1)} %bitcast.64), calls=%async_computation | async-start | bytes 6291456 | tf_op jit(solution)/shard_map/all_to_all | solution.py:110
  178.2 8.8 %copy-start.6 = (bf16[256,768]{1,0:T(8,128)(2,1)S(1)}, bf16[256,768]{1,0:T(8,128)(2,1)}, u32[]{:S(2)}) copy-start(bf16[256,768]{1,0:T(8,128)(2,1)} %reduce-scatter.2.cloned.1.call-done) | copy-start | bytes 1179652
  178.2 8.8 %collective-permute-start.1 = (bf16[128,768]{1,0:T(8,128)(2,1)}, bf16[128,768]{1,0:T(8,128)(2,1)}, u32[]{:S(2)}, u32[]{:S(2)}) collective-permute-start(bf16[128,768]{1,0:T(8,128)(2,1)} %dynamic-slice_bitcast_fusion.2), channel_id=1, source_target_pairs={{0,128},{128,0},{1,129},{129,1},{2,130},{130,2},{3,131},{131,3},{4... | collective-permute-start | bytes 589832 | tf_op jit(solution)/shard_map/ppermute | solution.py:107
Sparse Core Ops, SparseCore 0:
  10.4 73.2 all-gather.1
  133.0 43.4 reduce-scatter.1

commit v4 on v3

--- a/solution.py
+++ b/solution.py
@@ -59,6 +59,33 @@
     )
 
 
+def gather_rows(block):
+    rows, width = block.shape
+    z_count = lax.axis_size("z")
+    x_pos = lax.axis_index("xl")
+    z_pos = lax.axis_index("z")
+    chip_core = lax.axis_index("c")
+    peer = lax.ppermute(block, "xl", SWAP)
+    pair = jnp.stack([jnp.where(x_pos == 0, block, peer), jnp.where(x_pos == 0, peer, block)])
+    ahead = [(i, (i + 1) % z_count) for i in range(z_count)]
+    behind = [(i, (i - 1) % z_count) for i in range(z_count)]
+    ring = jnp.zeros((z_count,) + pair.shape, pair.dtype)
+    ring = lax.dynamic_update_index_in_dim(ring, pair, z_pos, 0)
+    fwd = pair
+    bwd = pair
+    for step in range(1, z_count // 2 + 1):
+        fwd = lax.ppermute(fwd, "z", ahead)
+        ring = lax.dynamic_update_index_in_dim(ring, fwd, (z_pos - step) % z_count, 0)
+        if step < z_count - z_count // 2:
+            bwd = lax.ppermute(bwd, "z", behind)
+            ring = lax.dynamic_update_index_in_dim(ring, bwd, (z_pos + step) % z_count, 0)
+    other = lax.ppermute(ring, "c", SWAP)
+    first = jnp.where(chip_core == 0, ring, other)
+    second = jnp.where(chip_core == 0, other, ring)
+    full = jnp.stack([first, second], 2)
+    return full.transpose(1, 0, 2, 3, 4).reshape(-1, width)
+
+
 def local(hidden_in, w_query, w_key, w_value, starts, key_cache, value_cache, grad_out):
     tokens_dev = hidden_in.shape[0]
     kv_local = w_key.shape[1] // HD
@@ -67,7 +94,7 @@
     query_cols = w_query.shape[1]
     kv_cols = w_key.shape[1]
     local_w = jnp.concatenate([w_query, w_key, w_value], 1)
-    full_w = lax.all_gather(local_w, BLK, axis=0, tiled=True)
+    full_w = gather_rows(local_w)
     proj = jnp.dot(hidden_in, full_w, preferred_element_type=jnp.float32)
     queries = proj[:, :query_cols].astype(jnp.bfloat16)
     new_keys = proj[:, query_cols : query_cols + kv_cols].astype(jnp.bfloat16)

time: 198 us -> 192 us (0.970)
  waiting for transfers between devices: 103 us -> 66.5 us
  starting transfers between devices: 7.85 us -> 27.8 us
  local copies, waits for them, and re-layouts: 21.4 us -> 33.8 us
  matrix products: 36.6 us -> 33 us
  other arithmetic: 12.1 us -> 15.2 us
    all_gather x1 -> x0, waiting for transfers between devices: 62.1 us -> none  [local(): full_w = lax.all_gather(local_w, BLK, axis=0, tiled=True)]
    ppermute x0 -> x9, waiting for transfers between devices: none -> 24.9 us  [the longest x4 21.6 us: gather_rows(): fwd = lax.ppermute(fwd, 'z', ahead)]
    ppermute x0 -> x9, starting transfers between devices: none -> 19.4 us  [the longest x3 9.38 us: gather_rows(): bwd = lax.ppermute(bwd, 'z', behind)]
    dynamic_update_slice x0 -> x7, local copies, waits for them, and re-layouts: none -> 5.49 us  [the longest x4 3.14 us: gather_rows(): lax.dynamic_update_index_in_dim(ring, fwd, (z_pos - step) % z_count, 0)]
    another operation x0 -> x4, other arithmetic: none -> 3.91 us  [the longest x2 3.84 us: gather_rows(): full = jnp.stack([first, second], 2)]
    unnamed x22 -> x34, local copies, waits for them, and re-layouts: 7.12 us -> 11 us
    dot_general x1, matrix products: 7.15 us -> 3.45 us  [local(): proj = jnp.dot(hidden_in, full_w, preferred_element_type=jnp.float32)]
    broadcast_in_dim x0 -> x1, local copies, waits for them, and re-layouts: none -> 1.98 us  [gather_rows(): ring = jnp.zeros((z_count,) + pair.shape, pair.dtype)]
  transfers between devices with their start and end apart: 5 -> 13, of which waited for: 4 -> 8; matrix products, arithmetic and copies ran while one was open for 14% -> 18% of each run, Pallas kernels for 0% -> 0%
where the time goes in v4:
time: 192 us; the launch traced here: 191 us
  waiting for transfers between devices  66.5 us (35%)
  local copies, waits for them, and re-layouts  33.8 us (18%)
  matrix products  33 us (17%)
  starting transfers between devices  27.8 us (14%)
  other arithmetic  15.2 us (8%)
  between operations  15 us (8%)
    reduce_scatter x1, waiting for transfers between devices, local(): ring_sum = lax.psum_scatter(chip_sum, 'z', scatter_dimension=0, tiled=True)  28.9 us
    ppermute x4, waiting for transfers between devices, gather_rows(): fwd = lax.ppermute(fwd, 'z', ahead)  21.6 us
    dot_general x3, matrix products, contract_last(): lax.dot_general(left, right, (((1,), (1,)), ((), ())), preferred_element_...  12.8 us
    unnamed x34, local copies, waits for them, and re-layouts  11 us
    ppermute x1, waiting for transfers between devices, local(): from_peer = lax.ppermute(part_other, 'c', SWAP)  9.97 us
    ppermute x3, starting transfers between devices, gather_rows(): bwd = lax.ppermute(bwd, 'z', behind)  9.38 us
    dot_general x4, matrix products, contract_first(): lax.dot_general(left, right, (((0,), (0,)), ((), ())), preferred_element_...  9.06 us
    all_to_all x1, starting transfers between devices, local(): gathered = lax.all_to_all(input_term, 'tp', 0, 0, tiled=True)  6.78 us
  transfers between devices with their start and end apart: 13, of which 8 were waited for; matrix products, arithmetic and copies ran while one was open for 18% of the time, Pallas kernels for 0%

profile of v4, /device:TPU:1, one launch (start us, length us, event | category | flops | bytes accessed | tf_op | source)
XLA Modules:
  0.0 191.3 jit_solution(18026144844274912014)
XLA Ops:
  7.2 0.9 constant_dynamic-update-slice_fusion.2
  8.1 0.8 constant_dynamic-update-slice_fusion.1
  8.9 0.8 constant_dynamic-update-slice_fusion
  9.7 2.1 %collective-permute-start = (bf16[128,768]{1,0:T(8,128)(2,1)S(1)}, bf16[128,768]{1,0:T(8,128)(2,1)S(1)}, u32[]{:S(2)}, u32[]{:S(2)}) collective-permute-start(bf16[128,768]{1,0:T(8,128)(2,1)S(1)} %constant_dynamic-update-slice_fusion), channel_id=1, source_target_pairs={{0,128},{128,0},{1,129},{129,1},{2,130},{130,2},{3,131},{131,3},{4... | collective-permute-start | bytes 589832 | tf_op jit(solution)/shard_map/ppermute | solution.py:68
  11.8 3.4 %collective-permute-done = bf16[128,768]{1,0:T(8,128)(2,1)S(1)} collective-permute-done((bf16[128,768]{1,0:T(8,128)(2,1)S(1)}, bf16[128,768]{1,0:T(8,128)(2,1)S(1)}, u32[]{:S(2)}, u32[]{:S(2)}) %collective-permute-start) | collective-permute-done | bytes 196640 | tf_op jit(solution)/shard_map/ppermute | solution.py:68
  15.2 2.9 %collective-permute-start.1 = (bf16[2,128,768]{2,1,0:T(8,128)(2,1)S(1)}, bf16[2,128,768]{2,1,0:T(8,128)(2,1)S(1)}, u32[]{:S(2)}, u32[]{:S(2)}) collective-permute-start(bf16[2,128,768]{2,1,0:T(8,128)(2,1)S(1)} %pad_maximum_fusion.2), channel_id=1, source_target_pairs={{0,16},{16,32},{32,48},{48,64},{64,80},{80,96},{96,112},{112,0},{1... | collective-permute-start | bytes 1179656 | tf_op jit(solution)/shard_map/ppermute | solution.py:77
  18.1 4.0 %collective-permute-start.2 = (bf16[2,128,768]{2,1,0:T(8,128)(2,1)S(1)}, bf16[2,128,768]{2,1,0:T(8,128)(2,1)S(1)}, u32[]{:S(2)}, u32[]{:S(2)}) collective-permute-start(bf16[2,128,768]{2,1,0:T(8,128)(2,1)S(1)} %pad_maximum_fusion.2), channel_id=1, source_target_pairs={{0,112},{16,0},{32,16},{48,32},{64,48},{80,64},{96,80},{112,96},{1... | collective-permute-start | bytes 1179656 | tf_op jit(solution)/shard_map/ppermute | solution.py:80
  22.2 2.0 %broadcast_in_dim.85 = bf16[8,2,128,768]{3,2,0,1:T(8,128)(2,1)} broadcast(bf16[]{:T(256)} %constant.119.clone.1), dimensions={} | broadcast | bytes 3145730 | tf_op jit(solution)/shard_map/broadcast_in_dim | solution.py:72
  24.2 0.8 bitcast_dynamic-update-slice_fusion.6
  25.0 5.1 %collective-permute-done.1 = bf16[2,128,768]{2,1,0:T(8,128)(2,1)S(1)} collective-permute-done((bf16[2,128,768]{2,1,0:T(8,128)(2,1)S(1)}, bf16[2,128,768]{2,1,0:T(8,128)(2,1)S(1)}, u32[]{:S(2)}, u32[]{:S(2)}) %collective-permute-start.1) | collective-permute-done | bytes 393248 | tf_op jit(solution)/shard_map/ppermute | solution.py:77
  30.1 2.7 %collective-permute-start.4 = (bf16[2,128,768]{2,1,0:T(8,128)(2,1)S(1)}, bf16[2,128,768]{2,1,0:T(8,128)(2,1)S(1)}, u32[]{:S(2)}, u32[]{:S(2)}) collective-permute-start(bf16[2,128,768]{2,1,0:T(8,128)(2,1)S(1)} %collective-permute-done.2), channel_id=1, source_target_pairs={{0,112},{16,0},{32,16},{48,32},{64,48},{80,64},{96,80},{112,96},{1... | collective-permute-start | bytes 1179656 | tf_op jit(solution)/shard_map/ppermute | solution.py:80
  32.7 0.8 bitcast_dynamic-update-slice_fusion.5
  33.5 0.8 bitcast_dynamic-update-slice_fusion.4
  34.3 5.5 %collective-permute-done.3 = bf16[2,128,768]{2,1,0:T(8,128)(2,1)S(1)} collective-permute-done((bf16[2,128,768]{2,1,0:T(8,128)(2,1)S(1)}, bf16[2,128,768]{2,1,0:T(8,128)(2,1)S(1)}, u32[]{:S(2)}, u32[]{:S(2)}) %collective-permute-start.3) | collective-permute-done | bytes 393248 | tf_op jit(solution)/shard_map/ppermute | solution.py:77
  39.8 2.7 %collective-permute-start.6 = (bf16[2,128,768]{2,1,0:T(8,128)(2,1)S(1)}, bf16[2,128,768]{2,1,0:T(8,128)(2,1)S(1)}, u32[]{:S(2)}, u32[]{:S(2)}) collective-permute-start(bf16[2,128,768]{2,1,0:T(8,128)(2,1)S(1)} %collective-permute-done.4), channel_id=1, source_target_pairs={{0,112},{16,0},{32,16},{48,32},{64,48},{80,64},{96,80},{112,96},{1... | collective-permute-start | bytes 1179656 | tf_op jit(solution)/shard_map/ppermute | solution.py:80
  42.5 0.8 bitcast_dynamic-update-slice_fusion.3
  43.3 0.8 bitcast_dynamic-update-slice_fusion.2
  44.1 4.7 %collective-permute-done.5 = bf16[2,128,768]{2,1,0:T(8,128)(2,1)S(1)} collective-permute-done((bf16[2,128,768]{2,1,0:T(8,128)(2,1)S(1)}, bf16[2,128,768]{2,1,0:T(8,128)(2,1)S(1)}, u32[]{:S(2)}, u32[]{:S(2)}) %collective-permute-start.5) | collective-permute-done | bytes 393248 | tf_op jit(solution)/shard_map/ppermute | solution.py:77
  48.8 0.8 bitcast_dynamic-update-slice_fusion.1
  49.6 0.8 bitcast_dynamic-update-slice_fusion
  50.3 6.3 %collective-permute-done.7 = bf16[2,128,768]{2,1,0:T(8,128)(2,1)S(1)} collective-permute-done((bf16[2,128,768]{2,1,0:T(8,128)(2,1)S(1)}, bf16[2,128,768]{2,1,0:T(8,128)(2,1)S(1)}, u32[]{:S(2)}, u32[]{:S(2)}) %collective-permute-start.7) | collective-permute-done | bytes 393248 | tf_op jit(solution)/shard_map/ppermute | solution.py:77
  56.6 0.8 bitcast_dynamic-update-slice_fusion.7
  57.4 5.0 %collective-permute-start.8 = (bf16[8,2,128,768]{3,2,0,1:T(8,128)(2,1)}, bf16[8,2,128,768]{3,2,0,1:T(8,128)(2,1)}, u32[]{:S(2)}, u32[]{:S(2)}) collective-permute-start(bf16[8,2,128,768]{3,2,0,1:T(8,128)(2,1)} %bitcast_dynamic-update-slice_fusion.7), channel_id=1, source_target_pairs={{0,8},{8,0},{1,9},{9,1},{2,10},{10,2},{3,11},{11,3},{4,12},{12,4},... | collective-permute-start | bytes 9437192 | tf_op jit(solution)/shard_map/ppermute | solution.py:82
  63.1 0.3 pad_add_fusion
  63.4 2.2 %broadcast_in_dim.83 = pred[4,384,1536]{1,0,2:T(4,128)(4,1)S(1)} broadcast(pred[384,1536]{0,1:T(8,128)(4,1)S(1)} %pad_add_fusion), dimensions={1,2} | broadcast | bytes 2949120 | tf_op jit(solution)/shard_map/while/body/eval_jaxpr/jit(_where)/broadcast_in_dim | solution.py:39
  65.6 2.6 %copy.69 = pred[192,8,4,384]{3,1,2,0:T(8,128)(4,1)} copy(pred[192,8,4,384]{3,2,1,0:T(4,128)(4,1)S(1)} %bitcast.111) | data formatting | bytes 4718592
  68.5 0.2 copy.62
  68.7 3.4 %copy.65 = bf16[384,4096]{0,1:T(8,128)(2,1)S(1)} copy(bf16[384,4096]{1,0:T(8,128)(2,1)} %param.8) | data formatting | bytes 6291456 | tf_op args[0]
  72.1 1.5 dynamic-slice_bitcast_fusion.1
  73.6 1.3 copy.67
  75.0 3.3 %select_bitcast_fusion.1 = (bf16[8,2,1,128,768]{4,3,2,0,1:T(8,128)(2,1)S(1)}, bf16[8,2,1,128,768]{4,3,2,0,1:T(8,128)(2,1)S(1)}) fusion(bf16[8,2,128,768]{3,2,0,1:T(8,128)(2,1)} %bitcast_dynamic-update-slice_fusion.7, bf16[8,2,128,768]{3,2,0,1:T(8,128)(2,1)} %collective-permute-done.8, pred[]{:T(512)S(6)} %eq.16), kind=kLoop, calls=%fused_computation.16 | loop fusion | flops 3145728 | bytes 12582913 | tf_op jit(solution)/shard_map/stack | solution.py:85
  78.3 0.6 pad_maximum_fusion
  78.9 2.1 %copy-done.3 = bf16[384,4096]{1,0:T(8,128)(2,1)S(1)} copy-done((bf16[384,4096]{1,0:T(8,128)(2,1)S(1)}, bf16[384,4096]{1,0:T(8,128)(2,1)}, u32[]{:S(2)}) %copy-start.3) | copy-done | bytes 3145752
  81.0 3.4 %fusion.5 = bf16[384,768]{0,1:T(8,128)(2,1)S(1)} fusion(bf16[4096,768]{1,0:T(8,128)(2,1)S(1)} %bitcast.113, bf16[384,4096]{1,0:T(8,128)(2,1)S(1)} %copy-done.3), kind=kOutput, calls=%fused_computation.23 | convolution fusion | flops 2416214016 | bytes 10027008 | tf_op jit(solution)/shard_map/dot_general | solution.py:98
  84.5 0.7 fusion.23
  85.2 0.2 copy.57
  85.4 1.1 copy.58
  86.5 1.7 copy.59
  88.2 2.7 %fusion.25 = (f32[1536]{0:T(1024)S(1)}, f32[1536,1536]{0,1:T(8,128)S(1)}) fusion(pred[1536,1536]{0,1:T(8,128)(4,1)S(1)} %bitcast.120, bf16[1536,128]{1,0:T(8,128)(2,1)S(1)} %bitcast.127, bf16[384,128]{1,0:T(8,128)(2,1)S(1)} %copy.58, bf16[1152,128]{1,0:T(8,128)(2,1)} %bitcast.133), kind=kOutput, calls=%fused_computation.61 | convolution fusion | flops 611842560 | bytes 12589056 | tf_op jit(solution)/shard_map/while/body/eval_jaxpr/dot_general | solution.py:14
  91.0 1.3 fusion.4
  92.3 4.7 %fusion.1 = (f32[1536]{0:T(1024)S(1)}, bf16[1536,1536]{0,1:T(8,128)(2,1)}, f32[1536,1536]{1,0:T(8,128)S(1)}) fusion(f32[1536]{0:T(1024)S(1)} %fusion.4, f32[1536,1536]{0,1:T(8,128)S(1)} %get-tuple-element.54, f32[1536]{0:T(1024)S(1)} %get-tuple-element.53, bf16[1536,128]{1,0:T(8,128)(2,1)S(1)} %bitcast.124, bf16[384,128]{1,0:T(8,128)(2,1)S(1)} %copy-done.9, ...), kind=kOutput, calls=%fused_computation.4 | convolution fusion | flops 618920448 | bytes 24397824 | tf_op jit(solution)/shard_map/while/body/eval_jaxpr/dot_general | solution.py:14
  97.0 6.5 %fusion.3 = bf16[1536,1536]{0,1:T(8,128)(2,1)} fusion(bf16[1536,1536]{0,1:T(8,128)(2,1)} %get-tuple-element.30, f32[1536,1536]{1,0:T(8,128)S(1)} %get-tuple-element.55, f32[1536]{0:T(1024)S(1)} %get-tuple-element.29), kind=kLoop, calls=%fused_computation.6 | loop fusion | flops 11796480 | bytes 18880512 | tf_op jit(solution)/shard_map/while/body/eval_jaxpr/convert_element_type | solution.py:48
  103.5 3.9 %convolution_convert_fusion.1 = bf16[1536,128]{1,0:T(8,128)(2,1)S(1)} fusion(bf16[1536,1536]{0,1:T(8,128)(2,1)} %fusion.3, bf16[384,128]{1,0:T(8,128)(2,1)} %copy-done.11, bf16[1152,128]{1,0:T(8,128)(2,1)} %bitcast.134), kind=kOutput, calls=%fused_computation.17 | convolution fusion | flops 604962816 | bytes 5505024 | tf_op jit(solution)/shard_map/while/body/eval_jaxpr/dot_general | solution.py:49
  107.4 1.9 fusion.10
  109.3 1.8 fusion.13
  111.0 0.2 copy.63
  111.3 1.8 fusion.22
  113.1 0.4 collective-permute-start.9
  113.7 10.0 %collective-permute-done.9 = f32[2048,768]{1,0:T(8,128)S(1)} collective-permute-done((f32[2048,768]{1,0:T(8,128)S(1)}, f32[2048,768]{1,0:T(8,128)S(1)}, u32[]{:S(2)}, u32[]{:S(2)}) %collective-permute-start.9) | collective-permute-done | bytes 6291488 | tf_op jit(solution)/shard_map/ppermute | solution.py:127
  123.6 3.6 %add_convert_fusion = bf16[2048,768]{1,0:T(8,128)(2,1)} fusion(f32[2048,768]{1,0:T(8,128)S(1)} %collective-permute-done.9, bf16[384,2048]{0,1:T(8,128)(2,1)S(1)} %bitcast.115, bf16[384,128]{0,1:T(8,128)(2,1)S(1)} %fusion.13, bf16[384,128]{0,1:T(8,128)(2,1)S(1)} %fusion.10, bf16[384,512]{0,1:T(8,128)(2,1)S(1)} %bitcast.117), kind=kOutput, calls=%fused_computation.12 | convolution fusion | flops 1212874752 | bytes 11599872 | tf_op jit(solution)/shard_map/dot_general | solution.py:20
  127.3 5.4 %convolution_convert_fusion = bf16[384,4096]{1,0:T(8,128)(2,1)S(1)} fusion(bf16[4096,768]{1,0:T(8,128)(2,1)} %bitcast.114, bf16[384,128]{0,1:T(8,128)(2,1)S(1)} %fusion.13, bf16[384,128]{0,1:T(8,128)(2,1)S(1)} %fusion.10, bf16[384,512]{0,1:T(8,128)(2,1)S(1)} %bitcast.118), kind=kOutput, calls=%fused_computation.13 | convolution fusion | flops 2419261440 | bytes 10027008 | tf_op jit(solution)/shard_map/dot_general | solution.py:14
  132.7 1.9 %copy.73 = bf16[48,8,8,512]{3,2,0,1:T(8,128)(2,1)} copy(bf16[48,8,8,512]{3,2,1,0:T(8,128)(2,1)S(1)} %bitcast.119) | data formatting | bytes 6291456 | tf_op jit(solution)/shard_map/reshape | solution.py:136
  134.7 6.8 %all-to-all-start = ((bf16[8,384,512]{2,1,0:T(8,128)(2,1)}), bf16[8,384,512]{2,1,0:T(8,128)(2,1)S(1)}, u32[]{:S(2)}, u32[]{:S(2)}) async-start(bf16[8,384,512]{2,1,0:T(8,128)(2,1)} %bitcast.107), calls=%async_computation | async-start | bytes 6291456 | tf_op jit(solution)/shard_map/all_to_all | solution.py:137
  141.4 28.9 %reduce-scatter.2.cloned.1.call-done = bf16[256,768]{1,0:T(8,128)(2,1)} async-done(((bf16[2048,768]{1,0:T(8,128)(2,1)}), bf16[256,768]{1,0:T(8,128)(2,1)}) %reduce-scatter.2.cloned.1.call-update) | async-done | bytes 393232 | tf_op jit(solution)/shard_map/reduce_scatter | solution.py:130
  170.3 1.6 dynamic-slice_bitcast_fusion.2
  171.9 1.3 collective-permute-start.10
  173.2 3.8 %convolution_convert_fusion.2 = bf16[1536,128]{1,0:T(8,128)(2,1)S(1)} fusion(bf16[1536,1536]{0,1:T(8,128)(2,1)} %get-tuple-element.30, bf16[384,128]{1,0:T(8,128)(2,1)S(1)} %copy-done.10, bf16[1152,128]{1,0:T(8,128)(2,1)S(1)} %bitcast.136), kind=kOutput, calls=%fused_computation.18 | convolution fusion | flops 604962816 | bytes 5505024 | tf_op jit(solution)/shard_map/while/body/eval_jaxpr/dot_general | solution.py:44
  177.0 0.3 copy.60
  177.3 0.8 copy.74
  178.1 2.7 %all-to-all-done = bf16[8,384,512]{2,1,0:T(8,128)(2,1)S(1)} async-done(((bf16[8,384,512]{2,1,0:T(8,128)(2,1)}), bf16[8,384,512]{2,1,0:T(8,128)(2,1)S(1)}, u32[]{:S(2)}, u32[]{:S(2)}) %all-to-all-start) | async-done | bytes 3145760 | tf_op jit(solution)/shard_map/all_to_all | solution.py:137
  180.8 1.3 reduce_sum.34
  182.1 1.0 fusion.16
  183.1 0.7 slice.42
  183.8 0.7 fusion.24
  (45 shorter events, 0.7 us)
Async XLA Ops:
  7.2 163.2 %reduce-scatter.2.cloned.1.call-start = ((), (), s32[]{:S(2)}) async-start(), calls=%async_computation.2 | async-start | bytes 3538944 | tf_op jit(solution)/shard_map/reduce_scatter | solution.py:130
  9.7 5.5 %collective-permute-start = (bf16[128,768]{1,0:T(8,128)(2,1)S(1)}, bf16[128,768]{1,0:T(8,128)(2,1)S(1)}, u32[]{:S(2)}, u32[]{:S(2)}) collective-permute-start(bf16[128,768]{1,0:T(8,128)(2,1)S(1)} %constant_dynamic-update-slice_fusion), channel_id=1, source_target_pairs={{0,128},{128,0},{1,129},{129,1},{2,130},{130,2},{3,131},{131,3},{4... | collective-permute-start | bytes 589832 | tf_op jit(solution)/shard_map/ppermute | solution.py:68
  15.2 14.8 %collective-permute-start.1 = (bf16[2,128,768]{2,1,0:T(8,128)(2,1)S(1)}, bf16[2,128,768]{2,1,0:T(8,128)(2,1)S(1)}, u32[]{:S(2)}, u32[]{:S(2)}) collective-permute-start(bf16[2,128,768]{2,1,0:T(8,128)(2,1)S(1)} %pad_maximum_fusion.2), channel_id=1, source_target_pairs={{0,16},{16,32},{32,48},{48,64},{64,80},{80,96},{96,112},{112,0},{1... | collective-permute-start | bytes 1179656 | tf_op jit(solution)/shard_map/ppermute | solution.py:77
  18.1 11.9 %collective-permute-start.2 = (bf16[2,128,768]{2,1,0:T(8,128)(2,1)S(1)}, bf16[2,128,768]{2,1,0:T(8,128)(2,1)S(1)}, u32[]{:S(2)}, u32[]{:S(2)}) collective-permute-start(bf16[2,128,768]{2,1,0:T(8,128)(2,1)S(1)} %pad_maximum_fusion.2), channel_id=1, source_target_pairs={{0,112},{16,0},{32,16},{48,32},{64,48},{80,64},{96,80},{112,96},{1... | collective-permute-start | bytes 1179656 | tf_op jit(solution)/shard_map/ppermute | solution.py:80
  30.1 9.8 %collective-permute-start.3 = (bf16[2,128,768]{2,1,0:T(8,128)(2,1)S(1)}, bf16[2,128,768]{2,1,0:T(8,128)(2,1)S(1)}, u32[]{:S(2)}, u32[]{:S(2)}) collective-permute-start(bf16[2,128,768]{2,1,0:T(8,128)(2,1)S(1)} %collective-permute-done.1), channel_id=1, source_target_pairs={{0,16},{16,32},{32,48},{48,64},{64,80},{80,96},{96,112},{112,0},{1... | collective-permute-start | bytes 1179656 | tf_op jit(solution)/shard_map/ppermute | solution.py:77
  30.1 9.8 %collective-permute-start.4 = (bf16[2,128,768]{2,1,0:T(8,128)(2,1)S(1)}, bf16[2,128,768]{2,1,0:T(8,128)(2,1)S(1)}, u32[]{:S(2)}, u32[]{:S(2)}) collective-permute-start(bf16[2,128,768]{2,1,0:T(8,128)(2,1)S(1)} %collective-permute-done.2), channel_id=1, source_target_pairs={{0,112},{16,0},{32,16},{48,32},{64,48},{80,64},{96,80},{112,96},{1... | collective-permute-start | bytes 1179656 | tf_op jit(solution)/shard_map/ppermute | solution.py:80
  39.8 8.9 %collective-permute-start.5 = (bf16[2,128,768]{2,1,0:T(8,128)(2,1)S(1)}, bf16[2,128,768]{2,1,0:T(8,128)(2,1)S(1)}, u32[]{:S(2)}, u32[]{:S(2)}) collective-permute-start(bf16[2,128,768]{2,1,0:T(8,128)(2,1)S(1)} %collective-permute-done.3), channel_id=1, source_target_pairs={{0,16},{16,32},{32,48},{48,64},{64,80},{80,96},{96,112},{112,0},{1... | collective-permute-start | bytes 1179656 | tf_op jit(solution)/shard_map/ppermute | solution.py:77
  39.8 9.7 %collective-permute-start.6 = (bf16[2,128,768]{2,1,0:T(8,128)(2,1)S(1)}, bf16[2,128,768]{2,1,0:T(8,128)(2,1)S(1)}, u32[]{:S(2)}, u32[]{:S(2)}) collective-permute-start(bf16[2,128,768]{2,1,0:T(8,128)(2,1)S(1)} %collective-permute-done.4), channel_id=1, source_target_pairs={{0,112},{16,0},{32,16},{48,32},{64,48},{80,64},{96,80},{112,96},{1... | collective-permute-start | bytes 1179656 | tf_op jit(solution)/shard_map/ppermute | solution.py:80
  48.8 7.8 %collective-permute-start.7 = (bf16[2,128,768]{2,1,0:T(8,128)(2,1)S(1)}, bf16[2,128,768]{2,1,0:T(8,128)(2,1)S(1)}, u32[]{:S(2)}, u32[]{:S(2)}) collective-permute-start(bf16[2,128,768]{2,1,0:T(8,128)(2,1)S(1)} %collective-permute-done.5), channel_id=1, source_target_pairs={{0,16},{16,32},{32,48},{48,64},{64,80},{80,96},{96,112},{112,0},{1... | collective-permute-start | bytes 1179656 | tf_op jit(solution)/shard_map/ppermute | solution.py:77
  57.4 17.6 %collective-permute-start.8 = (bf16[8,2,128,768]{3,2,0,1:T(8,128)(2,1)}, bf16[8,2,128,768]{3,2,0,1:T(8,128)(2,1)}, u32[]{:S(2)}, u32[]{:S(2)}) collective-permute-start(bf16[8,2,128,768]{3,2,0,1:T(8,128)(2,1)} %bitcast_dynamic-update-slice_fusion.7), channel_id=1, source_target_pairs={{0,8},{8,0},{1,9},{9,1},{2,10},{10,2},{3,11},{11,3},{4,12},{12,4},... | collective-permute-start | bytes 9437192 | tf_op jit(solution)/shard_map/ppermute | solution.py:82
  63.4 4.9 %copy-start.5 = (bf16[384,512]{1,0:T(8,128)(2,1)S(1)}, bf16[384,512]{1,0:T(8,128)(2,1)}, u32[]{:S(2)}) copy-start(bf16[384,512]{1,0:T(8,128)(2,1)} %param.15) | copy-start | bytes 1179652
  78.2 2.7 %copy-start.3 = (bf16[384,4096]{1,0:T(8,128)(2,1)S(1)}, bf16[384,4096]{1,0:T(8,128)(2,1)}, u32[]{:S(2)}) copy-start(bf16[384,4096]{1,0:T(8,128)(2,1)} %param.8) | copy-start | bytes 9437188
  78.8 5.6 %copy-start.1 = (bf16[8,2,2,128,768]{4,3,2,0,1:T(8,128)(2,1)}, bf16[8,2,2,128,768]{4,3,2,0,1:T(8,128)(2,1)S(1)}, u32[]{:S(2)}) copy-start(bf16[8,2,2,128,768]{4,3,2,0,1:T(8,128)(2,1)S(1)} %pad_maximum_fusion) | copy-start | bytes 18874372
  81.0 7.2 %copy-start.4 = (pred[192,8,4,384]{3,1,2,0:T(8,128)(4,1)S(1)}, pred[192,8,4,384]{3,1,2,0:T(8,128)(4,1)}, u32[]{:S(2)}) copy-start(pred[192,8,4,384]{3,1,2,0:T(8,128)(4,1)} %copy.69) | copy-start | bytes 7077892
  85.4 5.5 %copy-start.6 = (bf16[384,1,4,128]{3,0,2,1:T(8,128)(2,1)}, bf16[384,1,4,128]{3,0,2,1:T(8,128)(2,1)S(1)}, u32[]{:S(2)}) copy-start(bf16[384,1,4,128]{3,0,2,1:T(8,128)(2,1)S(1)} %copy.57) | copy-start | bytes 1179652
  86.5 4.4 %copy-start.11 = (bf16[384,128]{1,0:T(8,128)(2,1)}, bf16[384,128]{1,0:T(8,128)(2,1)S(1)}, u32[]{:S(2)}) copy-start(bf16[384,128]{1,0:T(8,128)(2,1)S(1)} %copy.58) | copy-start | bytes 294916
  90.9 1.3 copy-start.9
  90.9 1.3 copy-start.12
  103.5 3.9 %copy-start.7 = (bf16[384,1,4,128]{3,0,2,1:T(8,128)(2,1)S(1)}, bf16[384,1,4,128]{3,0,2,1:T(8,128)(2,1)}, u32[]{:S(2)}) copy-start(bf16[384,1,4,128]{3,0,2,1:T(8,128)(2,1)} %copy-done.6) | copy-start | bytes 1179652
  107.4 3.9 %copy-start = (bf16[384,8,2,1,128]{0,4,2,1,3:T(8,128)(2,1)S(1)}, bf16[384,8,2,1,128]{0,4,2,1,3:T(8,128)(2,1)}, u32[]{:S(2)}) copy-start(bf16[384,8,2,1,128]{0,4,2,1,3:T(8,128)(2,1)} %copy.67) | copy-start | bytes 4718596
  111.3 2.2 %copy-start.2 = (bf16[384,8,2,1,128]{0,4,3,1,2:T(8,128)(2,1)S(1)}, bf16[384,8,2,1,128]{0,4,3,1,2:T(8,128)(2,1)}, u32[]{:S(2)}) copy-start(bf16[384,8,2,1,128]{0,4,3,1,2:T(8,128)(2,1)} %get-tuple-element.33) | copy-start | bytes 4718596
  113.1 10.5 %collective-permute-start.9 = (f32[2048,768]{1,0:T(8,128)S(1)}, f32[2048,768]{1,0:T(8,128)S(1)}, u32[]{:S(2)}, u32[]{:S(2)}) collective-permute-start(f32[2048,768]{1,0:T(8,128)S(1)} %fusion.22), channel_id=1, source_target_pairs={{0,8},{8,0},{1,9},{9,1},{2,10},{10,2},{3,11},{11,3},{4,12},{12,4},... | collective-permute-start | bytes 18874376 | tf_op jit(solution)/shard_map/ppermute | solution.py:127
  134.7 38.6 %copy-start.10 = (bf16[384,128]{1,0:T(8,128)(2,1)S(1)}, bf16[384,128]{1,0:T(8,128)(2,1)}, u32[]{:S(2)}) copy-start(bf16[384,128]{1,0:T(8,128)(2,1)} %copy.59) | copy-start | bytes 294916
  134.7 38.6 %copy-start.13 = (bf16[1,1152,128]{2,1,0:T(8,128)(2,1)S(1)}, bf16[1,1152,128]{2,1,0:T(8,128)(2,1)}, u32[]{:S(2)}) copy-start(bf16[1,1152,128]{2,1,0:T(8,128)(2,1)} %param.14) | copy-start | bytes 884740
  134.7 46.1 %all-to-all-start = ((bf16[8,384,512]{2,1,0:T(8,128)(2,1)}), bf16[8,384,512]{2,1,0:T(8,128)(2,1)S(1)}, u32[]{:S(2)}, u32[]{:S(2)}) async-start(bf16[8,384,512]{2,1,0:T(8,128)(2,1)} %bitcast.107), calls=%async_computation | async-start | bytes 6291456 | tf_op jit(solution)/shard_map/all_to_all | solution.py:137
  171.9 10.2 %collective-permute-start.10 = (bf16[128,768]{1,0:T(8,128)(2,1)}, bf16[128,768]{1,0:T(8,128)(2,1)}, u32[]{:S(2)}, u32[]{:S(2)}) collective-permute-start(bf16[128,768]{1,0:T(8,128)(2,1)} %dynamic-slice_bitcast_fusion.2), channel_id=1, source_target_pairs={{0,128},{128,0},{1,129},{129,1},{2,130},{130,2},{3,131},{131,3},{4... | collective-permute-start | bytes 589832 | tf_op jit(solution)/shard_map/ppermute | solution.py:134
  177.0 5.1 %copy-start.8 = (bf16[256,768]{1,0:T(8,128)(2,1)S(1)}, bf16[256,768]{1,0:T(8,128)(2,1)}, u32[]{:S(2)}) copy-start(bf16[256,768]{1,0:T(8,128)(2,1)} %reduce-scatter.2.cloned.1.call-done) | copy-start | bytes 1179652
Sparse Core Ops, SparseCore 0:
  127.4 42.9 reduce-scatter.1

commit v5 on v4

--- a/solution.py
+++ b/solution.py
@@ -69,21 +69,25 @@
     pair = jnp.stack([jnp.where(x_pos == 0, block, peer), jnp.where(x_pos == 0, peer, block)])
     ahead = [(i, (i + 1) % z_count) for i in range(z_count)]
     behind = [(i, (i - 1) % z_count) for i in range(z_count)]
-    ring = jnp.zeros((z_count,) + pair.shape, pair.dtype)
-    ring = lax.dynamic_update_index_in_dim(ring, pair, z_pos, 0)
+    got = [(pair, z_pos)]
     fwd = pair
     bwd = pair
     for step in range(1, z_count // 2 + 1):
         fwd = lax.ppermute(fwd, "z", ahead)
-        ring = lax.dynamic_update_index_in_dim(ring, fwd, (z_pos - step) % z_count, 0)
+        got.append((fwd, (z_pos - step) % z_count))
         if step < z_count - z_count // 2:
             bwd = lax.ppermute(bwd, "z", behind)
-            ring = lax.dynamic_update_index_in_dim(ring, bwd, (z_pos + step) % z_count, 0)
-    other = lax.ppermute(ring, "c", SWAP)
-    first = jnp.where(chip_core == 0, ring, other)
-    second = jnp.where(chip_core == 0, other, ring)
-    full = jnp.stack([first, second], 2)
-    return full.transpose(1, 0, 2, 3, 4).reshape(-1, width)
+            got.append((bwd, (z_pos + step) % z_count))
+    full = jnp.zeros((2, z_count, 2, rows, width), block.dtype)
+    early = len(got) // 2 + 1
+    for lo, hi in ((0, early), (early, len(got))):
+        mine = jnp.stack([chunk for chunk, _ in got[lo:hi]])
+        theirs = lax.ppermute(mine, "c", SWAP)
+        for k in range(hi - lo):
+            place = got[lo + k][1]
+            full = lax.dynamic_update_slice(full, mine[k][:, None, None], (0, place, chip_core, 0, 0))
+            full = lax.dynamic_update_slice(full, theirs[k][:, None, None], (0, place, 1 - chip_core, 0, 0))
+    return full.reshape(-1, width)
 
 
 def local(hidden_in, w_query, w_key, w_value, starts, key_cache, value_cache, grad_out):
@@ -124,9 +128,9 @@
     cols_other = lax.dynamic_index_in_dim(by_place, 1 - chip_core, 3, False)
     cols_own = lax.dynamic_index_in_dim(by_place, chip_core, 3, False)
     part_other = contract_first(cols_other.reshape(tokens_dev, -1), grads_cat)
-    from_peer = lax.ppermute(part_other, "c", SWAP)
+    from_peer = lax.ppermute(part_other.astype(jnp.bfloat16), "c", SWAP)
     part_own = contract_first(cols_own.reshape(tokens_dev, -1), grads_cat)
-    chip_sum = (part_own + from_peer).astype(jnp.bfloat16)
+    chip_sum = (part_own + from_peer.astype(jnp.float32)).astype(jnp.bfloat16)
     ring_sum = lax.psum_scatter(chip_sum, "z", scatter_dimension=0, tiled=True)
     ring_sum = ring_sum.reshape(2, rows, -1)
     keep = lax.dynamic_index_in_dim(ring_sum, x_pos, 0, False)

time: 192 us -> 192 us (level)
  waiting for transfers between devices: 66.5 us -> 61.6 us
  local copies, waits for them, and re-layouts: 33.8 us -> 38.1 us
  matrix products: 33 us -> 36 us
  other arithmetic: 15.2 us -> 12.7 us
    ppermute x2 -> x3, waiting for transfers between devices: 9.97 us -> 5.42 us  [the longest x1 5.41 us: local(): from_peer = lax.ppermute(part_other.astype(jnp.bfloat16), 'c', SWAP)]
    dynamic_update_slice x7 -> x15, local copies, waits for them, and re-layouts: 5.49 us -> 9.63 us  [the longest x8 5.41 us: gather_rows(): lax.dynamic_update_slice(full, theirs[k][:, None, None], (0, place, 1 - c...]
    another operation x2 -> x1, other arithmetic: 3.84 us -> 1.4 us  [gather_rows(): mine = jnp.stack([chunk for chunk, _ in got[lo:hi]])]
    dot_general x4, matrix products: 9.06 us -> 11.2 us  [contract_first(): lax.dot_general(left, right, (((0,), (0,)), ((), ())), preferred_element_...]
    ppermute x2 -> x3, starting transfers between devices: 5.32 us -> 4.46 us  [the longest x2 4.09 us: gather_rows(): theirs = lax.ppermute(mine, 'c', SWAP)]
    unnamed x34 -> x55, local copies, waits for them, and re-layouts: 11 us -> 11.3 us
  transfers between devices with their start and end apart: 13 -> 14, of which waited for: 8 -> 7; matrix products, arithmetic and copies ran while one was open for 18% -> 21% of each run, Pallas kernels for 0% -> 0%
where the time goes in v5:
time: 192 us; the launch traced here: 191 us
  waiting for transfers between devices  61.6 us (32%)
  local copies, waits for them, and re-layouts  38.1 us (20%)
  matrix products  36 us (19%)
  starting transfers between devices  26.9 us (14%)
  between operations  15.3 us (8%)
  other arithmetic  12.7 us (7%)
    reduce_scatter x1, waiting for transfers between devices, local(): ring_sum = lax.psum_scatter(chip_sum, 'z', scatter_dimension=0, tiled=True)  29.8 us
    ppermute x4, waiting for transfers between devices, gather_rows(): fwd = lax.ppermute(fwd, 'z', ahead)  21.1 us
    dot_general x3, matrix products, contract_last(): lax.dot_general(left, right, (((1,), (1,)), ((), ())), preferred_element_...  12.8 us
    unnamed x55, local copies, waits for them, and re-layouts  11.3 us
    dot_general x4, matrix products, contract_first(): lax.dot_general(left, right, (((0,), (0,)), ((), ())), preferred_element_...  11.2 us
    ppermute x3, starting transfers between devices, gather_rows(): bwd = lax.ppermute(bwd, 'z', behind)  9.44 us
    all_to_all x1, starting transfers between devices, local(): gathered = lax.all_to_all(input_term, 'tp', 0, 0, tiled=True)  6.65 us
    convert_element_type x1, other arithmetic, head_pass(): (probs_wide * (grad_probs - row_dot) * factor).astype(jnp.bfloat16)  6.48 us
  transfers between devices with their start and end apart: 14, of which 7 were waited for; matrix products, arithmetic and copies ran while one was open for 21% of the time, Pallas kernels for 0%

profile of v5, /device:TPU:1, one launch (start us, length us, event | category | flops | bytes accessed | tf_op | source)
XLA Modules:
  0.0 190.6 jit_solution(16946360691351111825)
XLA Ops:
  7.2 0.9 constant_dynamic-update-slice_fusion.2
  8.1 0.8 constant_dynamic-update-slice_fusion.1
  8.9 0.8 constant_dynamic-update-slice_fusion
  9.7 2.1 %collective-permute-start = (bf16[128,768]{1,0:T(8,128)(2,1)S(1)}, bf16[128,768]{1,0:T(8,128)(2,1)S(1)}, u32[]{:S(2)}, u32[]{:S(2)}) collective-permute-start(bf16[128,768]{1,0:T(8,128)(2,1)S(1)} %constant_dynamic-update-slice_fusion), channel_id=1, source_target_pairs={{0,128},{128,0},{1,129},{129,1},{2,130},{130,2},{3,131},{131,3},{4... | collective-permute-start | bytes 589832 | tf_op jit(solution)/shard_map/ppermute | solution.py:68
  11.8 3.4 %collective-permute-done = bf16[128,768]{1,0:T(8,128)(2,1)S(1)} collective-permute-done((bf16[128,768]{1,0:T(8,128)(2,1)S(1)}, bf16[128,768]{1,0:T(8,128)(2,1)S(1)}, u32[]{:S(2)}, u32[]{:S(2)}) %collective-permute-start) | collective-permute-done | bytes 196640 | tf_op jit(solution)/shard_map/ppermute | solution.py:68
  15.2 2.9 %collective-permute-start.1 = (bf16[2,128,768]{2,1,0:T(8,128)(2,1)S(1)}, bf16[2,128,768]{2,1,0:T(8,128)(2,1)S(1)}, u32[]{:S(2)}, u32[]{:S(2)}) collective-permute-start(bf16[2,128,768]{2,1,0:T(8,128)(2,1)S(1)} %pad_maximum_fusion.2), channel_id=1, source_target_pairs={{0,16},{16,32},{32,48},{48,64},{64,80},{80,96},{96,112},{112,0},{1... | collective-permute-start | bytes 1179656 | tf_op jit(solution)/shard_map/ppermute | solution.py:76
  18.1 4.0 %collective-permute-start.2 = (bf16[2,128,768]{2,1,0:T(8,128)(2,1)S(1)}, bf16[2,128,768]{2,1,0:T(8,128)(2,1)S(1)}, u32[]{:S(2)}, u32[]{:S(2)}) collective-permute-start(bf16[2,128,768]{2,1,0:T(8,128)(2,1)S(1)} %pad_maximum_fusion.2), channel_id=1, source_target_pairs={{0,112},{16,0},{32,16},{48,32},{64,48},{80,64},{96,80},{112,96},{1... | collective-permute-start | bytes 1179656 | tf_op jit(solution)/shard_map/ppermute | solution.py:79
  22.2 0.8 bitcast_dynamic-update-slice_fusion.12
  22.9 7.1 %collective-permute-done.1 = bf16[2,128,768]{2,1,0:T(8,128)(2,1)S(1)} collective-permute-done((bf16[2,128,768]{2,1,0:T(8,128)(2,1)S(1)}, bf16[2,128,768]{2,1,0:T(8,128)(2,1)S(1)}, u32[]{:S(2)}, u32[]{:S(2)}) %collective-permute-start.1) | collective-permute-done | bytes 393248 | tf_op jit(solution)/shard_map/ppermute | solution.py:76
  30.1 2.7 %collective-permute-start.4 = (bf16[2,128,768]{2,1,0:T(8,128)(2,1)S(1)}, bf16[2,128,768]{2,1,0:T(8,128)(2,1)}, u32[]{:S(2)}, u32[]{:S(2)}) collective-permute-start(bf16[2,128,768]{2,1,0:T(8,128)(2,1)S(1)} %collective-permute-done.2), channel_id=1, source_target_pairs={{0,112},{16,0},{32,16},{48,32},{64,48},{80,64},{96,80},{112,96},{1... | collective-permute-start | bytes 1179656 | tf_op jit(solution)/shard_map/ppermute | solution.py:79
  32.7 0.8 bitcast_dynamic-update-slice_fusion.11
  33.5 0.8 bitcast_dynamic-update-slice_fusion.10
  34.3 5.5 %collective-permute-done.3 = bf16[2,128,768]{2,1,0:T(8,128)(2,1)S(1)} collective-permute-done((bf16[2,128,768]{2,1,0:T(8,128)(2,1)S(1)}, bf16[2,128,768]{2,1,0:T(8,128)(2,1)S(1)}, u32[]{:S(2)}, u32[]{:S(2)}) %collective-permute-start.3) | collective-permute-done | bytes 393248 | tf_op jit(solution)/shard_map/ppermute | solution.py:76
  39.8 0.8 bitcast_dynamic-update-slice_fusion.9
  40.7 1.8 bitcast_dynamic-update-slice_fusion.8
  42.5 3.0 %collective-permute-start.5 = (bf16[5,2,128,768]{3,2,1,0:T(8,128)(2,1)}, bf16[5,2,128,768]{3,2,1,0:T(8,128)(2,1)}, u32[]{:S(2)}, u32[]{:S(2)}) collective-permute-start(bf16[5,2,128,768]{3,2,1,0:T(8,128)(2,1)} %bitcast_dynamic-update-slice_fusion.8), channel_id=1, source_target_pairs={{0,8},{8,0},{1,9},{9,1},{2,10},{10,2},{3,11},{11,3},{4,12},{12,4},... | collective-permute-start | bytes 5898248 | tf_op jit(solution)/shard_map/ppermute | solution.py:85
  46.2 2.7 %collective-permute-start.7 = (bf16[2,128,768]{2,1,0:T(8,128)(2,1)}, bf16[2,128,768]{2,1,0:T(8,128)(2,1)}, u32[]{:S(2)}, u32[]{:S(2)}) collective-permute-start(bf16[2,128,768]{2,1,0:T(8,128)(2,1)} %collective-permute-done.4), channel_id=1, source_target_pairs={{0,112},{16,0},{32,16},{48,32},{64,48},{80,64},{96,80},{112,96},{1... | collective-permute-start | bytes 1179656 | tf_op jit(solution)/shard_map/ppermute | solution.py:79
  48.9 8.5 %collective-permute-done.6 = bf16[2,128,768]{2,1,0:T(8,128)(2,1)} collective-permute-done((bf16[2,128,768]{2,1,0:T(8,128)(2,1)S(1)}, bf16[2,128,768]{2,1,0:T(8,128)(2,1)}, u32[]{:S(2)}, u32[]{:S(2)}) %collective-permute-start.6) | collective-permute-done | bytes 393248 | tf_op jit(solution)/shard_map/ppermute | solution.py:76
  58.0 2.2 %broadcast_in_dim.58 = pred[4,384,1536]{1,0,2:T(4,128)(4,1)S(1)} broadcast(pred[384,1536]{0,1:T(8,128)(4,1)S(1)} %pad_add_fusion), dimensions={1,2} | broadcast | bytes 2949120 | tf_op jit(solution)/shard_map/while/body/eval_jaxpr/jit(_where)/broadcast_in_dim | solution.py:39
  60.2 2.7 %copy.90 = pred[192,8,4,384]{3,1,2,0:T(8,128)(4,1)} copy(pred[192,8,4,384]{3,2,1,0:T(4,128)(4,1)S(1)} %bitcast.164) | data formatting | bytes 4718592
  63.0 1.0 copy.83
  64.0 3.4 %copy.86 = bf16[384,4096]{0,1:T(8,128)(2,1)S(1)} copy(bf16[384,4096]{1,0:T(8,128)(2,1)} %param.8) | data formatting | bytes 6291456 | tf_op args[0]
  67.4 1.5 dynamic-slice_bitcast_fusion.1
  68.9 1.4 copy.88
  70.3 0.7 broadcast_in_dim.60
  71.1 1.4 pad_maximum_fusion
  72.5 1.1 collective-permute-start.9
  73.6 1.0 fusion.23
  74.7 1.0 fusion.22
  75.8 1.2 fusion.21
  77.0 1.0 fusion.20
  78.1 1.0 bitcast_dynamic-update-slice_fusion.3
  79.1 1.0 fusion.19
  80.1 1.0 bitcast_dynamic-update-slice_fusion.2
  81.2 1.0 bitcast_dynamic-update-slice_fusion.1
  82.3 1.0 bitcast_dynamic-update-slice_fusion
  83.4 3.5 %fusion.5 = bf16[384,768]{0,1:T(8,128)(2,1)S(1)} fusion(bf16[4096,768]{1,0:T(8,128)(2,1)S(1)} %bitcast.165, bf16[384,4096]{1,0:T(8,128)(2,1)S(1)} %copy-done.2), kind=kOutput, calls=%fused_computation.21 | convolution fusion | flops 2416214016 | bytes 10027008 | tf_op jit(solution)/shard_map/dot_general | solution.py:102
  87.4 0.7 copy.80
  88.1 2.7 %fusion.33 = (f32[1536]{0:T(1024)S(1)}, f32[1536,1536]{0,1:T(8,128)S(1)}) fusion(pred[1536,1536]{0,1:T(8,128)(4,1)S(1)} %bitcast.168, bf16[1536,128]{1,0:T(8,128)(2,1)S(1)} %bitcast.180, bf16[384,128]{1,0:T(8,128)(2,1)S(1)} %copy.79, bf16[1152,128]{1,0:T(8,128)(2,1)} %bitcast.186), kind=kOutput, calls=%fused_computation.81 | convolution fusion | flops 611842560 | bytes 12589056 | tf_op jit(solution)/shard_map/while/body/eval_jaxpr/dot_general | solution.py:14
  90.9 1.3 fusion.4
  92.2 4.6 %fusion.1 = (f32[1536]{0:T(1024)S(1)}, bf16[1536,1536]{0,1:T(8,128)(2,1)}, f32[1536,1536]{1,0:T(8,128)S(1)}) fusion(f32[1536]{0:T(1024)S(1)} %fusion.4, f32[1536,1536]{0,1:T(8,128)S(1)} %get-tuple-element.52, f32[1536]{0:T(1024)S(1)} %get-tuple-element.51, bf16[1536,128]{1,0:T(8,128)(2,1)S(1)} %bitcast.174, bf16[384,128]{1,0:T(8,128)(2,1)S(1)} %copy-done.16, ...), kind=kOutput, calls=%fused_computation.4 | convolution fusion | flops 618920448 | bytes 24397824 | tf_op jit(solution)/shard_map/while/body/eval_jaxpr/dot_general | solution.py:14
  96.8 6.5 %fusion.3 = bf16[1536,1536]{0,1:T(8,128)(2,1)} fusion(bf16[1536,1536]{0,1:T(8,128)(2,1)} %get-tuple-element.30, f32[1536,1536]{1,0:T(8,128)S(1)} %get-tuple-element.53, f32[1536]{0:T(1024)S(1)} %get-tuple-element.29), kind=kLoop, calls=%fused_computation.6 | loop fusion | flops 11796480 | bytes 18880512 | tf_op jit(solution)/shard_map/while/body/eval_jaxpr/convert_element_type | solution.py:48
  103.3 4.7 %convolution_convert_fusion.2 = bf16[1536,128]{1,0:T(8,128)(2,1)} fusion(bf16[1536,1536]{0,1:T(8,128)(2,1)} %fusion.3, bf16[384,128]{1,0:T(8,128)(2,1)} %copy-done.17, bf16[1152,128]{1,0:T(8,128)(2,1)} %bitcast.187), kind=kOutput, calls=%fused_computation.15 | convolution fusion | flops 604962816 | bytes 5505024 | tf_op jit(solution)/shard_map/while/body/eval_jaxpr/dot_general | solution.py:49
  108.1 2.4 %fusion.10 = bf16[384,128]{0,1:T(8,128)(2,1)} fusion(bf16[1536,128]{1,0:T(8,128)(2,1)S(1)} %bitcast.181, bf16[1536,1536]{0,1:T(8,128)(2,1)} %fusion.3), kind=kOutput, calls=%fused_computation.27 | convolution fusion | flops 151044096 | bytes 1671168 | tf_op jit(solution)/shard_map/while/body/eval_jaxpr/dot_general | solution.py:20
  110.5 2.4 %fusion.13 = bf16[384,128]{0,1:T(8,128)(2,1)} fusion(bf16[1536,128]{1,0:T(8,128)(2,1)S(1)} %bitcast.175, bf16[1536,1536]{0,1:T(8,128)(2,1)} %get-tuple-element.30), kind=kOutput, calls=%fused_computation.28 | convolution fusion | flops 151044096 | bytes 1671168 | tf_op jit(solution)/shard_map/while/body/eval_jaxpr/dot_general | solution.py:20
  112.9 1.3 copy.84
  114.2 2.8 %convolution_convert_fusion.1 = bf16[2048,768]{1,0:T(8,128)(2,1)S(1)} fusion(bf16[384,2048]{0,1:T(8,128)(2,1)S(1)} %bitcast.169, bf16[384,128]{0,1:T(8,128)(2,1)} %fusion.13, bf16[384,128]{0,1:T(8,128)(2,1)} %fusion.10, bf16[384,512]{0,1:T(8,128)(2,1)S(1)} %bitcast.177), kind=kOutput, calls=%fused_computation.13 | convolution fusion | flops 1211301888 | bytes 5308416 | tf_op jit(solution)/shard_map/dot_general | solution.py:20
  117.0 0.4 collective-permute-start.10
  117.6 5.4 %collective-permute-done.10 = bf16[2048,768]{1,0:T(8,128)(2,1)S(1)} collective-permute-done((bf16[2048,768]{1,0:T(8,128)(2,1)S(1)}, bf16[2048,768]{1,0:T(8,128)(2,1)S(1)}, u32[]{:S(2)}, u32[]{:S(2)}) %collective-permute-start.10) | collective-permute-done | bytes 3145760 | tf_op jit(solution)/shard_map/ppermute | solution.py:131
  123.1 3.6 %add_convert_fusion = bf16[2048,768]{1,0:T(8,128)(2,1)} fusion(bf16[2048,768]{1,0:T(8,128)(2,1)S(1)} %collective-permute-done.10, bf16[384,2048]{0,1:T(8,128)(2,1)S(1)} %bitcast.170, bf16[384,128]{0,1:T(8,128)(2,1)S(1)} %copy-done.21, bf16[384,128]{0,1:T(8,128)(2,1)S(1)} %copy-done.19, bf16[384,512]{0,1:T(8,128)(2,1)S(1)} %bitcast.178), kind=kOutput, calls=%fused_computation.11 | convolution fusion | flops 1214447616 | bytes 8454144 | tf_op jit(solution)/shard_map/dot_general | solution.py:20
  126.7 5.4 %convolution_convert_fusion = bf16[384,4096]{1,0:T(8,128)(2,1)S(1)} fusion(bf16[4096,768]{1,0:T(8,128)(2,1)} %bitcast.166, bf16[384,128]{0,1:T(8,128)(2,1)S(1)} %copy-done.22, bf16[384,128]{0,1:T(8,128)(2,1)S(1)} %copy-done.20, bf16[384,512]{0,1:T(8,128)(2,1)S(1)} %bitcast.179), kind=kOutput, calls=%fused_computation.12 | convolution fusion | flops 2419261440 | bytes 10027008 | tf_op jit(solution)/shard_map/dot_general | solution.py:14
  132.1 1.9 %copy.94 = bf16[48,8,8,512]{3,2,0,1:T(8,128)(2,1)} copy(bf16[48,8,8,512]{3,2,1,0:T(8,128)(2,1)S(1)} %bitcast.167) | data formatting | bytes 6291456 | tf_op jit(solution)/shard_map/reshape | solution.py:140
  134.1 6.6 %all-to-all-start = ((bf16[8,384,512]{2,1,0:T(8,128)(2,1)}), bf16[8,384,512]{2,1,0:T(8,128)(2,1)S(1)}, u32[]{:S(2)}, u32[]{:S(2)}) async-start(bf16[8,384,512]{2,1,0:T(8,128)(2,1)} %bitcast.160), calls=%async_computation | async-start | bytes 6291456 | tf_op jit(solution)/shard_map/all_to_all | solution.py:141
  140.7 29.8 %reduce-scatter.2.cloned.1.call-done = bf16[256,768]{1,0:T(8,128)(2,1)} async-done(((bf16[2048,768]{1,0:T(8,128)(2,1)}), bf16[256,768]{1,0:T(8,128)(2,1)}) %reduce-scatter.2.cloned.1.call-update) | async-done | bytes 393232 | tf_op jit(solution)/shard_map/reduce_scatter | solution.py:134
  170.6 1.6 dynamic-slice_bitcast_fusion.2
  172.2 1.2 collective-permute-start.11
  173.3 3.8 %convolution_convert_fusion.3 = bf16[1536,128]{1,0:T(8,128)(2,1)S(1)} fusion(bf16[1536,1536]{0,1:T(8,128)(2,1)} %get-tuple-element.30, bf16[384,128]{1,0:T(8,128)(2,1)} %copy.80, bf16[1152,128]{1,0:T(8,128)(2,1)} %bitcast.188), kind=kOutput, calls=%fused_computation.16 | convolution fusion | flops 604962816 | bytes 5505024 | tf_op jit(solution)/shard_map/while/body/eval_jaxpr/dot_general | solution.py:44
  177.2 0.3 copy.81
  177.5 0.8 copy.95
  178.3 1.8 all-to-all-done
  180.1 1.3 reduce_sum.34
  181.4 1.0 fusion.24
  182.4 0.7 slice.82
  183.1 0.7 fusion.32
  (77 shorter events, 1.8 us)
Async XLA Ops:
  7.2 163.4 %reduce-scatter.2.cloned.1.call-start = ((), (), s32[]{:S(2)}) async-start(), calls=%async_computation.2 | async-start | bytes 3538944 | tf_op jit(solution)/shard_map/reduce_scatter | solution.py:134
  9.7 5.5 %collective-permute-start = (bf16[128,768]{1,0:T(8,128)(2,1)S(1)}, bf16[128,768]{1,0:T(8,128)(2,1)S(1)}, u32[]{:S(2)}, u32[]{:S(2)}) collective-permute-start(bf16[128,768]{1,0:T(8,128)(2,1)S(1)} %constant_dynamic-update-slice_fusion), channel_id=1, source_target_pairs={{0,128},{128,0},{1,129},{129,1},{2,130},{130,2},{3,131},{131,3},{4... | collective-permute-start | bytes 589832 | tf_op jit(solution)/shard_map/ppermute | solution.py:68
  15.2 14.8 %collective-permute-start.1 = (bf16[2,128,768]{2,1,0:T(8,128)(2,1)S(1)}, bf16[2,128,768]{2,1,0:T(8,128)(2,1)S(1)}, u32[]{:S(2)}, u32[]{:S(2)}) collective-permute-start(bf16[2,128,768]{2,1,0:T(8,128)(2,1)S(1)} %pad_maximum_fusion.2), channel_id=1, source_target_pairs={{0,16},{16,32},{32,48},{48,64},{64,80},{80,96},{96,112},{112,0},{1... | collective-permute-start | bytes 1179656 | tf_op jit(solution)/shard_map/ppermute | solution.py:76
  18.1 11.9 %collective-permute-start.2 = (bf16[2,128,768]{2,1,0:T(8,128)(2,1)S(1)}, bf16[2,128,768]{2,1,0:T(8,128)(2,1)S(1)}, u32[]{:S(2)}, u32[]{:S(2)}) collective-permute-start(bf16[2,128,768]{2,1,0:T(8,128)(2,1)S(1)} %pad_maximum_fusion.2), channel_id=1, source_target_pairs={{0,112},{16,0},{32,16},{48,32},{64,48},{80,64},{96,80},{112,96},{1... | collective-permute-start | bytes 1179656 | tf_op jit(solution)/shard_map/ppermute | solution.py:79
  30.1 27.4 %copy-start.7 = (bf16[2,128,768]{2,1,0:T(8,128)(2,1)}, bf16[2,128,768]{2,1,0:T(8,128)(2,1)S(1)}, u32[]{:S(2)}) copy-start(bf16[2,128,768]{2,1,0:T(8,128)(2,1)S(1)} %collective-permute-done.1) | copy-start | bytes 1179652
  30.1 9.8 %collective-permute-start.3 = (bf16[2,128,768]{2,1,0:T(8,128)(2,1)S(1)}, bf16[2,128,768]{2,1,0:T(8,128)(2,1)S(1)}, u32[]{:S(2)}, u32[]{:S(2)}) collective-permute-start(bf16[2,128,768]{2,1,0:T(8,128)(2,1)S(1)} %collective-permute-done.1), channel_id=1, source_target_pairs={{0,16},{16,32},{32,48},{48,64},{64,80},{80,96},{96,112},{112,0},{1... | collective-permute-start | bytes 1179656 | tf_op jit(solution)/shard_map/ppermute | solution.py:76
  30.1 27.4 %copy-start.5 = (bf16[2,128,768]{2,1,0:T(8,128)(2,1)}, bf16[2,128,768]{2,1,0:T(8,128)(2,1)S(1)}, u32[]{:S(2)}) copy-start(bf16[2,128,768]{2,1,0:T(8,128)(2,1)S(1)} %collective-permute-done.2) | copy-start | bytes 1179652
  30.1 10.6 %collective-permute-start.4 = (bf16[2,128,768]{2,1,0:T(8,128)(2,1)S(1)}, bf16[2,128,768]{2,1,0:T(8,128)(2,1)}, u32[]{:S(2)}, u32[]{:S(2)}) collective-permute-start(bf16[2,128,768]{2,1,0:T(8,128)(2,1)S(1)} %collective-permute-done.2), channel_id=1, source_target_pairs={{0,112},{16,0},{32,16},{48,32},{64,48},{80,64},{96,80},{112,96},{1... | collective-permute-start | bytes 1179656 | tf_op jit(solution)/shard_map/ppermute | solution.py:79
  39.8 17.6 %copy-start.9 = (bf16[2,128,768]{2,1,0:T(8,128)(2,1)}, bf16[2,128,768]{2,1,0:T(8,128)(2,1)S(1)}, u32[]{:S(2)}) copy-start(bf16[2,128,768]{2,1,0:T(8,128)(2,1)S(1)} %collective-permute-done.3) | copy-start | bytes 1179652
  40.7 22.2 %copy-start.11 = (bf16[384,512]{1,0:T(8,128)(2,1)S(1)}, bf16[384,512]{1,0:T(8,128)(2,1)}, u32[]{:S(2)}) copy-start(bf16[384,512]{1,0:T(8,128)(2,1)} %param.15) | copy-start | bytes 1179652
  42.5 31.1 %collective-permute-start.5 = (bf16[5,2,128,768]{3,2,1,0:T(8,128)(2,1)}, bf16[5,2,128,768]{3,2,1,0:T(8,128)(2,1)}, u32[]{:S(2)}, u32[]{:S(2)}) collective-permute-start(bf16[5,2,128,768]{3,2,1,0:T(8,128)(2,1)} %bitcast_dynamic-update-slice_fusion.8), channel_id=1, source_target_pairs={{0,8},{8,0},{1,9},{9,1},{2,10},{10,2},{3,11},{11,3},{4,12},{12,4},... | collective-permute-start | bytes 5898248 | tf_op jit(solution)/shard_map/ppermute | solution.py:85
  45.4 12.0 %collective-permute-start.6 = (bf16[2,128,768]{2,1,0:T(8,128)(2,1)S(1)}, bf16[2,128,768]{2,1,0:T(8,128)(2,1)}, u32[]{:S(2)}, u32[]{:S(2)}) collective-permute-start(bf16[2,128,768]{2,1,0:T(8,128)(2,1)S(1)} %collective-permute-done.3), channel_id=1, source_target_pairs={{0,16},{16,32},{32,48},{48,64},{64,80},{80,96},{96,112},{112,0},{1... | collective-permute-start | bytes 1179656 | tf_op jit(solution)/shard_map/ppermute | solution.py:76
  46.2 24.9 %collective-permute-start.7 = (bf16[2,128,768]{2,1,0:T(8,128)(2,1)}, bf16[2,128,768]{2,1,0:T(8,128)(2,1)}, u32[]{:S(2)}, u32[]{:S(2)}) collective-permute-start(bf16[2,128,768]{2,1,0:T(8,128)(2,1)} %collective-permute-done.4), channel_id=1, source_target_pairs={{0,112},{16,0},{32,16},{48,32},{64,48},{80,64},{96,80},{112,96},{1... | collective-permute-start | bytes 1179656 | tf_op jit(solution)/shard_map/ppermute | solution.py:79
  57.4 13.6 %collective-permute-start.8 = (bf16[2,128,768]{2,1,0:T(8,128)(2,1)}, bf16[2,128,768]{2,1,0:T(8,128)(2,1)}, u32[]{:S(2)}, u32[]{:S(2)}) collective-permute-start(bf16[2,128,768]{2,1,0:T(8,128)(2,1)} %collective-permute-done.6), channel_id=1, source_target_pairs={{0,16},{16,32},{32,48},{48,64},{64,80},{80,96},{96,112},{112,0},{1... | collective-permute-start | bytes 1179656 | tf_op jit(solution)/shard_map/ppermute | solution.py:76
  70.3 4.4 %copy-start.8 = (bf16[2,128,768]{2,1,0:T(8,128)(2,1)S(1)}, bf16[2,128,768]{2,1,0:T(8,128)(2,1)}, u32[]{:S(2)}) copy-start(bf16[2,128,768]{2,1,0:T(8,128)(2,1)} %copy-done.7) | copy-start | bytes 1179652
  70.3 5.4 %copy-start.6 = (bf16[2,128,768]{2,1,0:T(8,128)(2,1)S(1)}, bf16[2,128,768]{2,1,0:T(8,128)(2,1)}, u32[]{:S(2)}) copy-start(bf16[2,128,768]{2,1,0:T(8,128)(2,1)} %copy-done.5) | copy-start | bytes 1179652
  71.0 6.0 %copy-start.10 = (bf16[2,128,768]{2,1,0:T(8,128)(2,1)S(1)}, bf16[2,128,768]{2,1,0:T(8,128)(2,1)}, u32[]{:S(2)}) copy-start(bf16[2,128,768]{2,1,0:T(8,128)(2,1)} %copy-done.9) | copy-start | bytes 1179652
  72.5 8.7 %collective-permute-start.9 = (bf16[3,2,128,768]{3,2,1,0:T(8,128)(2,1)S(1)}, bf16[3,2,128,768]{3,2,1,0:T(8,128)(2,1)S(1)}, u32[]{:S(2)}, u32[]{:S(2)}) collective-permute-start(bf16[3,2,128,768]{3,2,1,0:T(8,128)(2,1)S(1)} %pad_maximum_fusion), channel_id=1, source_target_pairs={{0,8},{8,0},{1,9},{9,1},{2,10},{10,2},{3,11},{11,3},{4,12},{12,4},... | collective-permute-start | bytes 3538952 | tf_op jit(solution)/shard_map/ppermute | solution.py:85
  75.7 7.6 %copy-start.2 = (bf16[384,4096]{1,0:T(8,128)(2,1)S(1)}, bf16[384,4096]{1,0:T(8,128)(2,1)}, u32[]{:S(2)}) copy-start(bf16[384,4096]{1,0:T(8,128)(2,1)} %param.8) | copy-start | bytes 9437188
  83.4 3.5 %copy-start = (bf16[2,8,2,128,768]{4,3,2,1,0:T(8,128)(2,1)}, bf16[2,8,2,128,768]{4,3,2,1,0:T(8,128)(2,1)S(1)}, u32[]{:S(2)}) copy-start(bf16[2,8,2,128,768]{4,3,2,1,0:T(8,128)(2,1)S(1)} %fusion.16) | copy-start | bytes 18874372
  83.4 4.7 %copy-start.3 = (pred[192,8,4,384]{3,1,2,0:T(8,128)(4,1)S(1)}, pred[192,8,4,384]{3,1,2,0:T(8,128)(4,1)}, u32[]{:S(2)}) copy-start(pred[192,8,4,384]{3,1,2,0:T(8,128)(4,1)} %copy.90) | copy-start | bytes 7077892
  87.2 3.6 %copy-start.13 = (bf16[384,1,4,128]{3,0,2,1:T(8,128)(2,1)}, bf16[384,1,4,128]{3,0,2,1:T(8,128)(2,1)S(1)}, u32[]{:S(2)}) copy-start(bf16[384,1,4,128]{3,0,2,1:T(8,128)(2,1)S(1)} %copy.78) | copy-start | bytes 1179652
  87.3 3.5 %copy-start.17 = (bf16[384,128]{1,0:T(8,128)(2,1)}, bf16[384,128]{1,0:T(8,128)(2,1)S(1)}, u32[]{:S(2)}) copy-start(bf16[384,128]{1,0:T(8,128)(2,1)S(1)} %copy.79) | copy-start | bytes 294916
  90.8 1.4 copy-start.12
  90.8 1.3 copy-start.16
  90.8 1.3 copy-start.18
  103.3 4.7 %copy-start.14 = (bf16[384,1,4,128]{3,0,2,1:T(8,128)(2,1)S(1)}, bf16[384,1,4,128]{3,0,2,1:T(8,128)(2,1)}, u32[]{:S(2)}) copy-start(bf16[384,1,4,128]{3,0,2,1:T(8,128)(2,1)} %copy-done.13) | copy-start | bytes 1179652
  103.3 10.9 %copy-start.4 = (bf16[384,8,2,1,128]{0,4,2,1,3:T(8,128)(2,1)S(1)}, bf16[384,8,2,1,128]{0,4,2,1,3:T(8,128)(2,1)}, u32[]{:S(2)}) copy-start(bf16[384,8,2,1,128]{0,4,2,1,3:T(8,128)(2,1)} %copy.88) | copy-start | bytes 4718596
  112.9 4.5 %copy-start.1 = (bf16[384,8,2,1,128]{0,4,3,1,2:T(8,128)(2,1)S(1)}, bf16[384,8,2,1,128]{0,4,3,1,2:T(8,128)(2,1)}, u32[]{:S(2)}) copy-start(bf16[384,8,2,1,128]{0,4,3,1,2:T(8,128)(2,1)} %get-tuple-element.31) | copy-start | bytes 4718596
  114.2 8.8 %copy-start.19 = (bf16[384,128]{0,1:T(8,128)(2,1)S(1)}, bf16[384,128]{0,1:T(8,128)(2,1)}, u32[]{:S(2)}) copy-start(bf16[384,128]{0,1:T(8,128)(2,1)} %fusion.10) | copy-start | bytes 294916
  114.2 8.8 %copy-start.21 = (bf16[384,128]{0,1:T(8,128)(2,1)S(1)}, bf16[384,128]{0,1:T(8,128)(2,1)}, u32[]{:S(2)}) copy-start(bf16[384,128]{0,1:T(8,128)(2,1)} %fusion.13) | copy-start | bytes 294916
  117.0 6.0 %collective-permute-start.10 = (bf16[2048,768]{1,0:T(8,128)(2,1)S(1)}, bf16[2048,768]{1,0:T(8,128)(2,1)S(1)}, u32[]{:S(2)}, u32[]{:S(2)}) collective-permute-start(bf16[2048,768]{1,0:T(8,128)(2,1)S(1)} %convolution_convert_fusion.1), channel_id=1, source_target_pairs={{0,8},{8,0},{1,9},{9,1},{2,10},{10,2},{3,11},{11,3},{4,12},{12,4},... | collective-permute-start | bytes 9437192 | tf_op jit(solution)/shard_map/ppermute | solution.py:131
  123.0 3.6 %copy-start.20 = (bf16[384,128]{0,1:T(8,128)(2,1)S(1)}, bf16[384,128]{0,1:T(8,128)(2,1)}, u32[]{:S(2)}) copy-start(bf16[384,128]{0,1:T(8,128)(2,1)} %fusion.10) | copy-start | bytes 294916
  123.1 3.6 %copy-start.22 = (bf16[384,128]{0,1:T(8,128)(2,1)S(1)}, bf16[384,128]{0,1:T(8,128)(2,1)}, u32[]{:S(2)}) copy-start(bf16[384,128]{0,1:T(8,128)(2,1)} %fusion.13) | copy-start | bytes 294916
  134.1 46.0 %all-to-all-start = ((bf16[8,384,512]{2,1,0:T(8,128)(2,1)}), bf16[8,384,512]{2,1,0:T(8,128)(2,1)S(1)}, u32[]{:S(2)}, u32[]{:S(2)}) async-start(bf16[8,384,512]{2,1,0:T(8,128)(2,1)} %bitcast.160), calls=%async_computation | async-start | bytes 6291456 | tf_op jit(solution)/shard_map/all_to_all | solution.py:141
  172.2 9.2 %copy-start.15 = (bf16[256,768]{1,0:T(8,128)(2,1)S(1)}, bf16[256,768]{1,0:T(8,128)(2,1)}, u32[]{:S(2)}) copy-start(bf16[256,768]{1,0:T(8,128)(2,1)} %reduce-scatter.2.cloned.1.call-done) | copy-start | bytes 1179652
  172.2 9.2 %collective-permute-start.11 = (bf16[128,768]{1,0:T(8,128)(2,1)}, bf16[128,768]{1,0:T(8,128)(2,1)}, u32[]{:S(2)}, u32[]{:S(2)}) collective-permute-start(bf16[128,768]{1,0:T(8,128)(2,1)} %dynamic-slice_bitcast_fusion.2), channel_id=1, source_target_pairs={{0,128},{128,0},{1,129},{129,1},{2,130},{130,2},{3,131},{131,3},{4... | collective-permute-start | bytes 589832 | tf_op jit(solution)/shard_map/ppermute | solution.py:138
Sparse Core Ops, SparseCore 0:
  126.8 43.7 reduce-scatter.1

commit v6 on v4

--- a/solution.py
+++ b/solution.py
@@ -124,9 +124,9 @@
     cols_other = lax.dynamic_index_in_dim(by_place, 1 - chip_core, 3, False)
     cols_own = lax.dynamic_index_in_dim(by_place, chip_core, 3, False)
     part_other = contract_first(cols_other.reshape(tokens_dev, -1), grads_cat)
-    from_peer = lax.ppermute(part_other, "c", SWAP)
+    from_peer = lax.ppermute(part_other.astype(jnp.bfloat16), "c", SWAP)
     part_own = contract_first(cols_own.reshape(tokens_dev, -1), grads_cat)
-    chip_sum = (part_own + from_peer).astype(jnp.bfloat16)
+    chip_sum = (part_own + from_peer.astype(jnp.float32)).astype(jnp.bfloat16)
     ring_sum = lax.psum_scatter(chip_sum, "z", scatter_dimension=0, tiled=True)
     ring_sum = ring_sum.reshape(2, rows, -1)
     keep = lax.dynamic_index_in_dim(ring_sum, x_pos, 0, False)

time: 192 us -> 188 us (0.979)
  waiting for transfers between devices: 66.5 us -> 62 us
    ppermute x1, waiting for transfers between devices: 9.97 us -> 5.46 us  [local(): from_peer = lax.ppermute(part_other.astype(jnp.bfloat16), 'c', SWAP)]
  transfers between devices with their start and end apart: 13 -> 13, of which waited for: 8 -> 8; matrix products, arithmetic and copies ran while one was open for 18% -> 19% of each run, Pallas kernels for 0% -> 0%
where the time goes in v6:
time: 188 us; the launch traced here: 187 us
  waiting for transfers between devices  62 us (33%)
  local copies, waits for them, and re-layouts  33.9 us (18%)
  matrix products  33 us (18%)
  starting transfers between devices  27.8 us (15%)
  other arithmetic  15.2 us (8%)
  between operations  15 us (8%)
    reduce_scatter x1, waiting for transfers between devices, local(): ring_sum = lax.psum_scatter(chip_sum, 'z', scatter_dimension=0, tiled=True)  28.9 us
    ppermute x4, waiting for transfers between devices, gather_rows(): fwd = lax.ppermute(fwd, 'z', ahead)  21.6 us
    dot_general x3, matrix products, contract_last(): lax.dot_general(left, right, (((1,), (1,)), ((), ())), preferred_element_...  12.8 us
    unnamed x34, local copies, waits for them, and re-layouts  11 us
    ppermute x3, starting transfers between devices, gather_rows(): bwd = lax.ppermute(bwd, 'z', behind)  9.38 us
    dot_general x4, matrix products, contract_first(): lax.dot_general(left, right, (((0,), (0,)), ((), ())), preferred_element_...  9.03 us
    all_to_all x1, starting transfers between devices, local(): gathered = lax.all_to_all(input_term, 'tp', 0, 0, tiled=True)  6.78 us
    convert_element_type x1, other arithmetic, head_pass(): (probs_wide * (grad_probs - row_dot) * factor).astype(jnp.bfloat16)  6.51 us
  transfers between devices with their start and end apart: 13, of which 8 were waited for; matrix products, arithmetic and copies ran while one was open for 19% of the time, Pallas kernels for 0%

profile of v6, /device:TPU:1, one launch (start us, length us, event | category | flops | bytes accessed | tf_op | source)
XLA Modules:
  0.0 186.8 jit_solution(7841439370694403270)
XLA Ops:
  7.2 0.9 constant_dynamic-update-slice_fusion.2
  8.1 0.8 constant_dynamic-update-slice_fusion.1
  8.9 0.8 constant_dynamic-update-slice_fusion
  9.7 2.1 %collective-permute-start = (bf16[128,768]{1,0:T(8,128)(2,1)S(1)}, bf16[128,768]{1,0:T(8,128)(2,1)S(1)}, u32[]{:S(2)}, u32[]{:S(2)}) collective-permute-start(bf16[128,768]{1,0:T(8,128)(2,1)S(1)} %constant_dynamic-update-slice_fusion), channel_id=1, source_target_pairs={{0,128},{128,0},{1,129},{129,1},{2,130},{130,2},{3,131},{131,3},{4... | collective-permute-start | bytes 589832 | tf_op jit(solution)/shard_map/ppermute | solution.py:68
  11.8 3.4 %collective-permute-done = bf16[128,768]{1,0:T(8,128)(2,1)S(1)} collective-permute-done((bf16[128,768]{1,0:T(8,128)(2,1)S(1)}, bf16[128,768]{1,0:T(8,128)(2,1)S(1)}, u32[]{:S(2)}, u32[]{:S(2)}) %collective-permute-start) | collective-permute-done | bytes 196640 | tf_op jit(solution)/shard_map/ppermute | solution.py:68
  15.2 2.9 %collective-permute-start.1 = (bf16[2,128,768]{2,1,0:T(8,128)(2,1)S(1)}, bf16[2,128,768]{2,1,0:T(8,128)(2,1)S(1)}, u32[]{:S(2)}, u32[]{:S(2)}) collective-permute-start(bf16[2,128,768]{2,1,0:T(8,128)(2,1)S(1)} %pad_maximum_fusion.2), channel_id=1, source_target_pairs={{0,16},{16,32},{32,48},{48,64},{64,80},{80,96},{96,112},{112,0},{1... | collective-permute-start | bytes 1179656 | tf_op jit(solution)/shard_map/ppermute | solution.py:77
  18.1 4.0 %collective-permute-start.2 = (bf16[2,128,768]{2,1,0:T(8,128)(2,1)S(1)}, bf16[2,128,768]{2,1,0:T(8,128)(2,1)S(1)}, u32[]{:S(2)}, u32[]{:S(2)}) collective-permute-start(bf16[2,128,768]{2,1,0:T(8,128)(2,1)S(1)} %pad_maximum_fusion.2), channel_id=1, source_target_pairs={{0,112},{16,0},{32,16},{48,32},{64,48},{80,64},{96,80},{112,96},{1... | collective-permute-start | bytes 1179656 | tf_op jit(solution)/shard_map/ppermute | solution.py:80
  22.2 2.0 %broadcast_in_dim.85 = bf16[8,2,128,768]{3,2,0,1:T(8,128)(2,1)} broadcast(bf16[]{:T(256)} %constant.119.clone.1), dimensions={} | broadcast | bytes 3145730 | tf_op jit(solution)/shard_map/broadcast_in_dim | solution.py:72
  24.2 0.8 bitcast_dynamic-update-slice_fusion.6
  25.0 5.1 %collective-permute-done.1 = bf16[2,128,768]{2,1,0:T(8,128)(2,1)S(1)} collective-permute-done((bf16[2,128,768]{2,1,0:T(8,128)(2,1)S(1)}, bf16[2,128,768]{2,1,0:T(8,128)(2,1)S(1)}, u32[]{:S(2)}, u32[]{:S(2)}) %collective-permute-start.1) | collective-permute-done | bytes 393248 | tf_op jit(solution)/shard_map/ppermute | solution.py:77
  30.1 2.7 %collective-permute-start.4 = (bf16[2,128,768]{2,1,0:T(8,128)(2,1)S(1)}, bf16[2,128,768]{2,1,0:T(8,128)(2,1)S(1)}, u32[]{:S(2)}, u32[]{:S(2)}) collective-permute-start(bf16[2,128,768]{2,1,0:T(8,128)(2,1)S(1)} %collective-permute-done.2), channel_id=1, source_target_pairs={{0,112},{16,0},{32,16},{48,32},{64,48},{80,64},{96,80},{112,96},{1... | collective-permute-start | bytes 1179656 | tf_op jit(solution)/shard_map/ppermute | solution.py:80
  32.7 0.8 bitcast_dynamic-update-slice_fusion.5
  33.5 0.8 bitcast_dynamic-update-slice_fusion.4
  34.3 5.5 %collective-permute-done.3 = bf16[2,128,768]{2,1,0:T(8,128)(2,1)S(1)} collective-permute-done((bf16[2,128,768]{2,1,0:T(8,128)(2,1)S(1)}, bf16[2,128,768]{2,1,0:T(8,128)(2,1)S(1)}, u32[]{:S(2)}, u32[]{:S(2)}) %collective-permute-start.3) | collective-permute-done | bytes 393248 | tf_op jit(solution)/shard_map/ppermute | solution.py:77
  39.8 2.7 %collective-permute-start.6 = (bf16[2,128,768]{2,1,0:T(8,128)(2,1)S(1)}, bf16[2,128,768]{2,1,0:T(8,128)(2,1)S(1)}, u32[]{:S(2)}, u32[]{:S(2)}) collective-permute-start(bf16[2,128,768]{2,1,0:T(8,128)(2,1)S(1)} %collective-permute-done.4), channel_id=1, source_target_pairs={{0,112},{16,0},{32,16},{48,32},{64,48},{80,64},{96,80},{112,96},{1... | collective-permute-start | bytes 1179656 | tf_op jit(solution)/shard_map/ppermute | solution.py:80
  42.5 0.8 bitcast_dynamic-update-slice_fusion.3
  43.3 0.8 bitcast_dynamic-update-slice_fusion.2
  44.1 4.7 %collective-permute-done.5 = bf16[2,128,768]{2,1,0:T(8,128)(2,1)S(1)} collective-permute-done((bf16[2,128,768]{2,1,0:T(8,128)(2,1)S(1)}, bf16[2,128,768]{2,1,0:T(8,128)(2,1)S(1)}, u32[]{:S(2)}, u32[]{:S(2)}) %collective-permute-start.5) | collective-permute-done | bytes 393248 | tf_op jit(solution)/shard_map/ppermute | solution.py:77
  48.8 0.8 bitcast_dynamic-update-slice_fusion.1
  49.6 0.8 bitcast_dynamic-update-slice_fusion
  50.3 6.3 %collective-permute-done.7 = bf16[2,128,768]{2,1,0:T(8,128)(2,1)S(1)} collective-permute-done((bf16[2,128,768]{2,1,0:T(8,128)(2,1)S(1)}, bf16[2,128,768]{2,1,0:T(8,128)(2,1)S(1)}, u32[]{:S(2)}, u32[]{:S(2)}) %collective-permute-start.7) | collective-permute-done | bytes 393248 | tf_op jit(solution)/shard_map/ppermute | solution.py:77
  56.6 0.8 bitcast_dynamic-update-slice_fusion.7
  57.4 5.0 %collective-permute-start.8 = (bf16[8,2,128,768]{3,2,0,1:T(8,128)(2,1)}, bf16[8,2,128,768]{3,2,0,1:T(8,128)(2,1)}, u32[]{:S(2)}, u32[]{:S(2)}) collective-permute-start(bf16[8,2,128,768]{3,2,0,1:T(8,128)(2,1)} %bitcast_dynamic-update-slice_fusion.7), channel_id=1, source_target_pairs={{0,8},{8,0},{1,9},{9,1},{2,10},{10,2},{3,11},{11,3},{4,12},{12,4},... | collective-permute-start | bytes 9437192 | tf_op jit(solution)/shard_map/ppermute | solution.py:82
  63.1 0.3 pad_add_fusion
  63.4 2.2 %broadcast_in_dim.83 = pred[4,384,1536]{1,0,2:T(4,128)(4,1)S(1)} broadcast(pred[384,1536]{0,1:T(8,128)(4,1)S(1)} %pad_add_fusion), dimensions={1,2} | broadcast | bytes 2949120 | tf_op jit(solution)/shard_map/while/body/eval_jaxpr/jit(_where)/broadcast_in_dim | solution.py:39
  65.6 2.6 %copy.69 = pred[192,8,4,384]{3,1,2,0:T(8,128)(4,1)} copy(pred[192,8,4,384]{3,2,1,0:T(4,128)(4,1)S(1)} %bitcast.111) | data formatting | bytes 4718592
  68.5 0.2 copy.62
  68.7 3.4 %copy.65 = bf16[384,4096]{0,1:T(8,128)(2,1)S(1)} copy(bf16[384,4096]{1,0:T(8,128)(2,1)} %param.8) | data formatting | bytes 6291456 | tf_op args[0]
  72.1 1.5 dynamic-slice_bitcast_fusion.1
  73.6 1.3 copy.67
  75.0 3.3 %select_bitcast_fusion.1 = (bf16[8,2,1,128,768]{4,3,2,0,1:T(8,128)(2,1)S(1)}, bf16[8,2,1,128,768]{4,3,2,0,1:T(8,128)(2,1)S(1)}) fusion(bf16[8,2,128,768]{3,2,0,1:T(8,128)(2,1)} %bitcast_dynamic-update-slice_fusion.7, bf16[8,2,128,768]{3,2,0,1:T(8,128)(2,1)} %collective-permute-done.8, pred[]{:T(512)S(6)} %eq.16), kind=kLoop, calls=%fused_computation.17 | loop fusion | flops 3145728 | bytes 12582913 | tf_op jit(solution)/shard_map/stack | solution.py:85
  78.3 0.6 pad_maximum_fusion
  78.9 2.1 %copy-done.2 = bf16[384,4096]{1,0:T(8,128)(2,1)S(1)} copy-done((bf16[384,4096]{1,0:T(8,128)(2,1)S(1)}, bf16[384,4096]{1,0:T(8,128)(2,1)}, u32[]{:S(2)}) %copy-start.2) | copy-done | bytes 3145752
  81.0 3.4 %fusion.5 = bf16[384,768]{0,1:T(8,128)(2,1)S(1)} fusion(bf16[4096,768]{1,0:T(8,128)(2,1)S(1)} %bitcast.112, bf16[384,4096]{1,0:T(8,128)(2,1)S(1)} %copy-done.2), kind=kOutput, calls=%fused_computation.24 | convolution fusion | flops 2416214016 | bytes 10027008 | tf_op jit(solution)/shard_map/dot_general | solution.py:98
  84.5 0.7 fusion.23
  85.2 0.2 copy.57
  85.4 1.1 copy.58
  86.5 1.7 copy.59
  88.2 2.7 %fusion.25 = (f32[1536]{0:T(1024)S(1)}, f32[1536,1536]{0,1:T(8,128)S(1)}) fusion(pred[1536,1536]{0,1:T(8,128)(4,1)S(1)} %bitcast.115, bf16[1536,128]{1,0:T(8,128)(2,1)S(1)} %bitcast.127, bf16[384,128]{1,0:T(8,128)(2,1)S(1)} %copy.58, bf16[1152,128]{1,0:T(8,128)(2,1)} %bitcast.133), kind=kOutput, calls=%fused_computation.62 | convolution fusion | flops 611842560 | bytes 12589056 | tf_op jit(solution)/shard_map/while/body/eval_jaxpr/dot_general | solution.py:14
  91.0 1.3 fusion.4
  92.3 4.7 %fusion.1 = (f32[1536]{0:T(1024)S(1)}, bf16[1536,1536]{0,1:T(8,128)(2,1)}, f32[1536,1536]{1,0:T(8,128)S(1)}) fusion(f32[1536]{0:T(1024)S(1)} %fusion.4, f32[1536,1536]{0,1:T(8,128)S(1)} %get-tuple-element.54, f32[1536]{0:T(1024)S(1)} %get-tuple-element.53, bf16[1536,128]{1,0:T(8,128)(2,1)S(1)} %bitcast.121, bf16[384,128]{1,0:T(8,128)(2,1)S(1)} %copy-done.9, ...), kind=kOutput, calls=%fused_computation.4 | convolution fusion | flops 618920448 | bytes 24397824 | tf_op jit(solution)/shard_map/while/body/eval_jaxpr/dot_general | solution.py:14
  97.0 6.5 %fusion.3 = bf16[1536,1536]{0,1:T(8,128)(2,1)} fusion(bf16[1536,1536]{0,1:T(8,128)(2,1)} %get-tuple-element.30, f32[1536,1536]{1,0:T(8,128)S(1)} %get-tuple-element.55, f32[1536]{0:T(1024)S(1)} %get-tuple-element.29), kind=kLoop, calls=%fused_computation.6 | loop fusion | flops 11796480 | bytes 18880512 | tf_op jit(solution)/shard_map/while/body/eval_jaxpr/convert_element_type | solution.py:48
  103.5 3.9 %convolution_convert_fusion.2 = bf16[1536,128]{1,0:T(8,128)(2,1)S(1)} fusion(bf16[1536,1536]{0,1:T(8,128)(2,1)} %fusion.3, bf16[384,128]{1,0:T(8,128)(2,1)} %copy-done.11, bf16[1152,128]{1,0:T(8,128)(2,1)} %bitcast.134), kind=kOutput, calls=%fused_computation.18 | convolution fusion | flops 604962816 | bytes 5505024 | tf_op jit(solution)/shard_map/while/body/eval_jaxpr/dot_general | solution.py:49
  107.4 1.9 %fusion.10 = bf16[384,128]{0,1:T(8,128)(2,1)S(1)} fusion(bf16[1536,128]{1,0:T(8,128)(2,1)S(1)} %bitcast.128, bf16[1536,1536]{0,1:T(8,128)(2,1)} %fusion.3), kind=kOutput, calls=%fused_computation.29 | convolution fusion | flops 151044096 | bytes 1671168 | tf_op jit(solution)/shard_map/while/body/eval_jaxpr/dot_general | solution.py:20
  109.3 1.8 fusion.13
  111.0 0.2 copy.63
  111.3 1.8 convolution_convert_fusion.1
  113.1 0.4 collective-permute-start.9
  113.7 5.5 %collective-permute-done.9 = bf16[2048,768]{1,0:T(8,128)(2,1)S(1)} collective-permute-done((bf16[2048,768]{1,0:T(8,128)(2,1)S(1)}, bf16[2048,768]{1,0:T(8,128)(2,1)S(1)}, u32[]{:S(2)}, u32[]{:S(2)}) %collective-permute-start.9) | collective-permute-done | bytes 3145760 | tf_op jit(solution)/shard_map/ppermute | solution.py:127
  119.1 3.6 %add_convert_fusion = bf16[2048,768]{1,0:T(8,128)(2,1)} fusion(bf16[2048,768]{1,0:T(8,128)(2,1)S(1)} %collective-permute-done.9, bf16[384,2048]{0,1:T(8,128)(2,1)S(1)} %bitcast.117, bf16[384,128]{0,1:T(8,128)(2,1)S(1)} %fusion.13, bf16[384,128]{0,1:T(8,128)(2,1)S(1)} %fusion.10, bf16[384,512]{0,1:T(8,128)(2,1)S(1)} %bitcast.125), kind=kOutput, calls=%fused_computation.12 | convolution fusion | flops 1214447616 | bytes 8454144 | tf_op jit(solution)/shard_map/dot_general | solution.py:20
  122.7 5.4 %convolution_convert_fusion = bf16[384,4096]{1,0:T(8,128)(2,1)S(1)} fusion(bf16[4096,768]{1,0:T(8,128)(2,1)} %bitcast.113, bf16[384,128]{0,1:T(8,128)(2,1)S(1)} %fusion.13, bf16[384,128]{0,1:T(8,128)(2,1)S(1)} %fusion.10, bf16[384,512]{0,1:T(8,128)(2,1)S(1)} %bitcast.126), kind=kOutput, calls=%fused_computation.13 | convolution fusion | flops 2419261440 | bytes 10027008 | tf_op jit(solution)/shard_map/dot_general | solution.py:14
  128.2 1.9 %copy.73 = bf16[48,8,8,512]{3,2,0,1:T(8,128)(2,1)} copy(bf16[48,8,8,512]{3,2,1,0:T(8,128)(2,1)S(1)} %bitcast.114) | data formatting | bytes 6291456 | tf_op jit(solution)/shard_map/reshape | solution.py:136
  130.1 6.8 %all-to-all-start = ((bf16[8,384,512]{2,1,0:T(8,128)(2,1)}), bf16[8,384,512]{2,1,0:T(8,128)(2,1)S(1)}, u32[]{:S(2)}, u32[]{:S(2)}) async-start(bf16[8,384,512]{2,1,0:T(8,128)(2,1)} %bitcast.107), calls=%async_computation | async-start | bytes 6291456 | tf_op jit(solution)/shard_map/all_to_all | solution.py:137
  136.9 28.9 %reduce-scatter.2.cloned.1.call-done = bf16[256,768]{1,0:T(8,128)(2,1)} async-done(((bf16[2048,768]{1,0:T(8,128)(2,1)}), bf16[256,768]{1,0:T(8,128)(2,1)}) %reduce-scatter.2.cloned.1.call-update) | async-done | bytes 393232 | tf_op jit(solution)/shard_map/reduce_scatter | solution.py:130
  165.8 1.6 dynamic-slice_bitcast_fusion.2
  167.4 1.3 collective-permute-start.10
  168.7 3.8 %convolution_convert_fusion.3 = bf16[1536,128]{1,0:T(8,128)(2,1)S(1)} fusion(bf16[1536,1536]{0,1:T(8,128)(2,1)} %get-tuple-element.30, bf16[384,128]{1,0:T(8,128)(2,1)S(1)} %copy-done.10, bf16[1152,128]{1,0:T(8,128)(2,1)S(1)} %bitcast.136), kind=kOutput, calls=%fused_computation.19 | convolution fusion | flops 604962816 | bytes 5505024 | tf_op jit(solution)/shard_map/while/body/eval_jaxpr/dot_general | solution.py:44
  172.4 0.3 copy.60
  172.7 0.8 copy.74
  173.5 2.7 %all-to-all-done = bf16[8,384,512]{2,1,0:T(8,128)(2,1)S(1)} async-done(((bf16[8,384,512]{2,1,0:T(8,128)(2,1)}), bf16[8,384,512]{2,1,0:T(8,128)(2,1)S(1)}, u32[]{:S(2)}, u32[]{:S(2)}) %all-to-all-start) | async-done | bytes 3145760 | tf_op jit(solution)/shard_map/all_to_all | solution.py:137
  176.3 1.3 reduce_sum.34
  177.6 1.0 fusion.16
  178.5 0.7 slice.42
  179.3 0.7 fusion.24
  (45 shorter events, 0.7 us)
Async XLA Ops:
  7.2 158.6 %reduce-scatter.2.cloned.1.call-start = ((), (), s32[]{:S(2)}) async-start(), calls=%async_computation.2 | async-start | bytes 3538944 | tf_op jit(solution)/shard_map/reduce_scatter | solution.py:130
  9.7 5.5 %collective-permute-start = (bf16[128,768]{1,0:T(8,128)(2,1)S(1)}, bf16[128,768]{1,0:T(8,128)(2,1)S(1)}, u32[]{:S(2)}, u32[]{:S(2)}) collective-permute-start(bf16[128,768]{1,0:T(8,128)(2,1)S(1)} %constant_dynamic-update-slice_fusion), channel_id=1, source_target_pairs={{0,128},{128,0},{1,129},{129,1},{2,130},{130,2},{3,131},{131,3},{4... | collective-permute-start | bytes 589832 | tf_op jit(solution)/shard_map/ppermute | solution.py:68
  15.2 14.8 %collective-permute-start.1 = (bf16[2,128,768]{2,1,0:T(8,128)(2,1)S(1)}, bf16[2,128,768]{2,1,0:T(8,128)(2,1)S(1)}, u32[]{:S(2)}, u32[]{:S(2)}) collective-permute-start(bf16[2,128,768]{2,1,0:T(8,128)(2,1)S(1)} %pad_maximum_fusion.2), channel_id=1, source_target_pairs={{0,16},{16,32},{32,48},{48,64},{64,80},{80,96},{96,112},{112,0},{1... | collective-permute-start | bytes 1179656 | tf_op jit(solution)/shard_map/ppermute | solution.py:77
  18.1 11.9 %collective-permute-start.2 = (bf16[2,128,768]{2,1,0:T(8,128)(2,1)S(1)}, bf16[2,128,768]{2,1,0:T(8,128)(2,1)S(1)}, u32[]{:S(2)}, u32[]{:S(2)}) collective-permute-start(bf16[2,128,768]{2,1,0:T(8,128)(2,1)S(1)} %pad_maximum_fusion.2), channel_id=1, source_target_pairs={{0,112},{16,0},{32,16},{48,32},{64,48},{80,64},{96,80},{112,96},{1... | collective-permute-start | bytes 1179656 | tf_op jit(solution)/shard_map/ppermute | solution.py:80
  30.1 9.8 %collective-permute-start.3 = (bf16[2,128,768]{2,1,0:T(8,128)(2,1)S(1)}, bf16[2,128,768]{2,1,0:T(8,128)(2,1)S(1)}, u32[]{:S(2)}, u32[]{:S(2)}) collective-permute-start(bf16[2,128,768]{2,1,0:T(8,128)(2,1)S(1)} %collective-permute-done.1), channel_id=1, source_target_pairs={{0,16},{16,32},{32,48},{48,64},{64,80},{80,96},{96,112},{112,0},{1... | collective-permute-start | bytes 1179656 | tf_op jit(solution)/shard_map/ppermute | solution.py:77
  30.1 9.8 %collective-permute-start.4 = (bf16[2,128,768]{2,1,0:T(8,128)(2,1)S(1)}, bf16[2,128,768]{2,1,0:T(8,128)(2,1)S(1)}, u32[]{:S(2)}, u32[]{:S(2)}) collective-permute-start(bf16[2,128,768]{2,1,0:T(8,128)(2,1)S(1)} %collective-permute-done.2), channel_id=1, source_target_pairs={{0,112},{16,0},{32,16},{48,32},{64,48},{80,64},{96,80},{112,96},{1... | collective-permute-start | bytes 1179656 | tf_op jit(solution)/shard_map/ppermute | solution.py:80
  39.8 8.9 %collective-permute-start.5 = (bf16[2,128,768]{2,1,0:T(8,128)(2,1)S(1)}, bf16[2,128,768]{2,1,0:T(8,128)(2,1)S(1)}, u32[]{:S(2)}, u32[]{:S(2)}) collective-permute-start(bf16[2,128,768]{2,1,0:T(8,128)(2,1)S(1)} %collective-permute-done.3), channel_id=1, source_target_pairs={{0,16},{16,32},{32,48},{48,64},{64,80},{80,96},{96,112},{112,0},{1... | collective-permute-start | bytes 1179656 | tf_op jit(solution)/shard_map/ppermute | solution.py:77
  39.8 9.7 %collective-permute-start.6 = (bf16[2,128,768]{2,1,0:T(8,128)(2,1)S(1)}, bf16[2,128,768]{2,1,0:T(8,128)(2,1)S(1)}, u32[]{:S(2)}, u32[]{:S(2)}) collective-permute-start(bf16[2,128,768]{2,1,0:T(8,128)(2,1)S(1)} %collective-permute-done.4), channel_id=1, source_target_pairs={{0,112},{16,0},{32,16},{48,32},{64,48},{80,64},{96,80},{112,96},{1... | collective-permute-start | bytes 1179656 | tf_op jit(solution)/shard_map/ppermute | solution.py:80
  48.8 7.8 %collective-permute-start.7 = (bf16[2,128,768]{2,1,0:T(8,128)(2,1)S(1)}, bf16[2,128,768]{2,1,0:T(8,128)(2,1)S(1)}, u32[]{:S(2)}, u32[]{:S(2)}) collective-permute-start(bf16[2,128,768]{2,1,0:T(8,128)(2,1)S(1)} %collective-permute-done.5), channel_id=1, source_target_pairs={{0,16},{16,32},{32,48},{48,64},{64,80},{80,96},{96,112},{112,0},{1... | collective-permute-start | bytes 1179656 | tf_op jit(solution)/shard_map/ppermute | solution.py:77
  57.4 17.6 %collective-permute-start.8 = (bf16[8,2,128,768]{3,2,0,1:T(8,128)(2,1)}, bf16[8,2,128,768]{3,2,0,1:T(8,128)(2,1)}, u32[]{:S(2)}, u32[]{:S(2)}) collective-permute-start(bf16[8,2,128,768]{3,2,0,1:T(8,128)(2,1)} %bitcast_dynamic-update-slice_fusion.7), channel_id=1, source_target_pairs={{0,8},{8,0},{1,9},{9,1},{2,10},{10,2},{3,11},{11,3},{4,12},{12,4},... | collective-permute-start | bytes 9437192 | tf_op jit(solution)/shard_map/ppermute | solution.py:82
  63.4 4.9 %copy-start.5 = (bf16[384,512]{1,0:T(8,128)(2,1)S(1)}, bf16[384,512]{1,0:T(8,128)(2,1)}, u32[]{:S(2)}) copy-start(bf16[384,512]{1,0:T(8,128)(2,1)} %param.15) | copy-start | bytes 1179652
  78.2 2.7 %copy-start.2 = (bf16[384,4096]{1,0:T(8,128)(2,1)S(1)}, bf16[384,4096]{1,0:T(8,128)(2,1)}, u32[]{:S(2)}) copy-start(bf16[384,4096]{1,0:T(8,128)(2,1)} %param.8) | copy-start | bytes 9437188
  78.8 5.6 %copy-start = (bf16[8,2,2,128,768]{4,3,2,0,1:T(8,128)(2,1)}, bf16[8,2,2,128,768]{4,3,2,0,1:T(8,128)(2,1)S(1)}, u32[]{:S(2)}) copy-start(bf16[8,2,2,128,768]{4,3,2,0,1:T(8,128)(2,1)S(1)} %pad_maximum_fusion) | copy-start | bytes 18874372
  81.0 7.2 %copy-start.3 = (pred[192,8,4,384]{3,1,2,0:T(8,128)(4,1)S(1)}, pred[192,8,4,384]{3,1,2,0:T(8,128)(4,1)}, u32[]{:S(2)}) copy-start(pred[192,8,4,384]{3,1,2,0:T(8,128)(4,1)} %copy.69) | copy-start | bytes 7077892
  85.4 5.5 %copy-start.6 = (bf16[384,1,4,128]{3,0,2,1:T(8,128)(2,1)}, bf16[384,1,4,128]{3,0,2,1:T(8,128)(2,1)S(1)}, u32[]{:S(2)}) copy-start(bf16[384,1,4,128]{3,0,2,1:T(8,128)(2,1)S(1)} %copy.57) | copy-start | bytes 1179652
  86.5 4.4 %copy-start.11 = (bf16[384,128]{1,0:T(8,128)(2,1)}, bf16[384,128]{1,0:T(8,128)(2,1)S(1)}, u32[]{:S(2)}) copy-start(bf16[384,128]{1,0:T(8,128)(2,1)S(1)} %copy.58) | copy-start | bytes 294916
  90.9 1.3 copy-start.9
  90.9 1.3 copy-start.12
  103.5 3.9 %copy-start.7 = (bf16[384,1,4,128]{3,0,2,1:T(8,128)(2,1)S(1)}, bf16[384,1,4,128]{3,0,2,1:T(8,128)(2,1)}, u32[]{:S(2)}) copy-start(bf16[384,1,4,128]{3,0,2,1:T(8,128)(2,1)} %copy-done.6) | copy-start | bytes 1179652
  107.4 3.9 %copy-start.4 = (bf16[384,8,2,1,128]{0,4,2,1,3:T(8,128)(2,1)S(1)}, bf16[384,8,2,1,128]{0,4,2,1,3:T(8,128)(2,1)}, u32[]{:S(2)}) copy-start(bf16[384,8,2,1,128]{0,4,2,1,3:T(8,128)(2,1)} %copy.67) | copy-start | bytes 4718596
  111.3 2.2 %copy-start.1 = (bf16[384,8,2,1,128]{0,4,3,1,2:T(8,128)(2,1)S(1)}, bf16[384,8,2,1,128]{0,4,3,1,2:T(8,128)(2,1)}, u32[]{:S(2)}) copy-start(bf16[384,8,2,1,128]{0,4,3,1,2:T(8,128)(2,1)} %get-tuple-element.33) | copy-start | bytes 4718596
  113.1 6.0 %collective-permute-start.9 = (bf16[2048,768]{1,0:T(8,128)(2,1)S(1)}, bf16[2048,768]{1,0:T(8,128)(2,1)S(1)}, u32[]{:S(2)}, u32[]{:S(2)}) collective-permute-start(bf16[2048,768]{1,0:T(8,128)(2,1)S(1)} %convolution_convert_fusion.1), channel_id=1, source_target_pairs={{0,8},{8,0},{1,9},{9,1},{2,10},{10,2},{3,11},{11,3},{4,12},{12,4},... | collective-permute-start | bytes 9437192 | tf_op jit(solution)/shard_map/ppermute | solution.py:127
  130.1 38.5 %copy-start.10 = (bf16[384,128]{1,0:T(8,128)(2,1)S(1)}, bf16[384,128]{1,0:T(8,128)(2,1)}, u32[]{:S(2)}) copy-start(bf16[384,128]{1,0:T(8,128)(2,1)} %copy.59) | copy-start | bytes 294916
  130.1 38.5 %copy-start.13 = (bf16[1,1152,128]{2,1,0:T(8,128)(2,1)S(1)}, bf16[1,1152,128]{2,1,0:T(8,128)(2,1)}, u32[]{:S(2)}) copy-start(bf16[1,1152,128]{2,1,0:T(8,128)(2,1)} %param.14) | copy-start | bytes 884740
  130.1 46.1 %all-to-all-start = ((bf16[8,384,512]{2,1,0:T(8,128)(2,1)}), bf16[8,384,512]{2,1,0:T(8,128)(2,1)S(1)}, u32[]{:S(2)}, u32[]{:S(2)}) async-start(bf16[8,384,512]{2,1,0:T(8,128)(2,1)} %bitcast.107), calls=%async_computation | async-start | bytes 6291456 | tf_op jit(solution)/shard_map/all_to_all | solution.py:137
  167.4 10.2 %collective-permute-start.10 = (bf16[128,768]{1,0:T(8,128)(2,1)}, bf16[128,768]{1,0:T(8,128)(2,1)}, u32[]{:S(2)}, u32[]{:S(2)}) collective-permute-start(bf16[128,768]{1,0:T(8,128)(2,1)} %dynamic-slice_bitcast_fusion.2), channel_id=1, source_target_pairs={{0,128},{128,0},{1,129},{129,1},{2,130},{130,2},{3,131},{131,3},{4... | collective-permute-start | bytes 589832 | tf_op jit(solution)/shard_map/ppermute | solution.py:134
  172.4 5.1 %copy-start.8 = (bf16[256,768]{1,0:T(8,128)(2,1)S(1)}, bf16[256,768]{1,0:T(8,128)(2,1)}, u32[]{:S(2)}) copy-start(bf16[256,768]{1,0:T(8,128)(2,1)} %reduce-scatter.2.cloned.1.call-done) | copy-start | bytes 1179652
Sparse Core Ops, SparseCore 0:
  122.8 42.8 reduce-scatter.1

commit v7 on v6

--- a/solution.py
+++ b/solution.py
@@ -71,14 +71,17 @@
     behind = [(i, (i - 1) % z_count) for i in range(z_count)]
     ring = jnp.zeros((z_count,) + pair.shape, pair.dtype)
     ring = lax.dynamic_update_index_in_dim(ring, pair, z_pos, 0)
-    fwd = pair
-    bwd = pair
-    for step in range(1, z_count // 2 + 1):
+    half = z_count // 2
+
+    def ring_step(step, carry):
+        ring, fwd, bwd = carry
         fwd = lax.ppermute(fwd, "z", ahead)
+        bwd = lax.ppermute(bwd, "z", behind)
         ring = lax.dynamic_update_index_in_dim(ring, fwd, (z_pos - step) % z_count, 0)
-        if step < z_count - z_count // 2:
-            bwd = lax.ppermute(bwd, "z", behind)
-            ring = lax.dynamic_update_index_in_dim(ring, bwd, (z_pos + step) % z_count, 0)
+        ring = lax.dynamic_update_index_in_dim(ring, bwd, (z_pos + step) % z_count, 0)
+        return ring, fwd, bwd
+
+    ring, _, _ = lax.fori_loop(1, half + 1, ring_step, (ring, pair, pair))
     other = lax.ppermute(ring, "c", SWAP)
     first = jnp.where(chip_core == 0, ring, other)
     second = jnp.where(chip_core == 0, other, ring)

time: 188 us -> 200 us (1.064)
  local copies, waits for them, and re-layouts: 33.9 us -> 39.9 us
  waiting for transfers between devices: 62 us -> 67 us
  starting transfers between devices: 27.8 us -> 30.5 us
    ppermute x7 -> x8, waiting for transfers between devices: 21.6 us -> 26.5 us  [the longest x4 26.5 us: ring_step(): fwd = lax.ppermute(fwd, 'z', ahead)]
    while x0 -> x9, local copies, waits for them, and re-layouts: none -> 4.07 us  [the longest x1 3.86 us: gather_rows(): ring, _, _ = lax.fori_loop(1, half + 1, ring_step, (ring, pair, pair))]
    unnamed x34 -> x39, local copies, waits for them, and re-layouts: 11 us -> 13.7 us
    ppermute x7 -> x8, starting transfers between devices: 12.3 us -> 14.8 us  [the longest x4 10.5 us: ring_step(): bwd = lax.ppermute(bwd, 'z', behind)]
    dynamic_update_slice x7 -> x8, local copies, waits for them, and re-layouts: 5.49 us -> 6.38 us  [the longest x4 3.22 us: ring_step(): lax.dynamic_update_index_in_dim(ring, fwd, (z_pos - step) % z_count, 0)]
  transfers between devices with their start and end apart: 13 -> 14, of which waited for: 8 -> 8; matrix products, arithmetic and copies ran while one was open for 19% -> 14% of each run, Pallas kernels for 0% -> 0%
where the time goes in v7:
time: 200 us; the launch traced here: 199 us
  waiting for transfers between devices  67 us (34%)
  local copies, waits for them, and re-layouts  39.9 us (20%)
  matrix products  33 us (16%)
  starting transfers between devices  30.5 us (15%)
  between operations  15 us (8%)
  other arithmetic  13.4 us (7%)
    reduce_scatter x1, waiting for transfers between devices, local(): ring_sum = lax.psum_scatter(chip_sum, 'z', scatter_dimension=0, tiled=True)  29 us
    ppermute x4, waiting for transfers between devices, ring_step(): fwd = lax.ppermute(fwd, 'z', ahead)  26.5 us
    unnamed x39, local copies, waits for them, and re-layouts  13.7 us
    dot_general x3, matrix products, contract_last(): lax.dot_general(left, right, (((1,), (1,)), ((), ())), preferred_element_...  12.8 us
    ppermute x4, starting transfers between devices, ring_step(): bwd = lax.ppermute(bwd, 'z', behind)  10.5 us
    dot_general x4, matrix products, contract_first(): lax.dot_general(left, right, (((0,), (0,)), ((), ())), preferred_element_...  9.04 us
    all_to_all x1, starting transfers between devices, local(): gathered = lax.all_to_all(input_term, 'tp', 0, 0, tiled=True)  6.79 us
    convert_element_type x1, other arithmetic, head_pass(): (probs_wide * (grad_probs - row_dot) * factor).astype(jnp.bfloat16)  6.51 us
  transfers between devices with their start and end apart: 14, of which 8 were waited for; matrix products, arithmetic and copies ran while one was open for 14% of the time, Pallas kernels for 0%

profile of v7, /device:TPU:1, one launch (start us, length us, event | category | flops | bytes accessed | tf_op | source)
XLA Modules:
  0.0 199.0 jit_solution(9488286222408283125)
XLA Ops:
  7.2 0.9 constant_dynamic-update-slice_fusion.2
  8.1 0.8 constant_dynamic-update-slice_fusion.1
  8.9 0.8 constant_dynamic-update-slice_fusion
  9.7 2.1 %collective-permute-start.2 = (bf16[128,768]{1,0:T(8,128)(2,1)S(1)}, bf16[128,768]{1,0:T(8,128)(2,1)S(1)}, u32[]{:S(2)}, u32[]{:S(2)}) collective-permute-start(bf16[128,768]{1,0:T(8,128)(2,1)S(1)} %constant_dynamic-update-slice_fusion), channel_id=1, source_target_pairs={{0,128},{128,0},{1,129},{129,1},{2,130},{130,2},{3,131},{131,3},{4... | collective-permute-start | bytes 589832 | tf_op jit(solution)/shard_map/ppermute | solution.py:68
  11.8 3.4 %collective-permute-done.2 = bf16[128,768]{1,0:T(8,128)(2,1)S(1)} collective-permute-done((bf16[128,768]{1,0:T(8,128)(2,1)S(1)}, bf16[128,768]{1,0:T(8,128)(2,1)S(1)}, u32[]{:S(2)}, u32[]{:S(2)}) %collective-permute-start.2) | collective-permute-done | bytes 196640 | tf_op jit(solution)/shard_map/ppermute | solution.py:68
  15.6 1.7 copy-done
  17.3 48.0 %while.12 = (s32[]{:T(128)}, bf16[8,2,128,768]{3,2,1,0:T(8,128)(2,1)}, bf16[2,128,768]{2,1,0:T(8,128)(2,1)S(1)}, bf16[2,128,768]{2,1,0:T(8,128)(2,1)S(1)}, s32[]...) while((s32[]{:T(128)}, bf16[8,2,128,768]{3,2,1,0:T(8,128)(2,1)}, ...), condition=%wide.region_1.2_spmd, body=%wide.region_0.1_spmd.sunk | while | flops 32 | bytes 6291947 | solution.py:84
  17.3 2.9 %collective-permute-start = (bf16[2,128,768]{2,1,0:T(8,128)(2,1)S(1)}, bf16[2,128,768]{2,1,0:T(8,128)(2,1)S(1)}, u32[]{:S(2)}, u32[]{:S(2)}) collective-permute-start(bf16[2,128,768]{2,1,0:T(8,128)(2,1)S(1)} %get-tuple-element.242), channel_id=1, source_target_pairs={{0,16},{16,32},{32,48},{48,64},{64,80},{80,96},{96,112},{112,0},{1... | collective-permute-start | bytes 1179656 | tf_op jit(solution)/shard_map/while/body/eval_jaxpr/ppermute | solution.py:78
  20.2 3.9 %collective-permute-start.1 = (bf16[2,128,768]{2,1,0:T(8,128)(2,1)S(1)}, bf16[2,128,768]{2,1,0:T(8,128)(2,1)S(1)}, u32[]{:S(2)}, u32[]{:S(2)}) collective-permute-start(bf16[2,128,768]{2,1,0:T(8,128)(2,1)S(1)} %get-tuple-element.243), channel_id=1, source_target_pairs={{0,112},{16,0},{32,16},{48,32},{64,48},{80,64},{96,80},{112,96},{1... | collective-permute-start | bytes 1179656 | tf_op jit(solution)/shard_map/while/body/eval_jaxpr/ppermute | solution.py:79
  24.1 8.0 %collective-permute-done = bf16[2,128,768]{2,1,0:T(8,128)(2,1)S(1)} collective-permute-done((bf16[2,128,768]{2,1,0:T(8,128)(2,1)S(1)}, bf16[2,128,768]{2,1,0:T(8,128)(2,1)S(1)}, u32[]{:S(2)}, u32[]{:S(2)}) %collective-permute-start) | collective-permute-done | bytes 393248 | tf_op jit(solution)/shard_map/while/body/eval_jaxpr/ppermute | solution.py:78
  32.2 0.8 bitcast_dynamic-update-slice_fusion.5
  32.9 0.8 bitcast_dynamic-update-slice_fusion.6
  33.7 2.7 %collective-permute-start.1 = (bf16[2,128,768]{2,1,0:T(8,128)(2,1)S(1)}, bf16[2,128,768]{2,1,0:T(8,128)(2,1)S(1)}, u32[]{:S(2)}, u32[]{:S(2)}) collective-permute-start(bf16[2,128,768]{2,1,0:T(8,128)(2,1)S(1)} %get-tuple-element.243), channel_id=1, source_target_pairs={{0,112},{16,0},{32,16},{48,32},{64,48},{80,64},{96,80},{112,96},{1... | collective-permute-start | bytes 1179656 | tf_op jit(solution)/shard_map/while/body/eval_jaxpr/ppermute | solution.py:79
  36.4 7.1 %collective-permute-done = bf16[2,128,768]{2,1,0:T(8,128)(2,1)S(1)} collective-permute-done((bf16[2,128,768]{2,1,0:T(8,128)(2,1)S(1)}, bf16[2,128,768]{2,1,0:T(8,128)(2,1)S(1)}, u32[]{:S(2)}, u32[]{:S(2)}) %collective-permute-start) | collective-permute-done | bytes 393248 | tf_op jit(solution)/shard_map/while/body/eval_jaxpr/ppermute | solution.py:78
  43.6 0.8 bitcast_dynamic-update-slice_fusion.5
  44.4 0.8 bitcast_dynamic-update-slice_fusion.6
  45.2 1.0 collective-permute-start
  46.2 1.7 collective-permute-start.1
  47.8 6.2 %collective-permute-done = bf16[2,128,768]{2,1,0:T(8,128)(2,1)S(1)} collective-permute-done((bf16[2,128,768]{2,1,0:T(8,128)(2,1)S(1)}, bf16[2,128,768]{2,1,0:T(8,128)(2,1)S(1)}, u32[]{:S(2)}, u32[]{:S(2)}) %collective-permute-start) | collective-permute-done | bytes 393248 | tf_op jit(solution)/shard_map/while/body/eval_jaxpr/ppermute | solution.py:78
  54.2 0.8 bitcast_dynamic-update-slice_fusion.5
  55.0 0.8 bitcast_dynamic-update-slice_fusion.6
  55.7 0.5 collective-permute-start
  56.3 2.1 %collective-permute-start.1 = (bf16[2,128,768]{2,1,0:T(8,128)(2,1)S(1)}, bf16[2,128,768]{2,1,0:T(8,128)(2,1)S(1)}, u32[]{:S(2)}, u32[]{:S(2)}) collective-permute-start(bf16[2,128,768]{2,1,0:T(8,128)(2,1)S(1)} %get-tuple-element.243), channel_id=1, source_target_pairs={{0,112},{16,0},{32,16},{48,32},{64,48},{80,64},{96,80},{112,96},{1... | collective-permute-start | bytes 1179656 | tf_op jit(solution)/shard_map/while/body/eval_jaxpr/ppermute | solution.py:79
  58.4 5.2 %collective-permute-done = bf16[2,128,768]{2,1,0:T(8,128)(2,1)S(1)} collective-permute-done((bf16[2,128,768]{2,1,0:T(8,128)(2,1)S(1)}, bf16[2,128,768]{2,1,0:T(8,128)(2,1)S(1)}, u32[]{:S(2)}, u32[]{:S(2)}) %collective-permute-start) | collective-permute-done | bytes 393248 | tf_op jit(solution)/shard_map/while/body/eval_jaxpr/ppermute | solution.py:78
  63.7 0.8 bitcast_dynamic-update-slice_fusion.5
  64.5 0.8 bitcast_dynamic-update-slice_fusion.6
  65.3 3.9 %copy.42 = bf16[8,2,128,768]{3,2,0,1:T(8,128)(2,1)} copy(bf16[8,2,128,768]{3,2,1,0:T(8,128)(2,1)} %get-tuple-element.174) | data formatting | bytes 6291456 | tf_op jit(solution)/shard_map/while | solution.py:84
  69.2 5.3 %collective-permute-start.3 = (bf16[8,2,128,768]{3,2,0,1:T(8,128)(2,1)}, bf16[8,2,128,768]{3,2,0,1:T(8,128)(2,1)}, u32[]{:S(2)}, u32[]{:S(2)}) collective-permute-start(bf16[8,2,128,768]{3,2,0,1:T(8,128)(2,1)} %copy.42), channel_id=1, source_target_pairs={{0,8},{8,0},{1,9},{9,1},{2,10},{10,2},{3,11},{11,3},{4,12},{12,4},... | collective-permute-start | bytes 9437192 | tf_op jit(solution)/shard_map/ppermute | solution.py:85
  75.5 2.2 %broadcast_in_dim.82 = pred[4,384,1536]{1,0,2:T(4,128)(4,1)S(1)} broadcast(pred[384,1536]{0,1:T(8,128)(4,1)S(1)} %pad_add_fusion), dimensions={1,2} | broadcast | bytes 2949120 | tf_op jit(solution)/shard_map/while/body/eval_jaxpr/jit(_where)/broadcast_in_dim | solution.py:39
  77.8 2.6 %copy.57 = pred[192,8,4,384]{3,1,2,0:T(8,128)(4,1)} copy(pred[192,8,4,384]{3,2,1,0:T(4,128)(4,1)S(1)} %bitcast.91) | data formatting | bytes 4718592
  80.8 3.4 %copy.53 = bf16[384,4096]{0,1:T(8,128)(2,1)S(1)} copy(bf16[384,4096]{1,0:T(8,128)(2,1)} %param.10) | data formatting | bytes 6291456 | tf_op args[0]
  84.2 1.5 dynamic-slice_bitcast_fusion.1
  85.7 1.3 copy.55
  87.1 1.1 copy-done.1
  88.2 2.3 %select_bitcast_fusion.1 = (bf16[8,2,1,128,768]{4,3,2,0,1:T(8,128)(2,1)S(1)}, bf16[8,2,1,128,768]{4,3,2,0,1:T(8,128)(2,1)S(1)}) fusion(bf16[8,2,128,768]{3,2,0,1:T(8,128)(2,1)} %collective-permute-done.3, pred[]{:T(512)S(6)} %eq.17, bf16[8,2,128,768]{3,2,1,0:T(8,128)(2,1)S(1)} %copy-done.1), kind=kLoop, calls=%fused_computation.19 | loop fusion | flops 3145728 | bytes 12582913 | tf_op jit(solution)/shard_map/stack | solution.py:88
  90.5 0.6 pad_maximum_fusion
  91.1 2.1 %copy-done.4 = bf16[384,4096]{1,0:T(8,128)(2,1)S(1)} copy-done((bf16[384,4096]{1,0:T(8,128)(2,1)S(1)}, bf16[384,4096]{1,0:T(8,128)(2,1)}, u32[]{:S(2)}) %copy-start.4) | copy-done | bytes 3145752
  93.2 3.4 %fusion.5 = bf16[384,768]{0,1:T(8,128)(2,1)S(1)} fusion(bf16[4096,768]{1,0:T(8,128)(2,1)S(1)} %bitcast.92, bf16[384,4096]{1,0:T(8,128)(2,1)S(1)} %copy-done.4), kind=kOutput, calls=%fused_computation.26 | convolution fusion | flops 2416214016 | bytes 10027008 | tf_op jit(solution)/shard_map/dot_general | solution.py:101
  96.7 0.7 fusion.23
  97.6 1.1 copy.46
  98.8 1.7 copy.47
  100.4 2.7 %fusion.25 = (f32[1536]{0:T(1024)S(1)}, f32[1536,1536]{0,1:T(8,128)S(1)}) fusion(pred[1536,1536]{0,1:T(8,128)(4,1)S(1)} %bitcast.95, bf16[1536,128]{1,0:T(8,128)(2,1)S(1)} %bitcast.107, bf16[384,128]{1,0:T(8,128)(2,1)S(1)} %copy.46, bf16[1152,128]{1,0:T(8,128)(2,1)} %bitcast.113), kind=kOutput, calls=%fused_computation.57 | convolution fusion | flops 611842560 | bytes 12589056 | tf_op jit(solution)/shard_map/while/body/eval_jaxpr/dot_general | solution.py:14
  103.2 1.3 fusion.4
  104.5 4.7 %fusion.1 = (f32[1536]{0:T(1024)S(1)}, bf16[1536,1536]{0,1:T(8,128)(2,1)}, f32[1536,1536]{1,0:T(8,128)S(1)}) fusion(f32[1536]{0:T(1024)S(1)} %fusion.4, f32[1536,1536]{0,1:T(8,128)S(1)} %get-tuple-element.198, f32[1536]{0:T(1024)S(1)} %get-tuple-element.197, bf16[1536,128]{1,0:T(8,128)(2,1)S(1)} %bitcast.101, bf16[384,128]{1,0:T(8,128)(2,1)S(1)} %copy-done.11, ...), kind=kOutput, calls=%fused_computation.6 | convolution fusion | flops 618920448 | bytes 24397824 | tf_op jit(solution)/shard_map/while/body/eval_jaxpr/dot_general | solution.py:14
  109.2 6.5 %fusion.3 = bf16[1536,1536]{0,1:T(8,128)(2,1)} fusion(bf16[1536,1536]{0,1:T(8,128)(2,1)} %get-tuple-element.186, f32[1536,1536]{1,0:T(8,128)S(1)} %get-tuple-element.199, f32[1536]{0:T(1024)S(1)} %get-tuple-element.185), kind=kLoop, calls=%fused_computation.8 | loop fusion | flops 11796480 | bytes 18880512 | tf_op jit(solution)/shard_map/while/body/eval_jaxpr/convert_element_type | solution.py:48
  115.7 3.9 %convolution_convert_fusion.2 = bf16[1536,128]{1,0:T(8,128)(2,1)S(1)} fusion(bf16[1536,1536]{0,1:T(8,128)(2,1)} %fusion.3, bf16[384,128]{1,0:T(8,128)(2,1)} %copy-done.13, bf16[1152,128]{1,0:T(8,128)(2,1)} %bitcast.114), kind=kOutput, calls=%fused_computation.20 | convolution fusion | flops 604962816 | bytes 5505024 | tf_op jit(solution)/shard_map/while/body/eval_jaxpr/dot_general | solution.py:49
  119.6 1.9 fusion.10
  121.5 1.8 fusion.13
  123.5 1.8 convolution_convert_fusion.1
  125.9 5.5 %collective-permute-done.4 = bf16[2048,768]{1,0:T(8,128)(2,1)S(1)} collective-permute-done((bf16[2048,768]{1,0:T(8,128)(2,1)S(1)}, bf16[2048,768]{1,0:T(8,128)(2,1)S(1)}, u32[]{:S(2)}, u32[]{:S(2)}) %collective-permute-start.4) | collective-permute-done | bytes 3145760 | tf_op jit(solution)/shard_map/ppermute | solution.py:130
  131.4 3.6 %add_convert_fusion = bf16[2048,768]{1,0:T(8,128)(2,1)} fusion(bf16[2048,768]{1,0:T(8,128)(2,1)S(1)} %collective-permute-done.4, bf16[384,2048]{0,1:T(8,128)(2,1)S(1)} %bitcast.97, bf16[384,128]{0,1:T(8,128)(2,1)S(1)} %fusion.13, bf16[384,128]{0,1:T(8,128)(2,1)S(1)} %fusion.10, bf16[384,512]{0,1:T(8,128)(2,1)S(1)} %bitcast.105), kind=kOutput, calls=%fused_computation.14 | convolution fusion | flops 1214447616 | bytes 8454144 | tf_op jit(solution)/shard_map/dot_general | solution.py:20
  135.0 5.4 %convolution_convert_fusion = bf16[384,4096]{1,0:T(8,128)(2,1)S(1)} fusion(bf16[4096,768]{1,0:T(8,128)(2,1)} %bitcast.93, bf16[384,128]{0,1:T(8,128)(2,1)S(1)} %fusion.13, bf16[384,128]{0,1:T(8,128)(2,1)S(1)} %fusion.10, bf16[384,512]{0,1:T(8,128)(2,1)S(1)} %bitcast.106), kind=kOutput, calls=%fused_computation.15 | convolution fusion | flops 2419261440 | bytes 10027008 | tf_op jit(solution)/shard_map/dot_general | solution.py:14
  140.4 2.0 copy.63
  142.4 6.8 %all-to-all-start = ((bf16[8,384,512]{2,1,0:T(8,128)(2,1)}), bf16[8,384,512]{2,1,0:T(8,128)(2,1)S(1)}, u32[]{:S(2)}, u32[]{:S(2)}) async-start(bf16[8,384,512]{2,1,0:T(8,128)(2,1)} %bitcast.83), calls=%async_computation | async-start | bytes 6291456 | tf_op jit(solution)/shard_map/all_to_all | solution.py:140
  149.2 29.0 %reduce-scatter.2.cloned.1.call-done = bf16[256,768]{1,0:T(8,128)(2,1)} async-done(((bf16[2048,768]{1,0:T(8,128)(2,1)}), bf16[256,768]{1,0:T(8,128)(2,1)}) %reduce-scatter.2.cloned.1.call-update) | async-done | bytes 393232 | tf_op jit(solution)/shard_map/reduce_scatter | solution.py:133
  178.2 1.6 dynamic-slice_bitcast_fusion.2
  179.8 1.1 collective-permute-start.5
  180.9 3.8 %convolution_convert_fusion.3 = bf16[1536,128]{1,0:T(8,128)(2,1)S(1)} fusion(bf16[1536,1536]{0,1:T(8,128)(2,1)} %get-tuple-element.186, bf16[384,128]{1,0:T(8,128)(2,1)S(1)} %copy-done.12, bf16[1152,128]{1,0:T(8,128)(2,1)S(1)} %bitcast.116), kind=kOutput, calls=%fused_computation.21 | convolution fusion | flops 604962816 | bytes 5505024 | tf_op jit(solution)/shard_map/while/body/eval_jaxpr/dot_general | solution.py:44
  185.0 0.8 copy.64
  185.8 2.7 %all-to-all-done = bf16[8,384,512]{2,1,0:T(8,128)(2,1)S(1)} async-done(((bf16[8,384,512]{2,1,0:T(8,128)(2,1)}), bf16[8,384,512]{2,1,0:T(8,128)(2,1)S(1)}, u32[]{:S(2)}, u32[]{:S(2)}) %all-to-all-start) | async-done | bytes 3145760 | tf_op jit(solution)/shard_map/all_to_all | solution.py:140
  188.5 1.3 reduce_sum.34
  189.8 1.0 fusion.16
  190.8 0.7 slice.42
  191.5 0.7 fusion.24
  (63 shorter events, 2.9 us)
Async XLA Ops:
  7.2 171.0 %reduce-scatter.2.cloned.1.call-start = ((), (), s32[]{:S(2)}) async-start(), calls=%async_computation.2 | async-start | bytes 3538944 | tf_op jit(solution)/shard_map/reduce_scatter | solution.py:133
  9.7 5.5 %collective-permute-start.2 = (bf16[128,768]{1,0:T(8,128)(2,1)S(1)}, bf16[128,768]{1,0:T(8,128)(2,1)S(1)}, u32[]{:S(2)}, u32[]{:S(2)}) collective-permute-start(bf16[128,768]{1,0:T(8,128)(2,1)S(1)} %constant_dynamic-update-slice_fusion), channel_id=1, source_target_pairs={{0,128},{128,0},{1,129},{129,1},{2,130},{130,2},{3,131},{131,3},{4... | collective-permute-start | bytes 589832 | tf_op jit(solution)/shard_map/ppermute | solution.py:68
  15.6 1.7 copy-start
  17.3 14.8 %collective-permute-start = (bf16[2,128,768]{2,1,0:T(8,128)(2,1)S(1)}, bf16[2,128,768]{2,1,0:T(8,128)(2,1)S(1)}, u32[]{:S(2)}, u32[]{:S(2)}) collective-permute-start(bf16[2,128,768]{2,1,0:T(8,128)(2,1)S(1)} %get-tuple-element.242), channel_id=1, source_target_pairs={{0,16},{16,32},{32,48},{48,64},{64,80},{80,96},{96,112},{112,0},{1... | collective-permute-start | bytes 1179656 | tf_op jit(solution)/shard_map/while/body/eval_jaxpr/ppermute | solution.py:78
  20.2 11.9 %collective-permute-start.1 = (bf16[2,128,768]{2,1,0:T(8,128)(2,1)S(1)}, bf16[2,128,768]{2,1,0:T(8,128)(2,1)S(1)}, u32[]{:S(2)}, u32[]{:S(2)}) collective-permute-start(bf16[2,128,768]{2,1,0:T(8,128)(2,1)S(1)} %get-tuple-element.243), channel_id=1, source_target_pairs={{0,112},{16,0},{32,16},{48,32},{64,48},{80,64},{96,80},{112,96},{1... | collective-permute-start | bytes 1179656 | tf_op jit(solution)/shard_map/while/body/eval_jaxpr/ppermute | solution.py:79
  33.7 9.8 %collective-permute-start = (bf16[2,128,768]{2,1,0:T(8,128)(2,1)S(1)}, bf16[2,128,768]{2,1,0:T(8,128)(2,1)S(1)}, u32[]{:S(2)}, u32[]{:S(2)}) collective-permute-start(bf16[2,128,768]{2,1,0:T(8,128)(2,1)S(1)} %get-tuple-element.242), channel_id=1, source_target_pairs={{0,16},{16,32},{32,48},{48,64},{64,80},{80,96},{96,112},{112,0},{1... | collective-permute-start | bytes 1179656 | tf_op jit(solution)/shard_map/while/body/eval_jaxpr/ppermute | solution.py:78
  33.7 9.8 %collective-permute-start.1 = (bf16[2,128,768]{2,1,0:T(8,128)(2,1)S(1)}, bf16[2,128,768]{2,1,0:T(8,128)(2,1)S(1)}, u32[]{:S(2)}, u32[]{:S(2)}) collective-permute-start(bf16[2,128,768]{2,1,0:T(8,128)(2,1)S(1)} %get-tuple-element.243), channel_id=1, source_target_pairs={{0,112},{16,0},{32,16},{48,32},{64,48},{80,64},{96,80},{112,96},{1... | collective-permute-start | bytes 1179656 | tf_op jit(solution)/shard_map/while/body/eval_jaxpr/ppermute | solution.py:79
  45.2 8.9 %collective-permute-start = (bf16[2,128,768]{2,1,0:T(8,128)(2,1)S(1)}, bf16[2,128,768]{2,1,0:T(8,128)(2,1)S(1)}, u32[]{:S(2)}, u32[]{:S(2)}) collective-permute-start(bf16[2,128,768]{2,1,0:T(8,128)(2,1)S(1)} %get-tuple-element.242), channel_id=1, source_target_pairs={{0,16},{16,32},{32,48},{48,64},{64,80},{80,96},{96,112},{112,0},{1... | collective-permute-start | bytes 1179656 | tf_op jit(solution)/shard_map/while/body/eval_jaxpr/ppermute | solution.py:78
  46.2 8.0 %collective-permute-start.1 = (bf16[2,128,768]{2,1,0:T(8,128)(2,1)S(1)}, bf16[2,128,768]{2,1,0:T(8,128)(2,1)S(1)}, u32[]{:S(2)}, u32[]{:S(2)}) collective-permute-start(bf16[2,128,768]{2,1,0:T(8,128)(2,1)S(1)} %get-tuple-element.243), channel_id=1, source_target_pairs={{0,112},{16,0},{32,16},{48,32},{64,48},{80,64},{96,80},{112,96},{1... | collective-permute-start | bytes 1179656 | tf_op jit(solution)/shard_map/while/body/eval_jaxpr/ppermute | solution.py:79
  55.7 7.8 %collective-permute-start = (bf16[2,128,768]{2,1,0:T(8,128)(2,1)S(1)}, bf16[2,128,768]{2,1,0:T(8,128)(2,1)S(1)}, u32[]{:S(2)}, u32[]{:S(2)}) collective-permute-start(bf16[2,128,768]{2,1,0:T(8,128)(2,1)S(1)} %get-tuple-element.242), channel_id=1, source_target_pairs={{0,16},{16,32},{32,48},{48,64},{64,80},{80,96},{96,112},{112,0},{1... | collective-permute-start | bytes 1179656 | tf_op jit(solution)/shard_map/while/body/eval_jaxpr/ppermute | solution.py:78
  56.3 7.3 %collective-permute-start.1 = (bf16[2,128,768]{2,1,0:T(8,128)(2,1)S(1)}, bf16[2,128,768]{2,1,0:T(8,128)(2,1)S(1)}, u32[]{:S(2)}, u32[]{:S(2)}) collective-permute-start(bf16[2,128,768]{2,1,0:T(8,128)(2,1)S(1)} %get-tuple-element.243), channel_id=1, source_target_pairs={{0,112},{16,0},{32,16},{48,32},{64,48},{80,64},{96,80},{112,96},{1... | collective-permute-start | bytes 1179656 | tf_op jit(solution)/shard_map/while/body/eval_jaxpr/ppermute | solution.py:79
  69.2 17.9 %collective-permute-start.3 = (bf16[8,2,128,768]{3,2,0,1:T(8,128)(2,1)}, bf16[8,2,128,768]{3,2,0,1:T(8,128)(2,1)}, u32[]{:S(2)}, u32[]{:S(2)}) collective-permute-start(bf16[8,2,128,768]{3,2,0,1:T(8,128)(2,1)} %copy.42), channel_id=1, source_target_pairs={{0,8},{8,0},{1,9},{9,1},{2,10},{10,2},{3,11},{11,3},{4,12},{12,4},... | collective-permute-start | bytes 9437192 | tf_op jit(solution)/shard_map/ppermute | solution.py:85
  75.5 4.8 %copy-start.7 = (bf16[384,512]{1,0:T(8,128)(2,1)S(1)}, bf16[384,512]{1,0:T(8,128)(2,1)}, u32[]{:S(2)}) copy-start(bf16[384,512]{1,0:T(8,128)(2,1)} %param.17) | copy-start | bytes 1179652
  85.7 2.5 %copy-start.1 = (bf16[8,2,128,768]{3,2,1,0:T(8,128)(2,1)S(1)}, bf16[8,2,128,768]{3,2,1,0:T(8,128)(2,1)}, u32[]{:S(2)}) copy-start(bf16[8,2,128,768]{3,2,1,0:T(8,128)(2,1)} %get-tuple-element.174) | copy-start | bytes 9437188
  90.5 2.7 %copy-start.4 = (bf16[384,4096]{1,0:T(8,128)(2,1)S(1)}, bf16[384,4096]{1,0:T(8,128)(2,1)}, u32[]{:S(2)}) copy-start(bf16[384,4096]{1,0:T(8,128)(2,1)} %param.10) | copy-start | bytes 9437188
  91.1 5.6 %copy-start.2 = (bf16[8,2,2,128,768]{4,3,2,0,1:T(8,128)(2,1)}, bf16[8,2,2,128,768]{4,3,2,0,1:T(8,128)(2,1)S(1)}, u32[]{:S(2)}) copy-start(bf16[8,2,2,128,768]{4,3,2,0,1:T(8,128)(2,1)S(1)} %pad_maximum_fusion) | copy-start | bytes 18874372
  93.2 7.2 %copy-start.5 = (pred[192,8,4,384]{3,1,2,0:T(8,128)(4,1)S(1)}, pred[192,8,4,384]{3,1,2,0:T(8,128)(4,1)}, u32[]{:S(2)}) copy-start(pred[192,8,4,384]{3,1,2,0:T(8,128)(4,1)} %copy.57) | copy-start | bytes 7077892
  97.6 5.5 %copy-start.8 = (bf16[384,1,4,128]{3,0,2,1:T(8,128)(2,1)}, bf16[384,1,4,128]{3,0,2,1:T(8,128)(2,1)S(1)}, u32[]{:S(2)}) copy-start(bf16[384,1,4,128]{3,0,2,1:T(8,128)(2,1)S(1)} %copy.45) | copy-start | bytes 1179652
  98.8 4.4 %copy-start.13 = (bf16[384,128]{1,0:T(8,128)(2,1)}, bf16[384,128]{1,0:T(8,128)(2,1)S(1)}, u32[]{:S(2)}) copy-start(bf16[384,128]{1,0:T(8,128)(2,1)S(1)} %copy.46) | copy-start | bytes 294916
  103.2 1.3 copy-start.11
  103.2 1.3 copy-start.14
  115.7 3.9 %copy-start.9 = (bf16[384,1,4,128]{3,0,2,1:T(8,128)(2,1)S(1)}, bf16[384,1,4,128]{3,0,2,1:T(8,128)(2,1)}, u32[]{:S(2)}) copy-start(bf16[384,1,4,128]{3,0,2,1:T(8,128)(2,1)} %copy-done.8) | copy-start | bytes 1179652
  119.6 3.9 %copy-start.6 = (bf16[384,8,2,1,128]{0,4,2,1,3:T(8,128)(2,1)S(1)}, bf16[384,8,2,1,128]{0,4,2,1,3:T(8,128)(2,1)}, u32[]{:S(2)}) copy-start(bf16[384,8,2,1,128]{0,4,2,1,3:T(8,128)(2,1)} %copy.55) | copy-start | bytes 4718596
  123.5 2.2 %copy-start.3 = (bf16[384,8,2,1,128]{0,4,3,1,2:T(8,128)(2,1)S(1)}, bf16[384,8,2,1,128]{0,4,3,1,2:T(8,128)(2,1)}, u32[]{:S(2)}) copy-start(bf16[384,8,2,1,128]{0,4,3,1,2:T(8,128)(2,1)} %get-tuple-element.189) | copy-start | bytes 4718596
  125.3 6.0 %collective-permute-start.4 = (bf16[2048,768]{1,0:T(8,128)(2,1)S(1)}, bf16[2048,768]{1,0:T(8,128)(2,1)S(1)}, u32[]{:S(2)}, u32[]{:S(2)}) collective-permute-start(bf16[2048,768]{1,0:T(8,128)(2,1)S(1)} %convolution_convert_fusion.1), channel_id=1, source_target_pairs={{0,8},{8,0},{1,9},{9,1},{2,10},{10,2},{3,11},{11,3},{4,12},{12,4},... | collective-permute-start | bytes 9437192 | tf_op jit(solution)/shard_map/ppermute | solution.py:130
  142.4 38.5 %copy-start.12 = (bf16[384,128]{1,0:T(8,128)(2,1)S(1)}, bf16[384,128]{1,0:T(8,128)(2,1)}, u32[]{:S(2)}) copy-start(bf16[384,128]{1,0:T(8,128)(2,1)} %copy.47) | copy-start | bytes 294916
  142.4 38.5 %copy-start.15 = (bf16[1,1152,128]{2,1,0:T(8,128)(2,1)S(1)}, bf16[1,1152,128]{2,1,0:T(8,128)(2,1)}, u32[]{:S(2)}) copy-start(bf16[1,1152,128]{2,1,0:T(8,128)(2,1)} %param.16) | copy-start | bytes 884740
  142.4 46.1 %all-to-all-start = ((bf16[8,384,512]{2,1,0:T(8,128)(2,1)}), bf16[8,384,512]{2,1,0:T(8,128)(2,1)S(1)}, u32[]{:S(2)}, u32[]{:S(2)}) async-start(bf16[8,384,512]{2,1,0:T(8,128)(2,1)} %bitcast.83), calls=%async_computation | async-start | bytes 6291456 | tf_op jit(solution)/shard_map/all_to_all | solution.py:140
  179.8 10.0 %collective-permute-start.5 = (bf16[128,768]{1,0:T(8,128)(2,1)}, bf16[128,768]{1,0:T(8,128)(2,1)}, u32[]{:S(2)}, u32[]{:S(2)}) collective-permute-start(bf16[128,768]{1,0:T(8,128)(2,1)} %dynamic-slice_bitcast_fusion.2), channel_id=1, source_target_pairs={{0,128},{128,0},{1,129},{129,1},{2,130},{130,2},{3,131},{131,3},{4... | collective-permute-start | bytes 589832 | tf_op jit(solution)/shard_map/ppermute | solution.py:137
  184.7 5.2 %copy-start.10 = (bf16[256,768]{1,0:T(8,128)(2,1)S(1)}, bf16[256,768]{1,0:T(8,128)(2,1)}, u32[]{:S(2)}) copy-start(bf16[256,768]{1,0:T(8,128)(2,1)} %reduce-scatter.2.cloned.1.call-done) | copy-start | bytes 1179652
Sparse Core Ops, SparseCore 0:
  135.1 43.0 reduce-scatter.1

commit v8 on v6

--- a/solution.py
+++ b/solution.py
@@ -125,6 +125,7 @@
     cols_own = lax.dynamic_index_in_dim(by_place, chip_core, 3, False)
     part_other = contract_first(cols_other.reshape(tokens_dev, -1), grads_cat)
     from_peer = lax.ppermute(part_other.astype(jnp.bfloat16), "c", SWAP)
+    from_peer, attended = lax.optimization_barrier((from_peer, attended))
     part_own = contract_first(cols_own.reshape(tokens_dev, -1), grads_cat)
     chip_sum = (part_own + from_peer.astype(jnp.float32)).astype(jnp.bfloat16)
     ring_sum = lax.psum_scatter(chip_sum, "z", scatter_dimension=0, tiled=True)

time: 188 us -> 188 us (level)
  matrix products: 33 us -> 29.6 us
  other arithmetic: 15.2 us -> 17.5 us
    ppermute x1, waiting for transfers between devices: 5.46 us -> 0.45 us  [local(): from_peer = lax.ppermute(part_other.astype(jnp.bfloat16), 'c', SWAP)]
    all_to_all x1, waiting for transfers between devices: 2.71 us -> 7.28 us  [local(): gathered = lax.all_to_all(input_term, 'tp', 0, 0, tiled=True)]
    convert_element_type x0 -> x1, other arithmetic: none -> 2.43 us  [local(): chip_sum = (part_own + from_peer.astype(jnp.float32)).astype(jnp.bfloat16)]
    dot_general x1, matrix products: 3.76 us -> 1.44 us  [head_pass(): jnp.dot(probs, value_list, preferred_element_type=jnp.float32)]
    unnamed x34 -> x38, local copies, waits for them, and re-layouts: 11 us -> 11.6 us
  transfers between devices with their start and end apart: 13 -> 13, of which waited for: 8 -> 8; matrix products, arithmetic and copies ran while one was open for 19% -> 18% of each run, Pallas kernels for 0% -> 0%
where the time goes in v8:
time: 188 us; the launch traced here: 187 us
  waiting for transfers between devices  61.8 us (33%)
  local copies, waits for them, and re-layouts  35.5 us (19%)
  matrix products  29.6 us (16%)
  starting transfers between devices  27.7 us (15%)
  other arithmetic  17.5 us (9%)
  between operations  15 us (8%)
    reduce_scatter x1, waiting for transfers between devices, local(): ring_sum = lax.psum_scatter(chip_sum, 'z', scatter_dimension=0, tiled=True)  29.1 us
    ppermute x4, waiting for transfers between devices, gather_rows(): fwd = lax.ppermute(fwd, 'z', ahead)  21.6 us
    dot_general x3, matrix products, contract_last(): lax.dot_general(left, right, (((1,), (1,)), ((), ())), preferred_element_...  12.8 us
    unnamed x38, local copies, waits for them, and re-layouts  11.6 us
    ppermute x3, starting transfers between devices, gather_rows(): bwd = lax.ppermute(bwd, 'z', behind)  9.38 us
    dot_general x4, matrix products, contract_first(): lax.dot_general(left, right, (((0,), (0,)), ((), ())), preferred_element_...  7.28 us
    all_to_all x1, waiting for transfers between devices, local(): gathered = lax.all_to_all(input_term, 'tp', 0, 0, tiled=True)  7.28 us
    all_to_all x1, starting transfers between devices, local(): gathered = lax.all_to_all(input_term, 'tp', 0, 0, tiled=True)  6.65 us
  transfers between devices with their start and end apart: 13, of which 8 were waited for; matrix products, arithmetic and copies ran while one was open for 18% of the time, Pallas kernels for 0%

profile of v8, /device:TPU:1, one launch (start us, length us, event | category | flops | bytes accessed | tf_op | source)
XLA Modules:
  0.0 187.3 jit_solution(8426756512168919770)
XLA Ops:
  7.2 0.9 constant_dynamic-update-slice_fusion.2
  8.1 0.8 constant_dynamic-update-slice_fusion.1
  8.9 0.8 constant_dynamic-update-slice_fusion
  9.7 2.1 %collective-permute-start = (bf16[128,768]{1,0:T(8,128)(2,1)S(1)}, bf16[128,768]{1,0:T(8,128)(2,1)S(1)}, u32[]{:S(2)}, u32[]{:S(2)}) collective-permute-start(bf16[128,768]{1,0:T(8,128)(2,1)S(1)} %constant_dynamic-update-slice_fusion), channel_id=1, source_target_pairs={{0,128},{128,0},{1,129},{129,1},{2,130},{130,2},{3,131},{131,3},{4... | collective-permute-start | bytes 589832 | tf_op jit(solution)/shard_map/ppermute | solution.py:68
  11.8 3.4 %collective-permute-done = bf16[128,768]{1,0:T(8,128)(2,1)S(1)} collective-permute-done((bf16[128,768]{1,0:T(8,128)(2,1)S(1)}, bf16[128,768]{1,0:T(8,128)(2,1)S(1)}, u32[]{:S(2)}, u32[]{:S(2)}) %collective-permute-start) | collective-permute-done | bytes 196640 | tf_op jit(solution)/shard_map/ppermute | solution.py:68
  15.2 2.9 %collective-permute-start.1 = (bf16[2,128,768]{2,1,0:T(8,128)(2,1)S(1)}, bf16[2,128,768]{2,1,0:T(8,128)(2,1)S(1)}, u32[]{:S(2)}, u32[]{:S(2)}) collective-permute-start(bf16[2,128,768]{2,1,0:T(8,128)(2,1)S(1)} %pad_maximum_fusion.2), channel_id=1, source_target_pairs={{0,16},{16,32},{32,48},{48,64},{64,80},{80,96},{96,112},{112,0},{1... | collective-permute-start | bytes 1179656 | tf_op jit(solution)/shard_map/ppermute | solution.py:77
  18.1 4.0 %collective-permute-start.2 = (bf16[2,128,768]{2,1,0:T(8,128)(2,1)S(1)}, bf16[2,128,768]{2,1,0:T(8,128)(2,1)S(1)}, u32[]{:S(2)}, u32[]{:S(2)}) collective-permute-start(bf16[2,128,768]{2,1,0:T(8,128)(2,1)S(1)} %pad_maximum_fusion.2), channel_id=1, source_target_pairs={{0,112},{16,0},{32,16},{48,32},{64,48},{80,64},{96,80},{112,96},{1... | collective-permute-start | bytes 1179656 | tf_op jit(solution)/shard_map/ppermute | solution.py:80
  22.2 2.0 %broadcast_in_dim.85 = bf16[8,2,128,768]{3,2,0,1:T(8,128)(2,1)} broadcast(bf16[]{:T(256)} %constant.121.clone.1), dimensions={} | broadcast | bytes 3145730 | tf_op jit(solution)/shard_map/broadcast_in_dim | solution.py:72
  24.2 0.8 bitcast_dynamic-update-slice_fusion.6
  24.9 5.1 %collective-permute-done.1 = bf16[2,128,768]{2,1,0:T(8,128)(2,1)S(1)} collective-permute-done((bf16[2,128,768]{2,1,0:T(8,128)(2,1)S(1)}, bf16[2,128,768]{2,1,0:T(8,128)(2,1)S(1)}, u32[]{:S(2)}, u32[]{:S(2)}) %collective-permute-start.1) | collective-permute-done | bytes 393248 | tf_op jit(solution)/shard_map/ppermute | solution.py:77
  30.1 2.7 %collective-permute-start.4 = (bf16[2,128,768]{2,1,0:T(8,128)(2,1)S(1)}, bf16[2,128,768]{2,1,0:T(8,128)(2,1)S(1)}, u32[]{:S(2)}, u32[]{:S(2)}) collective-permute-start(bf16[2,128,768]{2,1,0:T(8,128)(2,1)S(1)} %collective-permute-done.2), channel_id=1, source_target_pairs={{0,112},{16,0},{32,16},{48,32},{64,48},{80,64},{96,80},{112,96},{1... | collective-permute-start | bytes 1179656 | tf_op jit(solution)/shard_map/ppermute | solution.py:80
  32.7 0.8 bitcast_dynamic-update-slice_fusion.5
  33.5 0.8 bitcast_dynamic-update-slice_fusion.4
  34.3 5.5 %collective-permute-done.3 = bf16[2,128,768]{2,1,0:T(8,128)(2,1)S(1)} collective-permute-done((bf16[2,128,768]{2,1,0:T(8,128)(2,1)S(1)}, bf16[2,128,768]{2,1,0:T(8,128)(2,1)S(1)}, u32[]{:S(2)}, u32[]{:S(2)}) %collective-permute-start.3) | collective-permute-done | bytes 393248 | tf_op jit(solution)/shard_map/ppermute | solution.py:77
  39.8 2.7 %collective-permute-start.6 = (bf16[2,128,768]{2,1,0:T(8,128)(2,1)S(1)}, bf16[2,128,768]{2,1,0:T(8,128)(2,1)S(1)}, u32[]{:S(2)}, u32[]{:S(2)}) collective-permute-start(bf16[2,128,768]{2,1,0:T(8,128)(2,1)S(1)} %collective-permute-done.4), channel_id=1, source_target_pairs={{0,112},{16,0},{32,16},{48,32},{64,48},{80,64},{96,80},{112,96},{1... | collective-permute-start | bytes 1179656 | tf_op jit(solution)/shard_map/ppermute | solution.py:80
  42.5 0.8 bitcast_dynamic-update-slice_fusion.3
  43.3 0.8 bitcast_dynamic-update-slice_fusion.2
  44.1 4.7 %collective-permute-done.5 = bf16[2,128,768]{2,1,0:T(8,128)(2,1)S(1)} collective-permute-done((bf16[2,128,768]{2,1,0:T(8,128)(2,1)S(1)}, bf16[2,128,768]{2,1,0:T(8,128)(2,1)S(1)}, u32[]{:S(2)}, u32[]{:S(2)}) %collective-permute-start.5) | collective-permute-done | bytes 393248 | tf_op jit(solution)/shard_map/ppermute | solution.py:77
  48.8 0.8 bitcast_dynamic-update-slice_fusion.1
  49.6 0.8 bitcast_dynamic-update-slice_fusion
  50.3 6.3 %collective-permute-done.7 = bf16[2,128,768]{2,1,0:T(8,128)(2,1)S(1)} collective-permute-done((bf16[2,128,768]{2,1,0:T(8,128)(2,1)S(1)}, bf16[2,128,768]{2,1,0:T(8,128)(2,1)S(1)}, u32[]{:S(2)}, u32[]{:S(2)}) %collective-permute-start.7) | collective-permute-done | bytes 393248 | tf_op jit(solution)/shard_map/ppermute | solution.py:77
  56.6 0.8 bitcast_dynamic-update-slice_fusion.7
  57.4 5.0 %collective-permute-start.8 = (bf16[8,2,128,768]{3,2,0,1:T(8,128)(2,1)}, bf16[8,2,128,768]{3,2,0,1:T(8,128)(2,1)}, u32[]{:S(2)}, u32[]{:S(2)}) collective-permute-start(bf16[8,2,128,768]{3,2,0,1:T(8,128)(2,1)} %bitcast_dynamic-update-slice_fusion.7), channel_id=1, source_target_pairs={{0,8},{8,0},{1,9},{9,1},{2,10},{10,2},{3,11},{11,3},{4,12},{12,4},... | collective-permute-start | bytes 9437192 | tf_op jit(solution)/shard_map/ppermute | solution.py:82
  63.1 0.3 pad_add_fusion
  63.4 2.2 %broadcast_in_dim.83 = pred[4,384,1536]{1,0,2:T(4,128)(4,1)S(1)} broadcast(pred[384,1536]{0,1:T(8,128)(4,1)S(1)} %pad_add_fusion), dimensions={1,2} | broadcast | bytes 2949120 | tf_op jit(solution)/shard_map/while/body/eval_jaxpr/jit(_where)/broadcast_in_dim | solution.py:39
  65.6 2.7 %copy.69 = pred[192,8,4,384]{3,1,2,0:T(8,128)(4,1)} copy(pred[192,8,4,384]{3,2,1,0:T(4,128)(4,1)S(1)} %bitcast.111) | data formatting | bytes 4718592
  68.7 3.4 %copy.49 = bf16[384,4096]{0,1:T(8,128)(2,1)S(1)} copy(bf16[384,4096]{1,0:T(8,128)(2,1)} %param.8) | data formatting | bytes 6291456 | tf_op args[0]
  72.1 1.5 dynamic-slice_bitcast_fusion
  73.6 1.3 copy.50
  75.0 3.3 %select_bitcast_fusion.1 = (bf16[8,2,1,128,768]{4,3,2,0,1:T(8,128)(2,1)S(1)}, bf16[8,2,1,128,768]{4,3,2,0,1:T(8,128)(2,1)S(1)}) fusion(bf16[8,2,128,768]{3,2,0,1:T(8,128)(2,1)} %bitcast_dynamic-update-slice_fusion.7, bf16[8,2,128,768]{3,2,0,1:T(8,128)(2,1)} %collective-permute-done.8, pred[]{:T(512)S(6)} %eq.16), kind=kLoop, calls=%fused_computation.17 | loop fusion | flops 3145728 | bytes 12582913 | tf_op jit(solution)/shard_map/stack | solution.py:85
  78.2 0.6 pad_maximum_fusion
  78.8 2.1 %copy-done.2 = bf16[384,4096]{1,0:T(8,128)(2,1)S(1)} copy-done((bf16[384,4096]{1,0:T(8,128)(2,1)S(1)}, bf16[384,4096]{1,0:T(8,128)(2,1)}, u32[]{:S(2)}) %copy-start.2) | copy-done | bytes 3145752
  81.0 3.4 %fusion.5 = bf16[384,768]{0,1:T(8,128)(2,1)S(1)} fusion(bf16[4096,768]{1,0:T(8,128)(2,1)S(1)} %bitcast.113, bf16[384,4096]{1,0:T(8,128)(2,1)S(1)} %copy-done.2), kind=kOutput, calls=%fused_computation.24 | convolution fusion | flops 2416214016 | bytes 10027008 | tf_op jit(solution)/shard_map/dot_general | solution.py:98
  84.5 0.7 fusion.23
  85.4 1.1 copy.60
  86.5 1.7 copy.61
  88.2 2.7 %fusion.25 = (f32[1536]{0:T(1024)S(1)}, f32[1536,1536]{0,1:T(8,128)S(1)}) fusion(pred[1536,1536]{0,1:T(8,128)(4,1)S(1)} %bitcast.118, bf16[1536,128]{1,0:T(8,128)(2,1)S(1)} %bitcast.129, bf16[384,128]{1,0:T(8,128)(2,1)S(1)} %copy.60, bf16[1152,128]{1,0:T(8,128)(2,1)} %bitcast.135), kind=kOutput, calls=%fused_computation.62 | convolution fusion | flops 611842560 | bytes 12589056 | tf_op jit(solution)/shard_map/while/body/eval_jaxpr/dot_general | solution.py:14
  91.0 1.3 fusion.4
  92.3 4.7 %fusion.1 = (f32[1536]{0:T(1024)S(1)}, bf16[1536,1536]{0,1:T(8,128)(2,1)}, f32[1536,1536]{1,0:T(8,128)S(1)}) fusion(f32[1536]{0:T(1024)S(1)} %fusion.4, f32[1536,1536]{0,1:T(8,128)S(1)} %get-tuple-element.58, f32[1536]{0:T(1024)S(1)} %get-tuple-element.57, bf16[1536,128]{1,0:T(8,128)(2,1)S(1)} %bitcast.127, bf16[384,128]{1,0:T(8,128)(2,1)S(1)} %copy-done.9, ...), kind=kOutput, calls=%fused_computation.4 | convolution fusion | flops 618920448 | bytes 24397824 | tf_op jit(solution)/shard_map/while/body/eval_jaxpr/dot_general | solution.py:14
  97.0 6.5 %fusion.3 = bf16[1536,1536]{0,1:T(8,128)(2,1)} fusion(bf16[1536,1536]{0,1:T(8,128)(2,1)} %get-tuple-element.34, f32[1536,1536]{1,0:T(8,128)S(1)} %get-tuple-element.59, f32[1536]{0:T(1024)S(1)} %get-tuple-element.33), kind=kLoop, calls=%fused_computation.6 | loop fusion | flops 11796480 | bytes 18880512 | tf_op jit(solution)/shard_map/while/body/eval_jaxpr/convert_element_type | solution.py:48
  103.4 4.6 %convolution_convert_fusion.3 = bf16[1536,128]{1,0:T(8,128)(2,1)} fusion(bf16[1536,1536]{0,1:T(8,128)(2,1)} %fusion.3, bf16[384,128]{1,0:T(8,128)(2,1)} %copy-done.11, bf16[1152,128]{1,0:T(8,128)(2,1)} %bitcast.136), kind=kOutput, calls=%fused_computation.19 | convolution fusion | flops 604962816 | bytes 5505024 | tf_op jit(solution)/shard_map/while/body/eval_jaxpr/dot_general | solution.py:49
  108.1 1.9 %fusion.10 = bf16[384,128]{0,1:T(8,128)(2,1)S(1)} fusion(bf16[1536,128]{1,0:T(8,128)(2,1)S(1)} %bitcast.130, bf16[1536,1536]{0,1:T(8,128)(2,1)} %fusion.3), kind=kOutput, calls=%fused_computation.29 | convolution fusion | flops 151044096 | bytes 1671168 | tf_op jit(solution)/shard_map/while/body/eval_jaxpr/dot_general | solution.py:20
  110.0 1.8 fusion.13
  111.7 1.3 copy.64
  113.0 1.8 convolution_convert_fusion.1
  114.9 0.4 collective-permute-start.9
  115.7 0.3 copy-done.10
  116.1 1.4 convolution_convert_fusion.2
  117.5 0.3 copy.65
  117.8 0.8 copy.74
  118.6 1.8 fusion.22
  120.5 0.5 collective-permute-done.9
  120.9 2.4 %add_convert_fusion = bf16[2048,768]{1,0:T(8,128)(2,1)} fusion(f32[2048,768]{1,0:T(8,128)S(1)} %fusion.22, bf16[2048,768]{1,0:T(8,128)(2,1)S(1)} %collective-permute-done.9), kind=kLoop, calls=%fused_computation.12 | loop fusion | flops 4718592 | bytes 12582912 | tf_op jit(solution)/shard_map/convert_element_type | solution.py:130
  123.4 5.4 %convolution_convert_fusion = bf16[384,4096]{1,0:T(8,128)(2,1)S(1)} fusion(bf16[4096,768]{1,0:T(8,128)(2,1)} %bitcast.114, bf16[384,128]{0,1:T(8,128)(2,1)S(1)} %fusion.13, bf16[384,128]{0,1:T(8,128)(2,1)S(1)} %fusion.10, bf16[384,512]{0,1:T(8,128)(2,1)S(1)} %bitcast.121), kind=kOutput, calls=%fused_computation.13 | convolution fusion | flops 2419261440 | bytes 10027008 | tf_op jit(solution)/shard_map/dot_general | solution.py:14
  128.8 1.9 %copy.73 = bf16[48,8,8,512]{3,2,0,1:T(8,128)(2,1)} copy(bf16[48,8,8,512]{3,2,1,0:T(8,128)(2,1)S(1)} %bitcast.117) | data formatting | bytes 6291456 | tf_op jit(solution)/shard_map/reshape | solution.py:137
  130.7 6.6 %all-to-all-start = ((bf16[8,384,512]{2,1,0:T(8,128)(2,1)}), bf16[8,384,512]{2,1,0:T(8,128)(2,1)S(1)}, u32[]{:S(2)}, u32[]{:S(2)}) async-start(bf16[8,384,512]{2,1,0:T(8,128)(2,1)} %bitcast.107), calls=%async_computation | async-start | bytes 6291456 | tf_op jit(solution)/shard_map/all_to_all | solution.py:138
  137.4 29.1 %reduce-scatter.2.cloned.1.call-done = bf16[256,768]{1,0:T(8,128)(2,1)} async-done(((bf16[2048,768]{1,0:T(8,128)(2,1)}), bf16[256,768]{1,0:T(8,128)(2,1)}) %reduce-scatter.2.cloned.1.call-update) | async-done | bytes 393232 | tf_op jit(solution)/shard_map/reduce_scatter | solution.py:131
  166.5 1.7 dynamic-slice_bitcast_fusion.2
  168.2 1.3 collective-permute-start.10
  169.5 7.3 %all-to-all-done = bf16[8,384,512]{2,1,0:T(8,128)(2,1)S(1)} async-done(((bf16[8,384,512]{2,1,0:T(8,128)(2,1)}), bf16[8,384,512]{2,1,0:T(8,128)(2,1)S(1)}, u32[]{:S(2)}, u32[]{:S(2)}) %all-to-all-start) | async-done | bytes 3145760 | tf_op jit(solution)/shard_map/all_to_all | solution.py:138
  176.7 1.3 reduce_sum.34
  178.0 1.0 fusion.16
  179.0 0.7 slice.42
  179.8 0.7 fusion.24
  (51 shorter events, 1.5 us)
Async XLA Ops:
  7.2 159.3 %reduce-scatter.2.cloned.1.call-start = ((), (), s32[]{:S(2)}) async-start(), calls=%async_computation.2 | async-start | bytes 3538944 | tf_op jit(solution)/shard_map/reduce_scatter | solution.py:131
  9.7 5.5 %collective-permute-start = (bf16[128,768]{1,0:T(8,128)(2,1)S(1)}, bf16[128,768]{1,0:T(8,128)(2,1)S(1)}, u32[]{:S(2)}, u32[]{:S(2)}) collective-permute-start(bf16[128,768]{1,0:T(8,128)(2,1)S(1)} %constant_dynamic-update-slice_fusion), channel_id=1, source_target_pairs={{0,128},{128,0},{1,129},{129,1},{2,130},{130,2},{3,131},{131,3},{4... | collective-permute-start | bytes 589832 | tf_op jit(solution)/shard_map/ppermute | solution.py:68
  15.2 14.8 %collective-permute-start.1 = (bf16[2,128,768]{2,1,0:T(8,128)(2,1)S(1)}, bf16[2,128,768]{2,1,0:T(8,128)(2,1)S(1)}, u32[]{:S(2)}, u32[]{:S(2)}) collective-permute-start(bf16[2,128,768]{2,1,0:T(8,128)(2,1)S(1)} %pad_maximum_fusion.2), channel_id=1, source_target_pairs={{0,16},{16,32},{32,48},{48,64},{64,80},{80,96},{96,112},{112,0},{1... | collective-permute-start | bytes 1179656 | tf_op jit(solution)/shard_map/ppermute | solution.py:77
  18.1 11.9 %collective-permute-start.2 = (bf16[2,128,768]{2,1,0:T(8,128)(2,1)S(1)}, bf16[2,128,768]{2,1,0:T(8,128)(2,1)S(1)}, u32[]{:S(2)}, u32[]{:S(2)}) collective-permute-start(bf16[2,128,768]{2,1,0:T(8,128)(2,1)S(1)} %pad_maximum_fusion.2), channel_id=1, source_target_pairs={{0,112},{16,0},{32,16},{48,32},{64,48},{80,64},{96,80},{112,96},{1... | collective-permute-start | bytes 1179656 | tf_op jit(solution)/shard_map/ppermute | solution.py:80
  30.1 9.8 %collective-permute-start.3 = (bf16[2,128,768]{2,1,0:T(8,128)(2,1)S(1)}, bf16[2,128,768]{2,1,0:T(8,128)(2,1)S(1)}, u32[]{:S(2)}, u32[]{:S(2)}) collective-permute-start(bf16[2,128,768]{2,1,0:T(8,128)(2,1)S(1)} %collective-permute-done.1), channel_id=1, source_target_pairs={{0,16},{16,32},{32,48},{48,64},{64,80},{80,96},{96,112},{112,0},{1... | collective-permute-start | bytes 1179656 | tf_op jit(solution)/shard_map/ppermute | solution.py:77
  30.1 9.8 %collective-permute-start.4 = (bf16[2,128,768]{2,1,0:T(8,128)(2,1)S(1)}, bf16[2,128,768]{2,1,0:T(8,128)(2,1)S(1)}, u32[]{:S(2)}, u32[]{:S(2)}) collective-permute-start(bf16[2,128,768]{2,1,0:T(8,128)(2,1)S(1)} %collective-permute-done.2), channel_id=1, source_target_pairs={{0,112},{16,0},{32,16},{48,32},{64,48},{80,64},{96,80},{112,96},{1... | collective-permute-start | bytes 1179656 | tf_op jit(solution)/shard_map/ppermute | solution.py:80
  39.8 8.9 %collective-permute-start.5 = (bf16[2,128,768]{2,1,0:T(8,128)(2,1)S(1)}, bf16[2,128,768]{2,1,0:T(8,128)(2,1)S(1)}, u32[]{:S(2)}, u32[]{:S(2)}) collective-permute-start(bf16[2,128,768]{2,1,0:T(8,128)(2,1)S(1)} %collective-permute-done.3), channel_id=1, source_target_pairs={{0,16},{16,32},{32,48},{48,64},{64,80},{80,96},{96,112},{112,0},{1... | collective-permute-start | bytes 1179656 | tf_op jit(solution)/shard_map/ppermute | solution.py:77
  39.8 9.7 %collective-permute-start.6 = (bf16[2,128,768]{2,1,0:T(8,128)(2,1)S(1)}, bf16[2,128,768]{2,1,0:T(8,128)(2,1)S(1)}, u32[]{:S(2)}, u32[]{:S(2)}) collective-permute-start(bf16[2,128,768]{2,1,0:T(8,128)(2,1)S(1)} %collective-permute-done.4), channel_id=1, source_target_pairs={{0,112},{16,0},{32,16},{48,32},{64,48},{80,64},{96,80},{112,96},{1... | collective-permute-start | bytes 1179656 | tf_op jit(solution)/shard_map/ppermute | solution.py:80
  48.8 7.8 %collective-permute-start.7 = (bf16[2,128,768]{2,1,0:T(8,128)(2,1)S(1)}, bf16[2,128,768]{2,1,0:T(8,128)(2,1)S(1)}, u32[]{:S(2)}, u32[]{:S(2)}) collective-permute-start(bf16[2,128,768]{2,1,0:T(8,128)(2,1)S(1)} %collective-permute-done.5), channel_id=1, source_target_pairs={{0,16},{16,32},{32,48},{48,64},{64,80},{80,96},{96,112},{112,0},{1... | collective-permute-start | bytes 1179656 | tf_op jit(solution)/shard_map/ppermute | solution.py:77
  57.4 17.6 %collective-permute-start.8 = (bf16[8,2,128,768]{3,2,0,1:T(8,128)(2,1)}, bf16[8,2,128,768]{3,2,0,1:T(8,128)(2,1)}, u32[]{:S(2)}, u32[]{:S(2)}) collective-permute-start(bf16[8,2,128,768]{3,2,0,1:T(8,128)(2,1)} %bitcast_dynamic-update-slice_fusion.7), channel_id=1, source_target_pairs={{0,8},{8,0},{1,9},{9,1},{2,10},{10,2},{3,11},{11,3},{4,12},{12,4},... | collective-permute-start | bytes 9437192 | tf_op jit(solution)/shard_map/ppermute | solution.py:82
  63.4 4.9 %copy-start.5 = (bf16[384,512]{1,0:T(8,128)(2,1)S(1)}, bf16[384,512]{1,0:T(8,128)(2,1)}, u32[]{:S(2)}) copy-start(bf16[384,512]{1,0:T(8,128)(2,1)} %param.15) | copy-start | bytes 1179652
  78.2 2.7 %copy-start.2 = (bf16[384,4096]{1,0:T(8,128)(2,1)S(1)}, bf16[384,4096]{1,0:T(8,128)(2,1)}, u32[]{:S(2)}) copy-start(bf16[384,4096]{1,0:T(8,128)(2,1)} %param.8) | copy-start | bytes 9437188
  78.8 5.6 %copy-start = (bf16[8,2,2,128,768]{4,3,2,0,1:T(8,128)(2,1)}, bf16[8,2,2,128,768]{4,3,2,0,1:T(8,128)(2,1)S(1)}, u32[]{:S(2)}) copy-start(bf16[8,2,2,128,768]{4,3,2,0,1:T(8,128)(2,1)S(1)} %pad_maximum_fusion) | copy-start | bytes 18874372
  81.0 7.2 %copy-start.3 = (pred[192,8,4,384]{3,1,2,0:T(8,128)(4,1)S(1)}, pred[192,8,4,384]{3,1,2,0:T(8,128)(4,1)}, u32[]{:S(2)}) copy-start(pred[192,8,4,384]{3,1,2,0:T(8,128)(4,1)} %copy.69) | copy-start | bytes 7077892
  85.4 5.5 %copy-start.6 = (bf16[384,1,4,128]{3,0,2,1:T(8,128)(2,1)}, bf16[384,1,4,128]{3,0,2,1:T(8,128)(2,1)S(1)}, u32[]{:S(2)}) copy-start(bf16[384,1,4,128]{3,0,2,1:T(8,128)(2,1)S(1)} %copy.59) | copy-start | bytes 1179652
  86.5 4.4 %copy-start.11 = (bf16[384,128]{1,0:T(8,128)(2,1)}, bf16[384,128]{1,0:T(8,128)(2,1)S(1)}, u32[]{:S(2)}) copy-start(bf16[384,128]{1,0:T(8,128)(2,1)S(1)} %copy.60) | copy-start | bytes 294916
  90.9 1.3 copy-start.9
  90.9 1.3 copy-start.12
  103.4 4.6 %copy-start.7 = (bf16[384,1,4,128]{3,0,2,1:T(8,128)(2,1)S(1)}, bf16[384,1,4,128]{3,0,2,1:T(8,128)(2,1)}, u32[]{:S(2)}) copy-start(bf16[384,1,4,128]{3,0,2,1:T(8,128)(2,1)} %copy-done.6) | copy-start | bytes 1179652
  108.1 4.9 %copy-start.4 = (bf16[384,8,2,1,128]{0,4,2,1,3:T(8,128)(2,1)S(1)}, bf16[384,8,2,1,128]{0,4,2,1,3:T(8,128)(2,1)}, u32[]{:S(2)}) copy-start(bf16[384,8,2,1,128]{0,4,2,1,3:T(8,128)(2,1)} %copy.50) | copy-start | bytes 4718596
  111.7 3.7 %slice-start = ((s8[4718592]{0:T(1024)(128)(4,1)}), s8[524288]{0:T(1024)(128)(4,1)S(1)}, s32[]{:S(2)}) async-start(s8[4718592]{0:T(1024)(128)(4,1)} %bitcast.115), calls=%async_computation.3 | async-start | bytes 1048576
  113.0 2.2 %copy-start.1 = (bf16[384,8,2,1,128]{0,4,3,1,2:T(8,128)(2,1)S(1)}, bf16[384,8,2,1,128]{0,4,3,1,2:T(8,128)(2,1)}, u32[]{:S(2)}) copy-start(bf16[384,8,2,1,128]{0,4,3,1,2:T(8,128)(2,1)} %get-tuple-element.49) | copy-start | bytes 4718596
  113.0 2.7 %slice-start.1 = ((s8[4718592]{0:T(1024)(128)(4,1)}), s8[4194304]{0:T(1024)(128)(4,1)S(1)}, s32[]{:S(2)}) async-start(s8[4718592]{0:T(1024)(128)(4,1)} %bitcast.115), calls=%async_computation.4 | async-start | bytes 8388608
  114.9 1.1 copy-start.10
  114.9 1.2 copy-start.13
  114.9 6.0 %collective-permute-start.9 = (bf16[2048,768]{1,0:T(8,128)(2,1)S(1)}, bf16[2048,768]{1,0:T(8,128)(2,1)S(1)}, u32[]{:S(2)}, u32[]{:S(2)}) collective-permute-start(bf16[2048,768]{1,0:T(8,128)(2,1)S(1)} %convolution_convert_fusion.1), channel_id=1, source_target_pairs={{0,8},{8,0},{1,9},{9,1},{2,10},{10,2},{3,11},{11,3},{4,12},{12,4},... | collective-permute-start | bytes 9437192 | tf_op jit(solution)/shard_map/ppermute | solution.py:127
  130.7 46.0 %all-to-all-start = ((bf16[8,384,512]{2,1,0:T(8,128)(2,1)}), bf16[8,384,512]{2,1,0:T(8,128)(2,1)S(1)}, u32[]{:S(2)}, u32[]{:S(2)}) async-start(bf16[8,384,512]{2,1,0:T(8,128)(2,1)} %bitcast.107), calls=%async_computation | async-start | bytes 6291456 | tf_op jit(solution)/shard_map/all_to_all | solution.py:138
  166.5 11.6 %copy-start.8 = (bf16[256,768]{1,0:T(8,128)(2,1)S(1)}, bf16[256,768]{1,0:T(8,128)(2,1)}, u32[]{:S(2)}) copy-start(bf16[256,768]{1,0:T(8,128)(2,1)} %reduce-scatter.2.cloned.1.call-done) | copy-start | bytes 1179652
  168.2 9.9 %collective-permute-start.10 = (bf16[128,768]{1,0:T(8,128)(2,1)}, bf16[128,768]{1,0:T(8,128)(2,1)}, u32[]{:S(2)}, u32[]{:S(2)}) collective-permute-start(bf16[128,768]{1,0:T(8,128)(2,1)} %dynamic-slice_bitcast_fusion.2), channel_id=1, source_target_pairs={{0,128},{128,0},{1,129},{129,1},{2,130},{130,2},{3,131},{131,3},{4... | collective-permute-start | bytes 589832 | tf_op jit(solution)/shard_map/ppermute | solution.py:135
Sparse Core Ops, SparseCore 0:
  123.5 42.9 reduce-scatter.1

commit v9 on v8

--- a/solution.py
+++ b/solution.py
@@ -83,7 +83,7 @@
     first = jnp.where(chip_core == 0, ring, other)
     second = jnp.where(chip_core == 0, other, ring)
     full = jnp.stack([first, second], 2)
-    return full.transpose(1, 0, 2, 3, 4).reshape(-1, width)
+    return ring.reshape(-1, width), other.reshape(-1, width), full.transpose(1, 0, 2, 3, 4).reshape(-1, width)
 
 
 def local(hidden_in, w_query, w_key, w_value, starts, key_cache, value_cache, grad_out):
@@ -94,8 +94,15 @@
     query_cols = w_query.shape[1]
     kv_cols = w_key.shape[1]
     local_w = jnp.concatenate([w_query, w_key, w_value], 1)
-    full_w = gather_rows(local_w)
-    proj = jnp.dot(hidden_in, full_w, preferred_element_type=jnp.float32)
+    own_w, other_w, full_w = gather_rows(local_w)
+    z_count = lax.axis_size("z")
+    rows = w_query.shape[0]
+    chip_core = lax.axis_index("c")
+    by_place = hidden_in.reshape(tokens_dev, 2, z_count, 2, rows).transpose(0, 2, 1, 3, 4)
+    cols_other = lax.dynamic_index_in_dim(by_place, 1 - chip_core, 3, False).reshape(tokens_dev, -1)
+    cols_own = lax.dynamic_index_in_dim(by_place, chip_core, 3, False).reshape(tokens_dev, -1)
+    proj = jnp.dot(cols_own, own_w, preferred_element_type=jnp.float32)
+    proj = proj + jnp.dot(cols_other, other_w, preferred_element_type=jnp.float32)
     queries = proj[:, :query_cols].astype(jnp.bfloat16)
     new_keys = proj[:, query_cols : query_cols + kv_cols].astype(jnp.bfloat16)
     new_values = proj[:, query_cols + kv_cols :].astype(jnp.bfloat16)
@@ -116,17 +123,11 @@
     grad_values = results[3].transpose(1, 0, 2).reshape(tokens_dev, kv_local * HD)
     grads_cat = jnp.concatenate([grad_query, grad_keys, grad_values], 1)
     tp_count = lax.axis_size("tp")
-    z_count = lax.axis_size("z")
-    rows = w_query.shape[0]
-    chip_core = lax.axis_index("c")
     x_pos = lax.axis_index("xl")
-    by_place = hidden_in.reshape(tokens_dev, 2, z_count, 2, rows).transpose(0, 2, 1, 3, 4)
-    cols_other = lax.dynamic_index_in_dim(by_place, 1 - chip_core, 3, False)
-    cols_own = lax.dynamic_index_in_dim(by_place, chip_core, 3, False)
-    part_other = contract_first(cols_other.reshape(tokens_dev, -1), grads_cat)
+    part_other = contract_first(cols_other, grads_cat)
     from_peer = lax.ppermute(part_other.astype(jnp.bfloat16), "c", SWAP)
     from_peer, attended = lax.optimization_barrier((from_peer, attended))
-    part_own = contract_first(cols_own.reshape(tokens_dev, -1), grads_cat)
+    part_own = contract_first(cols_own, grads_cat)
     chip_sum = (part_own + from_peer.astype(jnp.float32)).astype(jnp.bfloat16)
     ring_sum = lax.psum_scatter(chip_sum, "z", scatter_dimension=0, tiled=True)
     ring_sum = ring_sum.reshape(2, rows, -1)

time: 188 us -> 181 us (0.963)
  local copies, waits for them, and re-layouts: 35.5 us -> 29.8 us
    dot_general x3, matrix products: 12.8 us -> 8.12 us  [contract_last(): lax.dot_general(left, right, (((1,), (1,)), ((), ())), preferred_element_...]
    dot_general x1 -> x2, matrix products: 3.44 us -> 7.73 us  [the longest x1 4.23 us: local(): jnp.dot(cols_other, other_w, preferred_element_type=jnp.float32)]
    dynamic_slice x3, local copies, waits for them, and re-layouts: 3.01 us -> 0.69 us  [the longest x2 0.51 us: local(): lax.dynamic_index_in_dim(by_place, chip_core, 3, False)]
    reduce_scatter x1, waiting for transfers between devices: 29.1 us -> 26.9 us  [local(): ring_sum = lax.psum_scatter(chip_sum, 'z', scatter_dimension=0, tiled=True)]
    all_to_all x1, waiting for transfers between devices: 7.28 us -> 9.42 us  [local(): gathered = lax.all_to_all(input_term, 'tp', 0, 0, tiled=True)]
    another operation x2 -> x1, other arithmetic: 3.84 us -> 3.26 us  [gather_rows(): full = jnp.stack([first, second], 2)]
    unnamed x38 -> x40, local copies, waits for them, and re-layouts: 11.6 us -> 11.4 us
  transfers between devices with their start and end apart: 13 -> 13, of which waited for: 8 -> 8; matrix products, arithmetic and copies ran while one was open for 18% -> 19% of each run, Pallas kernels for 0% -> 0%
where the time goes in v9:
time: 181 us; the launch traced here: 180 us
  waiting for transfers between devices  62.3 us (34%)
  local copies, waits for them, and re-layouts  29.8 us (16%)
  matrix products  28 us (15%)
  starting transfers between devices  27.6 us (15%)
  other arithmetic  17.6 us (10%)
  between operations  15.1 us (8%)
    reduce_scatter x1, waiting for transfers between devices, local(): ring_sum = lax.psum_scatter(chip_sum, 'z', scatter_dimension=0, tiled=True)  26.9 us
    ppermute x4, waiting for transfers between devices, gather_rows(): fwd = lax.ppermute(fwd, 'z', ahead)  21.6 us
    unnamed x40, local copies, waits for them, and re-layouts  11.4 us
    all_to_all x1, waiting for transfers between devices, local(): gathered = lax.all_to_all(input_term, 'tp', 0, 0, tiled=True)  9.42 us
    ppermute x3, starting transfers between devices, gather_rows(): bwd = lax.ppermute(bwd, 'z', behind)  9.38 us
    dot_general x3, matrix products, contract_last(): lax.dot_general(left, right, (((1,), (1,)), ((), ())), preferred_element_...  8.12 us
    all_to_all x1, starting transfers between devices, local(): gathered = lax.all_to_all(input_term, 'tp', 0, 0, tiled=True)  6.67 us
    convert_element_type x1, other arithmetic, head_pass(): (probs_wide * (grad_probs - row_dot) * factor).astype(jnp.bfloat16)  6.57 us
  transfers between devices with their start and end apart: 13, of which 8 were waited for; matrix products, arithmetic and copies ran while one was open for 19% of the time, Pallas kernels for 0%

profile of v9, /device:TPU:1, one launch (start us, length us, event | category | flops | bytes accessed | tf_op | source)
XLA Modules:
  0.0 180.3 jit_solution(7608025678987882559)
XLA Ops:
  7.2 0.9 constant_dynamic-update-slice_fusion.2
  8.1 0.8 constant_dynamic-update-slice_fusion.1
  8.9 0.8 constant_dynamic-update-slice_fusion
  9.7 2.1 %collective-permute-start = (bf16[128,768]{1,0:T(8,128)(2,1)S(1)}, bf16[128,768]{1,0:T(8,128)(2,1)S(1)}, u32[]{:S(2)}, u32[]{:S(2)}) collective-permute-start(bf16[128,768]{1,0:T(8,128)(2,1)S(1)} %constant_dynamic-update-slice_fusion), channel_id=1, source_target_pairs={{0,128},{128,0},{1,129},{129,1},{2,130},{130,2},{3,131},{131,3},{4... | collective-permute-start | bytes 589832 | tf_op jit(solution)/shard_map/ppermute | solution.py:68
  11.8 3.4 %collective-permute-done = bf16[128,768]{1,0:T(8,128)(2,1)S(1)} collective-permute-done((bf16[128,768]{1,0:T(8,128)(2,1)S(1)}, bf16[128,768]{1,0:T(8,128)(2,1)S(1)}, u32[]{:S(2)}, u32[]{:S(2)}) %collective-permute-start) | collective-permute-done | bytes 196640 | tf_op jit(solution)/shard_map/ppermute | solution.py:68
  15.2 2.9 %collective-permute-start.1 = (bf16[2,128,768]{2,1,0:T(8,128)(2,1)S(1)}, bf16[2,128,768]{2,1,0:T(8,128)(2,1)S(1)}, u32[]{:S(2)}, u32[]{:S(2)}) collective-permute-start(bf16[2,128,768]{2,1,0:T(8,128)(2,1)S(1)} %pad_maximum_fusion.1), channel_id=1, source_target_pairs={{0,16},{16,32},{32,48},{48,64},{64,80},{80,96},{96,112},{112,0},{1... | collective-permute-start | bytes 1179656 | tf_op jit(solution)/shard_map/ppermute | solution.py:77
  18.1 4.0 %collective-permute-start.2 = (bf16[2,128,768]{2,1,0:T(8,128)(2,1)S(1)}, bf16[2,128,768]{2,1,0:T(8,128)(2,1)S(1)}, u32[]{:S(2)}, u32[]{:S(2)}) collective-permute-start(bf16[2,128,768]{2,1,0:T(8,128)(2,1)S(1)} %pad_maximum_fusion.1), channel_id=1, source_target_pairs={{0,112},{16,0},{32,16},{48,32},{64,48},{80,64},{96,80},{112,96},{1... | collective-permute-start | bytes 1179656 | tf_op jit(solution)/shard_map/ppermute | solution.py:80
  22.2 2.0 %broadcast_in_dim.85 = bf16[8,2,128,768]{3,2,1,0:T(8,128)(2,1)} broadcast(bf16[]{:T(256)} %constant.122.clone.1), dimensions={} | broadcast | bytes 3145730 | tf_op jit(solution)/shard_map/broadcast_in_dim | solution.py:72
  24.1 0.8 bitcast_dynamic-update-slice_fusion.7
  25.0 5.1 %collective-permute-done.1 = bf16[2,128,768]{2,1,0:T(8,128)(2,1)S(1)} collective-permute-done((bf16[2,128,768]{2,1,0:T(8,128)(2,1)S(1)}, bf16[2,128,768]{2,1,0:T(8,128)(2,1)S(1)}, u32[]{:S(2)}, u32[]{:S(2)}) %collective-permute-start.1) | collective-permute-done | bytes 393248 | tf_op jit(solution)/shard_map/ppermute | solution.py:77
  30.1 2.7 %collective-permute-start.4 = (bf16[2,128,768]{2,1,0:T(8,128)(2,1)S(1)}, bf16[2,128,768]{2,1,0:T(8,128)(2,1)S(1)}, u32[]{:S(2)}, u32[]{:S(2)}) collective-permute-start(bf16[2,128,768]{2,1,0:T(8,128)(2,1)S(1)} %collective-permute-done.2), channel_id=1, source_target_pairs={{0,112},{16,0},{32,16},{48,32},{64,48},{80,64},{96,80},{112,96},{1... | collective-permute-start | bytes 1179656 | tf_op jit(solution)/shard_map/ppermute | solution.py:80
  32.7 0.8 bitcast_dynamic-update-slice_fusion.6
  33.5 0.8 bitcast_dynamic-update-slice_fusion.5
  34.3 5.5 %collective-permute-done.3 = bf16[2,128,768]{2,1,0:T(8,128)(2,1)S(1)} collective-permute-done((bf16[2,128,768]{2,1,0:T(8,128)(2,1)S(1)}, bf16[2,128,768]{2,1,0:T(8,128)(2,1)S(1)}, u32[]{:S(2)}, u32[]{:S(2)}) %collective-permute-start.3) | collective-permute-done | bytes 393248 | tf_op jit(solution)/shard_map/ppermute | solution.py:77
  39.8 2.7 %collective-permute-start.6 = (bf16[2,128,768]{2,1,0:T(8,128)(2,1)S(1)}, bf16[2,128,768]{2,1,0:T(8,128)(2,1)S(1)}, u32[]{:S(2)}, u32[]{:S(2)}) collective-permute-start(bf16[2,128,768]{2,1,0:T(8,128)(2,1)S(1)} %collective-permute-done.4), channel_id=1, source_target_pairs={{0,112},{16,0},{32,16},{48,32},{64,48},{80,64},{96,80},{112,96},{1... | collective-permute-start | bytes 1179656 | tf_op jit(solution)/shard_map/ppermute | solution.py:80
  42.5 0.8 bitcast_dynamic-update-slice_fusion.4
  43.3 0.8 bitcast_dynamic-update-slice_fusion.3
  44.1 4.7 %collective-permute-done.5 = bf16[2,128,768]{2,1,0:T(8,128)(2,1)S(1)} collective-permute-done((bf16[2,128,768]{2,1,0:T(8,128)(2,1)S(1)}, bf16[2,128,768]{2,1,0:T(8,128)(2,1)S(1)}, u32[]{:S(2)}, u32[]{:S(2)}) %collective-permute-start.5) | collective-permute-done | bytes 393248 | tf_op jit(solution)/shard_map/ppermute | solution.py:77
  48.8 0.8 bitcast_dynamic-update-slice_fusion.2
  49.5 0.8 bitcast_dynamic-update-slice_fusion.1
  50.3 6.3 %collective-permute-done.7 = bf16[2,128,768]{2,1,0:T(8,128)(2,1)S(1)} collective-permute-done((bf16[2,128,768]{2,1,0:T(8,128)(2,1)S(1)}, bf16[2,128,768]{2,1,0:T(8,128)(2,1)S(1)}, u32[]{:S(2)}, u32[]{:S(2)}) %collective-permute-start.7) | collective-permute-done | bytes 393248 | tf_op jit(solution)/shard_map/ppermute | solution.py:77
  56.6 0.8 bitcast_dynamic-update-slice_fusion
  57.4 5.0 %collective-permute-start.8 = (bf16[8,2,128,768]{3,2,1,0:T(8,128)(2,1)}, bf16[8,2,128,768]{3,2,1,0:T(8,128)(2,1)}, u32[]{:S(2)}, u32[]{:S(2)}) collective-permute-start(bf16[8,2,128,768]{3,2,1,0:T(8,128)(2,1)} %bitcast_dynamic-update-slice_fusion), channel_id=1, source_target_pairs={{0,8},{8,0},{1,9},{9,1},{2,10},{10,2},{3,11},{11,3},{4,12},{12,4},... | collective-permute-start | bytes 9437192 | tf_op jit(solution)/shard_map/ppermute | solution.py:82
  63.0 0.2 copy.40
  63.2 0.2 copy.41
  63.5 0.3 pad_add_fusion
  63.8 2.2 %broadcast_in_dim.83 = pred[4,384,1536]{1,0,2:T(4,128)(4,1)S(1)} broadcast(pred[384,1536]{0,1:T(8,128)(4,1)S(1)} %pad_add_fusion), dimensions={1,2} | broadcast | bytes 2949120 | tf_op jit(solution)/shard_map/while/body/eval_jaxpr/jit(_where)/broadcast_in_dim | solution.py:39
  66.1 2.6 %copy.47 = pred[192,8,4,384]{3,1,2,0:T(8,128)(4,1)} copy(pred[192,8,4,384]{3,2,1,0:T(4,128)(4,1)S(1)} %bitcast.96) | data formatting | bytes 4718592
  68.7 3.6 %copy.36 = bf16[384,4096]{0,1:T(8,128)(2,1)S(1)} copy(bf16[384,4096]{1,0:T(8,128)(2,1)} %param.8) | data formatting | bytes 6291456 | tf_op args[0]
  72.3 0.3 dynamic-slice_bitcast_fusion
  73.0 4.2 %fusion.26 = f32[384,768]{1,0:T(8,128)S(1)} fusion(bf16[384,2048]{0,1:T(8,128)(2,1)S(1)} %bitcast.107, bf16[2048,768]{1,0:T(8,128)(2,1)} %bitcast.17), kind=kOutput, calls=%fused_computation.63 | convolution fusion | flops 1207959552 | bytes 5898240 | tf_op jit(solution)/shard_map/dot_general | solution.py:105
  77.3 3.5 %fusion.5 = bf16[384,768]{1,0:T(8,128)(2,1)S(1)} fusion(f32[384,768]{1,0:T(8,128)S(1)} %fusion.26, bf16[384,2048]{0,1:T(8,128)(2,1)S(1)} %bitcast.97, bf16[2048,768]{1,0:T(8,128)(2,1)} %bitcast.16), kind=kOutput, calls=%fused_computation.24 | convolution fusion | flops 1208549376 | bytes 6488064 | tf_op jit(solution)/shard_map/dot_general | solution.py:104
  80.8 0.7 fusion.23
  81.7 2.9 %fusion.25 = (f32[1536]{0:T(1024)S(1)}, f32[1536,1536]{0,1:T(8,128)S(1)}) fusion(pred[1536,1536]{0,1:T(8,128)(4,1)S(1)} %bitcast.103, bf16[1536,128]{1,0:T(8,128)(2,1)S(1)} %bitcast.114, bf16[384,128]{1,0:T(8,128)(2,1)} %get-tuple-element.51, bf16[1152,128]{1,0:T(8,128)(2,1)} %bitcast.120), kind=kOutput, calls=%fused_computation.62 | convolution fusion | flops 611842560 | bytes 12589056 | tf_op jit(solution)/shard_map/while/body/eval_jaxpr/dot_general | solution.py:14
  84.6 1.3 fusion.4
  86.0 2.3 %fusion.1 = (f32[1536]{0:T(1024)S(1)}, bf16[1536,1536]{0,1:T(8,128)(2,1)S(1)}, f32[1536,1536]{1,0:T(8,128)S(1)}) fusion(f32[1536]{0:T(1024)S(1)} %fusion.4, f32[1536,1536]{0,1:T(8,128)S(1)} %get-tuple-element.58, f32[1536]{0:T(1024)S(1)} %get-tuple-element.57, bf16[1536,128]{1,0:T(8,128)(2,1)S(1)} %bitcast.112, bf16[384,128]{1,0:T(8,128)(2,1)S(1)} %copy-done.11, ...), kind=kOutput, calls=%fused_computation.4 | convolution fusion | flops 618920448 | bytes 24397824 | tf_op jit(solution)/shard_map/while/body/eval_jaxpr/dot_general | solution.py:14
  88.3 2.1 %copy-done.2 = bf16[1536,1536]{0,1:T(8,128)(2,1)} copy-done((bf16[1536,1536]{0,1:T(8,128)(2,1)}, bf16[1536,1536]{0,1:T(8,128)(2,1)S(1)}, u32[]{:S(2)}) %copy-start.2) | copy-done | bytes 4718616
  90.4 1.1 fusion.13
  91.5 6.6 %fusion.3 = bf16[1536,1536]{0,1:T(8,128)(2,1)} fusion(bf16[1536,1536]{0,1:T(8,128)(2,1)} %copy-done.2, f32[1536,1536]{1,0:T(8,128)S(1)} %get-tuple-element.59, f32[1536]{0:T(1024)S(1)} %get-tuple-element.33), kind=kLoop, calls=%fused_computation.6 | loop fusion | flops 11796480 | bytes 18880512 | tf_op jit(solution)/shard_map/while/body/eval_jaxpr/convert_element_type | solution.py:48
  98.1 1.8 fusion.10
  99.9 4.2 %convolution_convert_fusion.3 = bf16[1536,128]{1,0:T(8,128)(2,1)S(1)} fusion(bf16[1536,1536]{0,1:T(8,128)(2,1)} %fusion.3, bf16[384,128]{1,0:T(8,128)(2,1)} %get-tuple-element.51, bf16[1152,128]{1,0:T(8,128)(2,1)} %bitcast.121), kind=kOutput, calls=%fused_computation.19 | convolution fusion | flops 604962816 | bytes 5505024 | tf_op jit(solution)/shard_map/while/body/eval_jaxpr/dot_general | solution.py:49
  104.1 0.2 copy.42
  104.4 1.8 %convolution_convert_fusion.1 = bf16[2048,768]{1,0:T(8,128)(2,1)S(1)} fusion(bf16[384,2048]{0,1:T(8,128)(2,1)S(1)} %bitcast.108, bf16[384,128]{0,1:T(8,128)(2,1)S(1)} %copy-done.10, bf16[384,128]{0,1:T(8,128)(2,1)S(1)} %fusion.10, bf16[384,512]{0,1:T(8,128)(2,1)S(1)} %bitcast.104), kind=kOutput, calls=%fused_computation.14 | convolution fusion | flops 1211301888 | bytes 5308416 | tf_op jit(solution)/shard_map/dot_general | solution.py:20
  106.4 0.2 slice-done.1
  106.7 1.4 convolution_convert_fusion.2
  108.1 0.3 copy.43
  108.4 0.8 copy.52
  109.2 1.8 %fusion.22 = f32[2048,768]{1,0:T(8,128)S(1)} fusion(bf16[384,2048]{0,1:T(8,128)(2,1)S(1)} %bitcast.98, bf16[384,128]{0,1:T(8,128)(2,1)S(1)} %copy-done.10, bf16[384,128]{0,1:T(8,128)(2,1)S(1)} %fusion.10, bf16[384,512]{0,1:T(8,128)(2,1)S(1)} %bitcast.105), kind=kOutput, calls=%fused_computation.59 | convolution fusion | flops 1209729024 | bytes 8454144 | tf_op jit(solution)/shard_map/dot_general | solution.py:20
  111.0 0.9 collective-permute-done.9
  112.0 2.3 %add_convert_fusion = bf16[2048,768]{1,0:T(8,128)(2,1)} fusion(f32[2048,768]{1,0:T(8,128)S(1)} %fusion.22, bf16[2048,768]{1,0:T(8,128)(2,1)S(1)} %collective-permute-done.9), kind=kLoop, calls=%fused_computation.12 | loop fusion | flops 4718592 | bytes 12582912 | tf_op jit(solution)/shard_map/convert_element_type | solution.py:131
  114.4 3.3 %select_bitcast_fusion.1 = (bf16[8,2,1,128,768]{4,3,1,0,2:T(8,128)(2,1)S(1)}, bf16[8,2,1,128,768]{4,3,1,0,2:T(8,128)(2,1)S(1)}) fusion(bf16[8,2,128,768]{3,2,1,0:T(8,128)(2,1)} %bitcast_dynamic-update-slice_fusion, bf16[8,2,128,768]{3,2,1,0:T(8,128)(2,1)} %collective-permute-done.8, pred[]{:T(512)S(6)} %eq.17), kind=kLoop, calls=%fused_computation.17 | loop fusion | flops 3145728 | bytes 12582913 | tf_op jit(solution)/shard_map/stack | solution.py:85
  117.6 0.6 maximum_bitcast_fusion
  118.2 0.6 copy.44
  118.9 3.0 %convolution_convert_fusion = bf16[384,4096]{1,0:T(8,128)(2,1)S(1)} fusion(bf16[4096,768]{1,0:T(8,128)(2,1)S(1)} %bitcast.99, bf16[384,128]{0,1:T(8,128)(2,1)S(1)} %copy-done.10, bf16[384,128]{0,1:T(8,128)(2,1)S(1)} %fusion.10, bf16[384,512]{0,1:T(8,128)(2,1)S(1)} %bitcast.106), kind=kOutput, calls=%fused_computation.13 | convolution fusion | flops 2419261440 | bytes 10027008 | tf_op jit(solution)/shard_map/dot_general | solution.py:14
  121.8 2.0 %copy.51 = bf16[48,8,8,512]{3,2,0,1:T(8,128)(2,1)} copy(bf16[48,8,8,512]{3,2,1,0:T(8,128)(2,1)S(1)} %bitcast.102) | data formatting | bytes 6291456 | tf_op jit(solution)/shard_map/reshape | solution.py:138
  123.8 6.7 %all-to-all-start = ((bf16[8,384,512]{2,1,0:T(8,128)(2,1)}), bf16[8,384,512]{2,1,0:T(8,128)(2,1)S(1)}, u32[]{:S(2)}, u32[]{:S(2)}) async-start(bf16[8,384,512]{2,1,0:T(8,128)(2,1)} %bitcast.92), calls=%async_computation | async-start | bytes 6291456 | tf_op jit(solution)/shard_map/all_to_all | solution.py:139
  130.5 26.9 %reduce-scatter.2.cloned.1.call-done = bf16[256,768]{1,0:T(8,128)(2,1)} async-done(((bf16[2048,768]{1,0:T(8,128)(2,1)}), bf16[256,768]{1,0:T(8,128)(2,1)}) %reduce-scatter.2.cloned.1.call-update) | async-done | bytes 393232 | tf_op jit(solution)/shard_map/reduce_scatter | solution.py:132
  157.4 1.7 dynamic-slice_bitcast_fusion.2
  159.1 1.3 collective-permute-start.10
  160.4 9.4 %all-to-all-done = bf16[8,384,512]{2,1,0:T(8,128)(2,1)S(1)} async-done(((bf16[8,384,512]{2,1,0:T(8,128)(2,1)}), bf16[8,384,512]{2,1,0:T(8,128)(2,1)S(1)}, u32[]{:S(2)}, u32[]{:S(2)}) %all-to-all-start) | async-done | bytes 3145760 | tf_op jit(solution)/shard_map/all_to_all | solution.py:139
  169.8 1.3 reduce_sum.34
  171.1 1.0 fusion.16
  172.1 0.7 fusion.24
  172.8 0.7 slice.42
  (54 shorter events, 1.0 us)
Async XLA Ops:
  7.2 150.2 %reduce-scatter.2.cloned.1.call-start = ((), (), s32[]{:S(2)}) async-start(), calls=%async_computation.2 | async-start | bytes 3538944 | tf_op jit(solution)/shard_map/reduce_scatter | solution.py:132
  9.7 5.5 %collective-permute-start = (bf16[128,768]{1,0:T(8,128)(2,1)S(1)}, bf16[128,768]{1,0:T(8,128)(2,1)S(1)}, u32[]{:S(2)}, u32[]{:S(2)}) collective-permute-start(bf16[128,768]{1,0:T(8,128)(2,1)S(1)} %constant_dynamic-update-slice_fusion), channel_id=1, source_target_pairs={{0,128},{128,0},{1,129},{129,1},{2,130},{130,2},{3,131},{131,3},{4... | collective-permute-start | bytes 589832 | tf_op jit(solution)/shard_map/ppermute | solution.py:68
  15.2 14.8 %collective-permute-start.1 = (bf16[2,128,768]{2,1,0:T(8,128)(2,1)S(1)}, bf16[2,128,768]{2,1,0:T(8,128)(2,1)S(1)}, u32[]{:S(2)}, u32[]{:S(2)}) collective-permute-start(bf16[2,128,768]{2,1,0:T(8,128)(2,1)S(1)} %pad_maximum_fusion.1), channel_id=1, source_target_pairs={{0,16},{16,32},{32,48},{48,64},{64,80},{80,96},{96,112},{112,0},{1... | collective-permute-start | bytes 1179656 | tf_op jit(solution)/shard_map/ppermute | solution.py:77
  18.1 11.9 %collective-permute-start.2 = (bf16[2,128,768]{2,1,0:T(8,128)(2,1)S(1)}, bf16[2,128,768]{2,1,0:T(8,128)(2,1)S(1)}, u32[]{:S(2)}, u32[]{:S(2)}) collective-permute-start(bf16[2,128,768]{2,1,0:T(8,128)(2,1)S(1)} %pad_maximum_fusion.1), channel_id=1, source_target_pairs={{0,112},{16,0},{32,16},{48,32},{64,48},{80,64},{96,80},{112,96},{1... | collective-permute-start | bytes 1179656 | tf_op jit(solution)/shard_map/ppermute | solution.py:80
  24.1 38.9 %copy-start.6 = (bf16[384,512]{1,0:T(8,128)(2,1)S(1)}, bf16[384,512]{1,0:T(8,128)(2,1)}, u32[]{:S(2)}) copy-start(bf16[384,512]{1,0:T(8,128)(2,1)} %param.15) | copy-start | bytes 1179652
  30.1 9.8 %collective-permute-start.3 = (bf16[2,128,768]{2,1,0:T(8,128)(2,1)S(1)}, bf16[2,128,768]{2,1,0:T(8,128)(2,1)S(1)}, u32[]{:S(2)}, u32[]{:S(2)}) collective-permute-start(bf16[2,128,768]{2,1,0:T(8,128)(2,1)S(1)} %collective-permute-done.1), channel_id=1, source_target_pairs={{0,16},{16,32},{32,48},{48,64},{64,80},{80,96},{96,112},{112,0},{1... | collective-permute-start | bytes 1179656 | tf_op jit(solution)/shard_map/ppermute | solution.py:77
  30.1 9.8 %collective-permute-start.4 = (bf16[2,128,768]{2,1,0:T(8,128)(2,1)S(1)}, bf16[2,128,768]{2,1,0:T(8,128)(2,1)S(1)}, u32[]{:S(2)}, u32[]{:S(2)}) collective-permute-start(bf16[2,128,768]{2,1,0:T(8,128)(2,1)S(1)} %collective-permute-done.2), channel_id=1, source_target_pairs={{0,112},{16,0},{32,16},{48,32},{64,48},{80,64},{96,80},{112,96},{1... | collective-permute-start | bytes 1179656 | tf_op jit(solution)/shard_map/ppermute | solution.py:80
  39.8 8.9 %collective-permute-start.5 = (bf16[2,128,768]{2,1,0:T(8,128)(2,1)S(1)}, bf16[2,128,768]{2,1,0:T(8,128)(2,1)S(1)}, u32[]{:S(2)}, u32[]{:S(2)}) collective-permute-start(bf16[2,128,768]{2,1,0:T(8,128)(2,1)S(1)} %collective-permute-done.3), channel_id=1, source_target_pairs={{0,16},{16,32},{32,48},{48,64},{64,80},{80,96},{96,112},{112,0},{1... | collective-permute-start | bytes 1179656 | tf_op jit(solution)/shard_map/ppermute | solution.py:77
  39.8 9.7 %collective-permute-start.6 = (bf16[2,128,768]{2,1,0:T(8,128)(2,1)S(1)}, bf16[2,128,768]{2,1,0:T(8,128)(2,1)S(1)}, u32[]{:S(2)}, u32[]{:S(2)}) collective-permute-start(bf16[2,128,768]{2,1,0:T(8,128)(2,1)S(1)} %collective-permute-done.4), channel_id=1, source_target_pairs={{0,112},{16,0},{32,16},{48,32},{64,48},{80,64},{96,80},{112,96},{1... | collective-permute-start | bytes 1179656 | tf_op jit(solution)/shard_map/ppermute | solution.py:80
  48.8 7.8 %collective-permute-start.7 = (bf16[2,128,768]{2,1,0:T(8,128)(2,1)S(1)}, bf16[2,128,768]{2,1,0:T(8,128)(2,1)S(1)}, u32[]{:S(2)}, u32[]{:S(2)}) collective-permute-start(bf16[2,128,768]{2,1,0:T(8,128)(2,1)S(1)} %collective-permute-done.5), channel_id=1, source_target_pairs={{0,16},{16,32},{32,48},{48,64},{64,80},{80,96},{96,112},{112,0},{1... | collective-permute-start | bytes 1179656 | tf_op jit(solution)/shard_map/ppermute | solution.py:77
  57.4 15.6 %collective-permute-start.8 = (bf16[8,2,128,768]{3,2,1,0:T(8,128)(2,1)}, bf16[8,2,128,768]{3,2,1,0:T(8,128)(2,1)}, u32[]{:S(2)}, u32[]{:S(2)}) collective-permute-start(bf16[8,2,128,768]{3,2,1,0:T(8,128)(2,1)} %bitcast_dynamic-update-slice_fusion), channel_id=1, source_target_pairs={{0,8},{8,0},{1,9},{9,1},{2,10},{10,2},{3,11},{11,3},{4,12},{12,4},... | collective-permute-start | bytes 9437192 | tf_op jit(solution)/shard_map/ppermute | solution.py:82
  72.8 4.5 %copy-start = (bf16[384,8,2,1,128]{0,4,2,1,3:T(8,128)(2,1)}, bf16[384,8,2,1,128]{0,4,2,1,3:T(8,128)(2,1)S(1)}, u32[]{:S(2)}) copy-start(bf16[384,8,2,1,128]{0,4,2,1,3:T(8,128)(2,1)S(1)} %copy.38) | copy-start | bytes 4718596
  73.0 4.3 %copy-start.4 = (bf16[384,8,2,1,128]{0,4,2,1,3:T(8,128)(2,1)}, bf16[384,8,2,1,128]{0,4,2,1,3:T(8,128)(2,1)S(1)}, u32[]{:S(2)}) copy-start(bf16[384,8,2,1,128]{0,4,2,1,3:T(8,128)(2,1)S(1)} %copy.37) | copy-start | bytes 4718596
  77.3 4.4 %copy-start.3 = (pred[192,8,4,384]{3,1,2,0:T(8,128)(4,1)S(1)}, pred[192,8,4,384]{3,1,2,0:T(8,128)(4,1)}, u32[]{:S(2)}) copy-start(pred[192,8,4,384]{3,1,2,0:T(8,128)(4,1)} %copy.47) | copy-start | bytes 7077892
  81.7 2.9 %copy-start.7 = (bf16[384,1,4,128]{3,0,2,1:T(8,128)(2,1)}, bf16[384,1,4,128]{3,0,2,1:T(8,128)(2,1)S(1)}, u32[]{:S(2)}) copy-start(bf16[384,1,4,128]{3,0,2,1:T(8,128)(2,1)S(1)} %copy.39) | copy-start | bytes 1179652
  84.6 1.4 copy-start.11
  84.6 1.3 copy-start.13
  88.3 2.1 %copy-start.2 = (bf16[1536,1536]{0,1:T(8,128)(2,1)}, bf16[1536,1536]{0,1:T(8,128)(2,1)S(1)}, u32[]{:S(2)}) copy-start(bf16[1536,1536]{0,1:T(8,128)(2,1)S(1)} %get-tuple-element.34) | copy-start | bytes 14155780
  91.5 6.6 %copy-start.8 = (bf16[384,1,4,128]{3,0,2,1:T(8,128)(2,1)S(1)}, bf16[384,1,4,128]{3,0,2,1:T(8,128)(2,1)}, u32[]{:S(2)}) copy-start(bf16[384,1,4,128]{3,0,2,1:T(8,128)(2,1)} %copy-done.7) | copy-start | bytes 1179652
  99.9 4.5 %copy-start.5 = (bf16[384,8,2,1,128]{0,4,2,1,3:T(8,128)(2,1)S(1)}, bf16[384,8,2,1,128]{0,4,2,1,3:T(8,128)(2,1)}, u32[]{:S(2)}) copy-start(bf16[384,8,2,1,128]{0,4,2,1,3:T(8,128)(2,1)} %copy-done.4) | copy-start | bytes 4718596
  99.9 4.5 %copy-start.10 = (bf16[384,128]{0,1:T(8,128)(2,1)S(1)}, bf16[384,128]{0,1:T(8,128)(2,1)}, u32[]{:S(2)}) copy-start(bf16[384,128]{0,1:T(8,128)(2,1)} %fusion.13) | copy-start | bytes 294916
  104.1 2.2 %slice-start = ((s8[4718592]{0:T(1024)(128)(4,1)}), s8[524288]{0:T(1024)(128)(4,1)S(1)}, s32[]{:S(2)}) async-start(s8[4718592]{0:T(1024)(128)(4,1)} %bitcast.100), calls=%async_computation.3 | async-start | bytes 1048576
  104.4 2.2 %slice-start.1 = ((s8[4718592]{0:T(1024)(128)(4,1)}), s8[4194304]{0:T(1024)(128)(4,1)S(1)}, s32[]{:S(2)}) async-start(s8[4718592]{0:T(1024)(128)(4,1)} %bitcast.100), calls=%async_computation.4 | async-start | bytes 8388608
  104.4 2.2 %copy-start.12 = (bf16[384,128]{1,0:T(8,128)(2,1)S(1)}, bf16[384,128]{1,0:T(8,128)(2,1)}, u32[]{:S(2)}) copy-start(bf16[384,128]{1,0:T(8,128)(2,1)} %get-tuple-element.52) | copy-start | bytes 294916
  104.4 2.3 %copy-start.14 = (bf16[1,1152,128]{2,1,0:T(8,128)(2,1)S(1)}, bf16[1,1152,128]{2,1,0:T(8,128)(2,1)}, u32[]{:S(2)}) copy-start(bf16[1,1152,128]{2,1,0:T(8,128)(2,1)} %param.14) | copy-start | bytes 884740
  106.2 3.0 %copy-start.1 = (bf16[384,8,2,1,128]{0,4,2,1,3:T(8,128)(2,1)S(1)}, bf16[384,8,2,1,128]{0,4,2,1,3:T(8,128)(2,1)}, u32[]{:S(2)}) copy-start(bf16[384,8,2,1,128]{0,4,2,1,3:T(8,128)(2,1)} %copy-done) | copy-start | bytes 4718596
  106.2 5.7 %collective-permute-start.9 = (bf16[2048,768]{1,0:T(8,128)(2,1)S(1)}, bf16[2048,768]{1,0:T(8,128)(2,1)S(1)}, u32[]{:S(2)}, u32[]{:S(2)}) collective-permute-start(bf16[2048,768]{1,0:T(8,128)(2,1)S(1)} %convolution_convert_fusion.1), channel_id=1, source_target_pairs={{0,8},{8,0},{1,9},{9,1},{2,10},{10,2},{3,11},{11,3},{4,12},{12,4},... | collective-permute-start | bytes 9437192 | tf_op jit(solution)/shard_map/ppermute | solution.py:128
  123.8 46.0 %all-to-all-start = ((bf16[8,384,512]{2,1,0:T(8,128)(2,1)}), bf16[8,384,512]{2,1,0:T(8,128)(2,1)S(1)}, u32[]{:S(2)}, u32[]{:S(2)}) async-start(bf16[8,384,512]{2,1,0:T(8,128)(2,1)} %bitcast.92), calls=%async_computation | async-start | bytes 6291456 | tf_op jit(solution)/shard_map/all_to_all | solution.py:139
  157.4 13.8 %copy-start.9 = (bf16[256,768]{1,0:T(8,128)(2,1)S(1)}, bf16[256,768]{1,0:T(8,128)(2,1)}, u32[]{:S(2)}) copy-start(bf16[256,768]{1,0:T(8,128)(2,1)} %reduce-scatter.2.cloned.1.call-done) | copy-start | bytes 1179652
  159.1 12.1 %collective-permute-start.10 = (bf16[128,768]{1,0:T(8,128)(2,1)}, bf16[128,768]{1,0:T(8,128)(2,1)}, u32[]{:S(2)}, u32[]{:S(2)}) collective-permute-start(bf16[128,768]{1,0:T(8,128)(2,1)} %dynamic-slice_bitcast_fusion.2), channel_id=1, source_target_pairs={{0,128},{128,0},{1,129},{129,1},{2,130},{130,2},{3,131},{131,3},{4... | collective-permute-start | bytes 589832 | tf_op jit(solution)/shard_map/ppermute | solution.py:136
Sparse Core Ops, SparseCore 0:
  114.5 42.8 reduce-scatter.1

commit v10 on v9

--- a/solution.py
+++ b/solution.py
@@ -131,11 +131,13 @@
     chip_sum = (part_own + from_peer.astype(jnp.float32)).astype(jnp.bfloat16)
     ring_sum = lax.psum_scatter(chip_sum, "z", scatter_dimension=0, tiled=True)
     ring_sum = ring_sum.reshape(2, rows, -1)
+    from_x = lax.ppermute(ring_sum, "xl", SWAP)
     keep = lax.dynamic_index_in_dim(ring_sum, x_pos, 0, False)
-    give = lax.dynamic_index_in_dim(ring_sum, 1 - x_pos, 0, False)
-    summed = keep.astype(jnp.float32) + lax.ppermute(give, "xl", SWAP).astype(jnp.float32)
-    input_term = contract_last(grads_cat, full_w).astype(jnp.bfloat16)
-    input_term = input_term.reshape(tokens_dev, tp_count, -1).transpose(1, 0, 2)
+    summed = keep.astype(jnp.float32) + lax.dynamic_index_in_dim(from_x, x_pos, 0, False).astype(jnp.float32)
+    by_target = full_w.reshape(tp_count, -1, full_w.shape[1])
+    input_term = jnp.einsum(
+        "tk,cjk->ctj", grads_cat, by_target, preferred_element_type=jnp.float32
+    ).astype(jnp.bfloat16)
     gathered = lax.all_to_all(input_term, "tp", 0, 0, tiled=True)
     grad_in = jnp.sum(gathered.astype(jnp.float32), axis=0).astype(jnp.bfloat16)
     summed = summed * (tokens_dev * lax.axis_size(BLK)) ** (-0.5)

time: 181 us -> 185 us (1.022)
  waiting for transfers between devices: 62.3 us -> 66.7 us
  local copies, waits for them, and re-layouts: 29.8 us -> 27.4 us
  matrix products: 28 us -> 29.9 us
    dot_general x0 -> x1, matrix products: none -> 4.86 us  [local(): jnp.einsum('tk,cjk->ctj', grads_cat, by_target, preferred_element_type=jn...]
    dot_general x3 -> x2, matrix products: 8.12 us -> 5.16 us  [contract_last(): lax.dot_general(left, right, (((1,), (1,)), ((), ())), preferred_element_...]
    ppermute x1, waiting for transfers between devices: 0.01 us -> 2.66 us  [local(): from_x = lax.ppermute(ring_sum, 'xl', SWAP)]
    reshape x1 -> x0, local copies, waits for them, and re-layouts: 1.97 us -> none  [local(): input_term = input_term.reshape(tokens_dev, tp_count, -1).transpose(1, 0, 2)]
  transfers between devices with their start and end apart: 13 -> 13, of which waited for: 8 -> 9; matrix products, arithmetic and copies ran while one was open for 19% -> 18% of each run, Pallas kernels for 0% -> 0%
where the time goes in v10:
time: 185 us; the launch traced here: 184 us
  waiting for transfers between devices  66.7 us (36%)
  matrix products  29.9 us (16%)
  starting transfers between devices  27.5 us (15%)
  local copies, waits for them, and re-layouts  27.4 us (15%)
  other arithmetic  17 us (9%)
  between operations  15.1 us (8%)
    reduce_scatter x1, waiting for transfers between devices, local(): ring_sum = lax.psum_scatter(chip_sum, 'z', scatter_dimension=0, tiled=True)  26.9 us
    ppermute x4, waiting for transfers between devices, gather_rows(): fwd = lax.ppermute(fwd, 'z', ahead)  21.6 us
    unnamed x40, local copies, waits for them, and re-layouts  12.4 us
    all_to_all x1, waiting for transfers between devices, local(): gathered = lax.all_to_all(input_term, 'tp', 0, 0, tiled=True)  11.2 us
    ppermute x3, starting transfers between devices, gather_rows(): bwd = lax.ppermute(bwd, 'z', behind)  9.38 us
    all_to_all x1, starting transfers between devices, local(): gathered = lax.all_to_all(input_term, 'tp', 0, 0, tiled=True)  6.66 us
    convert_element_type x1, other arithmetic, head_pass(): (probs_wide * (grad_probs - row_dot) * factor).astype(jnp.bfloat16)  6.58 us
    dot_general x4, matrix products, contract_first(): lax.dot_general(left, right, (((0,), (0,)), ((), ())), preferred_element_...  6.52 us
  transfers between devices with their start and end apart: 13, of which 9 were waited for; matrix products, arithmetic and copies ran while one was open for 18% of the time, Pallas kernels for 0%

profile of v10, /device:TPU:1, one launch (start us, length us, event | category | flops | bytes accessed | tf_op | source)
XLA Modules:
  0.0 183.7 jit_solution(12186014240572495690)
XLA Ops:
  7.2 0.9 constant_dynamic-update-slice_fusion.2
  8.1 0.8 constant_dynamic-update-slice_fusion.1
  8.9 0.8 constant_dynamic-update-slice_fusion
  9.7 2.1 %collective-permute-start = (bf16[128,768]{1,0:T(8,128)(2,1)S(1)}, bf16[128,768]{1,0:T(8,128)(2,1)S(1)}, u32[]{:S(2)}, u32[]{:S(2)}) collective-permute-start(bf16[128,768]{1,0:T(8,128)(2,1)S(1)} %constant_dynamic-update-slice_fusion), channel_id=1, source_target_pairs={{0,128},{128,0},{1,129},{129,1},{2,130},{130,2},{3,131},{131,3},{4... | collective-permute-start | bytes 589832 | tf_op jit(solution)/shard_map/ppermute | solution.py:68
  11.8 3.4 %collective-permute-done = bf16[128,768]{1,0:T(8,128)(2,1)S(1)} collective-permute-done((bf16[128,768]{1,0:T(8,128)(2,1)S(1)}, bf16[128,768]{1,0:T(8,128)(2,1)S(1)}, u32[]{:S(2)}, u32[]{:S(2)}) %collective-permute-start) | collective-permute-done | bytes 196640 | tf_op jit(solution)/shard_map/ppermute | solution.py:68
  15.2 2.9 %collective-permute-start.1 = (bf16[2,128,768]{2,1,0:T(8,128)(2,1)S(1)}, bf16[2,128,768]{2,1,0:T(8,128)(2,1)S(1)}, u32[]{:S(2)}, u32[]{:S(2)}) collective-permute-start(bf16[2,128,768]{2,1,0:T(8,128)(2,1)S(1)} %pad_maximum_fusion.1), channel_id=1, source_target_pairs={{0,16},{16,32},{32,48},{48,64},{64,80},{80,96},{96,112},{112,0},{1... | collective-permute-start | bytes 1179656 | tf_op jit(solution)/shard_map/ppermute | solution.py:77
  18.1 4.0 %collective-permute-start.2 = (bf16[2,128,768]{2,1,0:T(8,128)(2,1)S(1)}, bf16[2,128,768]{2,1,0:T(8,128)(2,1)S(1)}, u32[]{:S(2)}, u32[]{:S(2)}) collective-permute-start(bf16[2,128,768]{2,1,0:T(8,128)(2,1)S(1)} %pad_maximum_fusion.1), channel_id=1, source_target_pairs={{0,112},{16,0},{32,16},{48,32},{64,48},{80,64},{96,80},{112,96},{1... | collective-permute-start | bytes 1179656 | tf_op jit(solution)/shard_map/ppermute | solution.py:80
  22.2 2.0 %broadcast_in_dim.85 = bf16[8,2,128,768]{3,2,1,0:T(8,128)(2,1)} broadcast(bf16[]{:T(256)} %constant.121.clone.1), dimensions={} | broadcast | bytes 3145730 | tf_op jit(solution)/shard_map/broadcast_in_dim | solution.py:72
  24.1 0.8 bitcast_dynamic-update-slice_fusion.7
  25.0 5.1 %collective-permute-done.1 = bf16[2,128,768]{2,1,0:T(8,128)(2,1)S(1)} collective-permute-done((bf16[2,128,768]{2,1,0:T(8,128)(2,1)S(1)}, bf16[2,128,768]{2,1,0:T(8,128)(2,1)S(1)}, u32[]{:S(2)}, u32[]{:S(2)}) %collective-permute-start.1) | collective-permute-done | bytes 393248 | tf_op jit(solution)/shard_map/ppermute | solution.py:77
  30.1 2.7 %collective-permute-start.4 = (bf16[2,128,768]{2,1,0:T(8,128)(2,1)S(1)}, bf16[2,128,768]{2,1,0:T(8,128)(2,1)S(1)}, u32[]{:S(2)}, u32[]{:S(2)}) collective-permute-start(bf16[2,128,768]{2,1,0:T(8,128)(2,1)S(1)} %collective-permute-done.2), channel_id=1, source_target_pairs={{0,112},{16,0},{32,16},{48,32},{64,48},{80,64},{96,80},{112,96},{1... | collective-permute-start | bytes 1179656 | tf_op jit(solution)/shard_map/ppermute | solution.py:80
  32.7 0.8 bitcast_dynamic-update-slice_fusion.6
  33.5 0.8 bitcast_dynamic-update-slice_fusion.5
  34.3 5.5 %collective-permute-done.3 = bf16[2,128,768]{2,1,0:T(8,128)(2,1)S(1)} collective-permute-done((bf16[2,128,768]{2,1,0:T(8,128)(2,1)S(1)}, bf16[2,128,768]{2,1,0:T(8,128)(2,1)S(1)}, u32[]{:S(2)}, u32[]{:S(2)}) %collective-permute-start.3) | collective-permute-done | bytes 393248 | tf_op jit(solution)/shard_map/ppermute | solution.py:77
  39.8 2.7 %collective-permute-start.6 = (bf16[2,128,768]{2,1,0:T(8,128)(2,1)S(1)}, bf16[2,128,768]{2,1,0:T(8,128)(2,1)S(1)}, u32[]{:S(2)}, u32[]{:S(2)}) collective-permute-start(bf16[2,128,768]{2,1,0:T(8,128)(2,1)S(1)} %collective-permute-done.4), channel_id=1, source_target_pairs={{0,112},{16,0},{32,16},{48,32},{64,48},{80,64},{96,80},{112,96},{1... | collective-permute-start | bytes 1179656 | tf_op jit(solution)/shard_map/ppermute | solution.py:80
  42.5 0.8 bitcast_dynamic-update-slice_fusion.4
  43.3 0.8 bitcast_dynamic-update-slice_fusion.3
  44.1 4.7 %collective-permute-done.5 = bf16[2,128,768]{2,1,0:T(8,128)(2,1)S(1)} collective-permute-done((bf16[2,128,768]{2,1,0:T(8,128)(2,1)S(1)}, bf16[2,128,768]{2,1,0:T(8,128)(2,1)S(1)}, u32[]{:S(2)}, u32[]{:S(2)}) %collective-permute-start.5) | collective-permute-done | bytes 393248 | tf_op jit(solution)/shard_map/ppermute | solution.py:77
  48.8 0.8 bitcast_dynamic-update-slice_fusion.2
  49.5 0.8 bitcast_dynamic-update-slice_fusion.1
  50.3 6.3 %collective-permute-done.7 = bf16[2,128,768]{2,1,0:T(8,128)(2,1)S(1)} collective-permute-done((bf16[2,128,768]{2,1,0:T(8,128)(2,1)S(1)}, bf16[2,128,768]{2,1,0:T(8,128)(2,1)S(1)}, u32[]{:S(2)}, u32[]{:S(2)}) %collective-permute-start.7) | collective-permute-done | bytes 393248 | tf_op jit(solution)/shard_map/ppermute | solution.py:77
  56.6 0.8 bitcast_dynamic-update-slice_fusion
  57.4 5.0 %collective-permute-start.8 = (bf16[8,2,128,768]{3,2,1,0:T(8,128)(2,1)}, bf16[8,2,128,768]{3,2,1,0:T(8,128)(2,1)}, u32[]{:S(2)}, u32[]{:S(2)}) collective-permute-start(bf16[8,2,128,768]{3,2,1,0:T(8,128)(2,1)} %bitcast_dynamic-update-slice_fusion), channel_id=1, source_target_pairs={{0,8},{8,0},{1,9},{9,1},{2,10},{10,2},{3,11},{11,3},{4,12},{12,4},... | collective-permute-start | bytes 9437192 | tf_op jit(solution)/shard_map/ppermute | solution.py:82
  63.0 0.2 copy.47
  63.2 0.2 copy.48
  63.5 0.3 pad_add_fusion
  63.9 2.2 %broadcast_in_dim.83 = pred[4,384,1536]{1,0,2:T(4,128)(4,1)S(1)} broadcast(pred[384,1536]{0,1:T(8,128)(4,1)S(1)} %pad_add_fusion), dimensions={1,2} | broadcast | bytes 2949120 | tf_op jit(solution)/shard_map/while/body/eval_jaxpr/jit(_where)/broadcast_in_dim | solution.py:39
  66.1 2.6 %copy.55 = pred[192,8,4,384]{3,1,2,0:T(8,128)(4,1)} copy(pred[192,8,4,384]{3,2,1,0:T(4,128)(4,1)S(1)} %bitcast.96) | data formatting | bytes 4718592
  68.7 3.6 %copy.43 = bf16[384,4096]{0,1:T(8,128)(2,1)S(1)} copy(bf16[384,4096]{1,0:T(8,128)(2,1)} %param.8) | data formatting | bytes 6291456 | tf_op args[0]
  72.3 0.3 dynamic-slice_bitcast_fusion
  72.6 0.2 copy.45
  73.0 4.2 %fusion.26 = f32[384,768]{1,0:T(8,128)S(1)} fusion(bf16[384,2048]{0,1:T(8,128)(2,1)S(1)} %bitcast.106, bf16[2048,768]{1,0:T(8,128)(2,1)} %bitcast.17), kind=kOutput, calls=%fused_computation.62 | convolution fusion | flops 1207959552 | bytes 5898240 | tf_op jit(solution)/shard_map/dot_general | solution.py:105
  77.3 3.5 %fusion.5 = bf16[384,768]{1,0:T(8,128)(2,1)S(1)} fusion(f32[384,768]{1,0:T(8,128)S(1)} %fusion.26, bf16[384,2048]{0,1:T(8,128)(2,1)S(1)} %bitcast.98, bf16[2048,768]{1,0:T(8,128)(2,1)} %bitcast.16), kind=kOutput, calls=%fused_computation.23 | convolution fusion | flops 1208549376 | bytes 6488064 | tf_op jit(solution)/shard_map/dot_general | solution.py:104
  80.8 0.7 fusion.23
  81.7 2.9 %fusion.25 = (f32[1536]{0:T(1024)S(1)}, f32[1536,1536]{0,1:T(8,128)S(1)}) fusion(pred[1536,1536]{0,1:T(8,128)(4,1)S(1)} %bitcast.102, bf16[1536,128]{1,0:T(8,128)(2,1)S(1)} %bitcast.114, bf16[384,128]{1,0:T(8,128)(2,1)} %get-tuple-element.56, bf16[1152,128]{1,0:T(8,128)(2,1)} %bitcast.120), kind=kOutput, calls=%fused_computation.61 | convolution fusion | flops 611842560 | bytes 12589056 | tf_op jit(solution)/shard_map/while/body/eval_jaxpr/dot_general | solution.py:14
  84.6 1.3 fusion.4
  86.0 2.3 %fusion.1 = (f32[1536]{0:T(1024)S(1)}, bf16[1536,1536]{0,1:T(8,128)(2,1)S(1)}, f32[1536,1536]{1,0:T(8,128)S(1)}) fusion(f32[1536]{0:T(1024)S(1)} %fusion.4, f32[1536,1536]{0,1:T(8,128)S(1)} %get-tuple-element.63, f32[1536]{0:T(1024)S(1)} %get-tuple-element.62, bf16[1536,128]{1,0:T(8,128)(2,1)S(1)} %bitcast.112, bf16[384,128]{1,0:T(8,128)(2,1)S(1)} %copy-done.10, ...), kind=kOutput, calls=%fused_computation.4 | convolution fusion | flops 618920448 | bytes 24397824 | tf_op jit(solution)/shard_map/while/body/eval_jaxpr/dot_general | solution.py:14
  88.3 2.1 %copy-done.2 = bf16[1536,1536]{0,1:T(8,128)(2,1)} copy-done((bf16[1536,1536]{0,1:T(8,128)(2,1)}, bf16[1536,1536]{0,1:T(8,128)(2,1)S(1)}, u32[]{:S(2)}) %copy-start.2) | copy-done | bytes 4718616
  90.4 1.2 fusion.13
  91.6 6.6 %fusion.3 = bf16[1536,1536]{0,1:T(8,128)(2,1)} fusion(bf16[1536,1536]{0,1:T(8,128)(2,1)} %copy-done.2, f32[1536,1536]{1,0:T(8,128)S(1)} %get-tuple-element.64, f32[1536]{0:T(1024)S(1)} %get-tuple-element.50), kind=kLoop, calls=%fused_computation.6 | loop fusion | flops 11796480 | bytes 18880512 | tf_op jit(solution)/shard_map/while/body/eval_jaxpr/convert_element_type | solution.py:48
  98.2 1.8 fusion.10
  100.0 4.2 %convolution_convert_fusion.2 = bf16[1536,128]{1,0:T(8,128)(2,1)S(1)} fusion(bf16[1536,1536]{0,1:T(8,128)(2,1)} %fusion.3, bf16[384,128]{1,0:T(8,128)(2,1)} %get-tuple-element.56, bf16[1152,128]{1,0:T(8,128)(2,1)} %bitcast.121), kind=kOutput, calls=%fused_computation.18 | convolution fusion | flops 604962816 | bytes 5505024 | tf_op jit(solution)/shard_map/while/body/eval_jaxpr/dot_general | solution.py:49
  104.5 0.3 copy.49
  104.9 1.8 convolution_convert_fusion
  107.0 1.4 convolution_convert_fusion.1
  108.5 0.3 copy.52
  108.8 0.8 copy.60
  109.6 1.8 fusion.22
  111.4 1.0 collective-permute-done.9
  112.4 2.3 %add_convert_fusion = bf16[2048,768]{1,0:T(8,128)(2,1)} fusion(f32[2048,768]{1,0:T(8,128)S(1)} %fusion.22, bf16[2048,768]{1,0:T(8,128)(2,1)S(1)} %collective-permute-done.9), kind=kLoop, calls=%fused_computation.12 | loop fusion | flops 4718592 | bytes 12582912 | tf_op jit(solution)/shard_map/convert_element_type | solution.py:131
  114.8 3.3 %select_bitcast_fusion.1 = (bf16[8,2,1,128,768]{4,3,1,0,2:T(8,128)(2,1)S(1)}, bf16[8,2,1,128,768]{4,3,1,0,2:T(8,128)(2,1)S(1)}) fusion(bf16[8,2,128,768]{3,2,1,0:T(8,128)(2,1)} %bitcast_dynamic-update-slice_fusion, bf16[8,2,128,768]{3,2,1,0:T(8,128)(2,1)} %collective-permute-done.8, pred[]{:T(512)S(6)} %eq.17), kind=kLoop, calls=%fused_computation.16 | loop fusion | flops 3145728 | bytes 12582913 | tf_op jit(solution)/shard_map/stack | solution.py:85
  118.1 0.6 maximum_bitcast_fusion
  118.6 0.6 copy.53
  119.3 4.9 %convert_bitcast_fusion = bf16[8,384,512]{1,2,0:T(8,128)(2,1)} fusion(bf16[8,512,768]{2,1,0:T(8,128)(2,1)S(1)} %bitcast.97, bf16[384,128]{1,0:T(8,128)(2,1)S(1)} %copy.51, bf16[384,128]{1,0:T(8,128)(2,1)S(1)} %copy.50, bf16[384,512]{1,0:T(8,128)(2,1)S(1)} %bitcast.105), kind=kOutput, calls=%fused_computation.14 | convolution fusion | flops 2419261440 | bytes 10027008 | tf_op jit(solution)/shard_map/tk,cjk->ctj/dot_general | solution.py:138
  124.2 6.7 %all-to-all-start = ((bf16[8,384,512]{1,2,0:T(8,128)(2,1)}), bf16[8,384,512]{1,2,0:T(8,128)(2,1)S(1)}, u32[]{:S(2)}, u32[]{:S(2)}) async-start(bf16[8,384,512]{1,2,0:T(8,128)(2,1)} %convert_bitcast_fusion), calls=%async_computation | async-start | bytes 6291456 | tf_op jit(solution)/shard_map/all_to_all | solution.py:141
  130.8 26.9 %reduce-scatter.2.cloned.1.call-done = bf16[256,768]{1,0:T(8,128)(2,1)} async-done(((bf16[2048,768]{1,0:T(8,128)(2,1)}), bf16[256,768]{1,0:T(8,128)(2,1)}) %reduce-scatter.2.cloned.1.call-update) | async-done | bytes 393232 | tf_op jit(solution)/shard_map/reduce_scatter | solution.py:132
  157.7 1.3 collective-permute-start.10
  159.0 11.2 %all-to-all-done = bf16[8,384,512]{1,2,0:T(8,128)(2,1)S(1)} async-done(((bf16[8,384,512]{1,2,0:T(8,128)(2,1)}), bf16[8,384,512]{1,2,0:T(8,128)(2,1)S(1)}, u32[]{:S(2)}, u32[]{:S(2)}) %all-to-all-start) | async-done | bytes 3145760 | tf_op jit(solution)/shard_map/all_to_all | solution.py:141
  170.2 0.6 reduce_sum.34
  170.8 0.9 copy.54
  171.8 2.7 %collective-permute-done.10 = bf16[2,128,768]{2,1,0:T(8,128)(2,1)} collective-permute-done((bf16[2,128,768]{2,1,0:T(8,128)(2,1)}, bf16[2,128,768]{2,1,0:T(8,128)(2,1)}, u32[]{:S(2)}, u32[]{:S(2)}) %collective-permute-start.10) | collective-permute-done | bytes 393248 | tf_op jit(solution)/shard_map/ppermute | solution.py:134
  174.4 1.1 multiply_bitcast_fusion
  175.5 0.7 fusion.24
  176.2 0.7 slice.42
  (54 shorter events, 1.3 us)
Async XLA Ops:
  7.2 150.5 %reduce-scatter.2.cloned.1.call-start = ((), (), s32[]{:S(2)}) async-start(), calls=%async_computation.2 | async-start | bytes 3538944 | tf_op jit(solution)/shard_map/reduce_scatter | solution.py:132
  9.7 5.5 %collective-permute-start = (bf16[128,768]{1,0:T(8,128)(2,1)S(1)}, bf16[128,768]{1,0:T(8,128)(2,1)S(1)}, u32[]{:S(2)}, u32[]{:S(2)}) collective-permute-start(bf16[128,768]{1,0:T(8,128)(2,1)S(1)} %constant_dynamic-update-slice_fusion), channel_id=1, source_target_pairs={{0,128},{128,0},{1,129},{129,1},{2,130},{130,2},{3,131},{131,3},{4... | collective-permute-start | bytes 589832 | tf_op jit(solution)/shard_map/ppermute | solution.py:68
  15.2 14.8 %collective-permute-start.1 = (bf16[2,128,768]{2,1,0:T(8,128)(2,1)S(1)}, bf16[2,128,768]{2,1,0:T(8,128)(2,1)S(1)}, u32[]{:S(2)}, u32[]{:S(2)}) collective-permute-start(bf16[2,128,768]{2,1,0:T(8,128)(2,1)S(1)} %pad_maximum_fusion.1), channel_id=1, source_target_pairs={{0,16},{16,32},{32,48},{48,64},{64,80},{80,96},{96,112},{112,0},{1... | collective-permute-start | bytes 1179656 | tf_op jit(solution)/shard_map/ppermute | solution.py:77
  18.1 11.9 %collective-permute-start.2 = (bf16[2,128,768]{2,1,0:T(8,128)(2,1)S(1)}, bf16[2,128,768]{2,1,0:T(8,128)(2,1)S(1)}, u32[]{:S(2)}, u32[]{:S(2)}) collective-permute-start(bf16[2,128,768]{2,1,0:T(8,128)(2,1)S(1)} %pad_maximum_fusion.1), channel_id=1, source_target_pairs={{0,112},{16,0},{32,16},{48,32},{64,48},{80,64},{96,80},{112,96},{1... | collective-permute-start | bytes 1179656 | tf_op jit(solution)/shard_map/ppermute | solution.py:80
  24.1 38.9 %copy-start.6 = (bf16[384,512]{1,0:T(8,128)(2,1)S(1)}, bf16[384,512]{1,0:T(8,128)(2,1)}, u32[]{:S(2)}) copy-start(bf16[384,512]{1,0:T(8,128)(2,1)} %param.15) | copy-start | bytes 1179652
  30.1 9.8 %collective-permute-start.3 = (bf16[2,128,768]{2,1,0:T(8,128)(2,1)S(1)}, bf16[2,128,768]{2,1,0:T(8,128)(2,1)S(1)}, u32[]{:S(2)}, u32[]{:S(2)}) collective-permute-start(bf16[2,128,768]{2,1,0:T(8,128)(2,1)S(1)} %collective-permute-done.1), channel_id=1, source_target_pairs={{0,16},{16,32},{32,48},{48,64},{64,80},{80,96},{96,112},{112,0},{1... | collective-permute-start | bytes 1179656 | tf_op jit(solution)/shard_map/ppermute | solution.py:77
  30.1 9.8 %collective-permute-start.4 = (bf16[2,128,768]{2,1,0:T(8,128)(2,1)S(1)}, bf16[2,128,768]{2,1,0:T(8,128)(2,1)S(1)}, u32[]{:S(2)}, u32[]{:S(2)}) collective-permute-start(bf16[2,128,768]{2,1,0:T(8,128)(2,1)S(1)} %collective-permute-done.2), channel_id=1, source_target_pairs={{0,112},{16,0},{32,16},{48,32},{64,48},{80,64},{96,80},{112,96},{1... | collective-permute-start | bytes 1179656 | tf_op jit(solution)/shard_map/ppermute | solution.py:80
  39.8 8.9 %collective-permute-start.5 = (bf16[2,128,768]{2,1,0:T(8,128)(2,1)S(1)}, bf16[2,128,768]{2,1,0:T(8,128)(2,1)S(1)}, u32[]{:S(2)}, u32[]{:S(2)}) collective-permute-start(bf16[2,128,768]{2,1,0:T(8,128)(2,1)S(1)} %collective-permute-done.3), channel_id=1, source_target_pairs={{0,16},{16,32},{32,48},{48,64},{64,80},{80,96},{96,112},{112,0},{1... | collective-permute-start | bytes 1179656 | tf_op jit(solution)/shard_map/ppermute | solution.py:77
  39.8 9.7 %collective-permute-start.6 = (bf16[2,128,768]{2,1,0:T(8,128)(2,1)S(1)}, bf16[2,128,768]{2,1,0:T(8,128)(2,1)S(1)}, u32[]{:S(2)}, u32[]{:S(2)}) collective-permute-start(bf16[2,128,768]{2,1,0:T(8,128)(2,1)S(1)} %collective-permute-done.4), channel_id=1, source_target_pairs={{0,112},{16,0},{32,16},{48,32},{64,48},{80,64},{96,80},{112,96},{1... | collective-permute-start | bytes 1179656 | tf_op jit(solution)/shard_map/ppermute | solution.py:80
  48.8 7.8 %collective-permute-start.7 = (bf16[2,128,768]{2,1,0:T(8,128)(2,1)S(1)}, bf16[2,128,768]{2,1,0:T(8,128)(2,1)S(1)}, u32[]{:S(2)}, u32[]{:S(2)}) collective-permute-start(bf16[2,128,768]{2,1,0:T(8,128)(2,1)S(1)} %collective-permute-done.5), channel_id=1, source_target_pairs={{0,16},{16,32},{32,48},{48,64},{64,80},{80,96},{96,112},{112,0},{1... | collective-permute-start | bytes 1179656 | tf_op jit(solution)/shard_map/ppermute | solution.py:77
  57.4 15.6 %collective-permute-start.8 = (bf16[8,2,128,768]{3,2,1,0:T(8,128)(2,1)}, bf16[8,2,128,768]{3,2,1,0:T(8,128)(2,1)}, u32[]{:S(2)}, u32[]{:S(2)}) collective-permute-start(bf16[8,2,128,768]{3,2,1,0:T(8,128)(2,1)} %bitcast_dynamic-update-slice_fusion), channel_id=1, source_target_pairs={{0,8},{8,0},{1,9},{9,1},{2,10},{10,2},{3,11},{11,3},{4,12},{12,4},... | collective-permute-start | bytes 9437192 | tf_op jit(solution)/shard_map/ppermute | solution.py:82
  72.8 4.5 %copy-start = (bf16[384,8,2,1,128]{0,4,2,1,3:T(8,128)(2,1)}, bf16[384,8,2,1,128]{0,4,2,1,3:T(8,128)(2,1)S(1)}, u32[]{:S(2)}) copy-start(bf16[384,8,2,1,128]{0,4,2,1,3:T(8,128)(2,1)S(1)} %copy.45) | copy-start | bytes 4718596
  73.0 4.3 %copy-start.4 = (bf16[384,8,2,1,128]{0,4,2,1,3:T(8,128)(2,1)}, bf16[384,8,2,1,128]{0,4,2,1,3:T(8,128)(2,1)S(1)}, u32[]{:S(2)}) copy-start(bf16[384,8,2,1,128]{0,4,2,1,3:T(8,128)(2,1)S(1)} %copy.44) | copy-start | bytes 4718596
  77.3 4.4 %copy-start.3 = (pred[192,8,4,384]{3,1,2,0:T(8,128)(4,1)S(1)}, pred[192,8,4,384]{3,1,2,0:T(8,128)(4,1)}, u32[]{:S(2)}) copy-start(pred[192,8,4,384]{3,1,2,0:T(8,128)(4,1)} %copy.55) | copy-start | bytes 7077892
  81.7 2.9 %copy-start.7 = (bf16[384,1,4,128]{3,0,2,1:T(8,128)(2,1)}, bf16[384,1,4,128]{3,0,2,1:T(8,128)(2,1)S(1)}, u32[]{:S(2)}) copy-start(bf16[384,1,4,128]{3,0,2,1:T(8,128)(2,1)S(1)} %copy.46) | copy-start | bytes 1179652
  84.6 1.4 copy-start.10
  84.6 1.3 copy-start.12
  88.3 2.1 %copy-start.2 = (bf16[1536,1536]{0,1:T(8,128)(2,1)}, bf16[1536,1536]{0,1:T(8,128)(2,1)S(1)}, u32[]{:S(2)}) copy-start(bf16[1536,1536]{0,1:T(8,128)(2,1)S(1)} %get-tuple-element.51) | copy-start | bytes 14155780
  91.6 6.6 %copy-start.8 = (bf16[384,1,4,128]{3,0,2,1:T(8,128)(2,1)S(1)}, bf16[384,1,4,128]{3,0,2,1:T(8,128)(2,1)}, u32[]{:S(2)}) copy-start(bf16[384,1,4,128]{3,0,2,1:T(8,128)(2,1)} %copy-done.7) | copy-start | bytes 1179652
  99.9 4.3 %copy-start.9 = (bf16[384,128]{0,1:T(8,128)(2,1)S(1)}, bf16[384,128]{0,1:T(8,128)(2,1)}, u32[]{:S(2)}) copy-start(bf16[384,128]{0,1:T(8,128)(2,1)} %fusion.13) | copy-start | bytes 294916
  99.9 4.9 %copy-start.5 = (bf16[384,8,2,1,128]{0,4,2,1,3:T(8,128)(2,1)S(1)}, bf16[384,8,2,1,128]{0,4,2,1,3:T(8,128)(2,1)}, u32[]{:S(2)}) copy-start(bf16[384,8,2,1,128]{0,4,2,1,3:T(8,128)(2,1)} %copy-done.4) | copy-start | bytes 4718596
  99.9 6.9 %slice-start = ((s8[4718592]{0:T(1024)(128)(4,1)}), s8[524288]{0:T(1024)(128)(4,1)S(1)}, s32[]{:S(2)}) async-start(s8[4718592]{0:T(1024)(128)(4,1)} %bitcast.100), calls=%async_computation.3 | async-start | bytes 1048576
  104.8 2.2 %slice-start.1 = ((s8[4718592]{0:T(1024)(128)(4,1)}), s8[4194304]{0:T(1024)(128)(4,1)S(1)}, s32[]{:S(2)}) async-start(s8[4718592]{0:T(1024)(128)(4,1)} %bitcast.100), calls=%async_computation.4 | async-start | bytes 8388608
  104.9 2.1 %copy-start.11 = (bf16[384,128]{1,0:T(8,128)(2,1)S(1)}, bf16[384,128]{1,0:T(8,128)(2,1)}, u32[]{:S(2)}) copy-start(bf16[384,128]{1,0:T(8,128)(2,1)} %get-tuple-element.57) | copy-start | bytes 294916
  104.9 2.2 %copy-start.13 = (bf16[1,1152,128]{2,1,0:T(8,128)(2,1)S(1)}, bf16[1,1152,128]{2,1,0:T(8,128)(2,1)}, u32[]{:S(2)}) copy-start(bf16[1,1152,128]{2,1,0:T(8,128)(2,1)} %param.14) | copy-start | bytes 884740
  106.7 2.9 %copy-start.1 = (bf16[384,8,2,1,128]{0,4,2,1,3:T(8,128)(2,1)S(1)}, bf16[384,8,2,1,128]{0,4,2,1,3:T(8,128)(2,1)}, u32[]{:S(2)}) copy-start(bf16[384,8,2,1,128]{0,4,2,1,3:T(8,128)(2,1)} %copy-done) | copy-start | bytes 4718596
  106.7 5.7 %collective-permute-start.9 = (bf16[2048,768]{1,0:T(8,128)(2,1)S(1)}, bf16[2048,768]{1,0:T(8,128)(2,1)S(1)}, u32[]{:S(2)}, u32[]{:S(2)}) collective-permute-start(bf16[2048,768]{1,0:T(8,128)(2,1)S(1)} %convolution_convert_fusion), channel_id=1, source_target_pairs={{0,8},{8,0},{1,9},{9,1},{2,10},{10,2},{3,11},{11,3},{4,12},{12,4},... | collective-permute-start | bytes 9437192 | tf_op jit(solution)/shard_map/ppermute | solution.py:128
  124.2 46.0 %all-to-all-start = ((bf16[8,384,512]{1,2,0:T(8,128)(2,1)}), bf16[8,384,512]{1,2,0:T(8,128)(2,1)S(1)}, u32[]{:S(2)}, u32[]{:S(2)}) async-start(bf16[8,384,512]{1,2,0:T(8,128)(2,1)} %convert_bitcast_fusion), calls=%async_computation | async-start | bytes 6291456 | tf_op jit(solution)/shard_map/all_to_all | solution.py:141
  157.7 16.7 %collective-permute-start.10 = (bf16[2,128,768]{2,1,0:T(8,128)(2,1)}, bf16[2,128,768]{2,1,0:T(8,128)(2,1)}, u32[]{:S(2)}, u32[]{:S(2)}) collective-permute-start(bf16[2,128,768]{2,1,0:T(8,128)(2,1)} %bitcast.118), channel_id=1, source_target_pairs={{0,128},{128,0},{1,129},{129,1},{2,130},{130,2},{3,131},{131,3},{4... | collective-permute-start | bytes 1179656 | tf_op jit(solution)/shard_map/ppermute | solution.py:134
Sparse Core Ops, SparseCore 0:
  114.9 42.7 reduce-scatter.1

commit v11 on v9

--- a/solution.py
+++ b/solution.py
@@ -131,9 +131,9 @@
     chip_sum = (part_own + from_peer.astype(jnp.float32)).astype(jnp.bfloat16)
     ring_sum = lax.psum_scatter(chip_sum, "z", scatter_dimension=0, tiled=True)
     ring_sum = ring_sum.reshape(2, rows, -1)
+    from_x = lax.ppermute(ring_sum, "xl", SWAP)
     keep = lax.dynamic_index_in_dim(ring_sum, x_pos, 0, False)
-    give = lax.dynamic_index_in_dim(ring_sum, 1 - x_pos, 0, False)
-    summed = keep.astype(jnp.float32) + lax.ppermute(give, "xl", SWAP).astype(jnp.float32)
+    summed = keep.astype(jnp.float32) + lax.dynamic_index_in_dim(from_x, x_pos, 0, False).astype(jnp.float32)
     input_term = contract_last(grads_cat, full_w).astype(jnp.bfloat16)
     input_term = input_term.reshape(tokens_dev, tp_count, -1).transpose(1, 0, 2)
     gathered = lax.all_to_all(input_term, "tp", 0, 0, tiled=True)

time: 181 us -> 185 us (1.022)
  waiting for transfers between devices: 62.3 us -> 66.9 us
    ppermute x1, waiting for transfers between devices: 0.01 us -> 2.94 us  [local(): from_x = lax.ppermute(ring_sum, 'xl', SWAP)]
  transfers between devices with their start and end apart: 13 -> 13, of which waited for: 8 -> 9; matrix products, arithmetic and copies ran while one was open for 19% -> 18% of each run, Pallas kernels for 0% -> 0%
where the time goes in v11:
time: 185 us; the launch traced here: 183 us
  waiting for transfers between devices  66.9 us (36%)
  local copies, waits for them, and re-layouts  28.1 us (15%)
  matrix products  28 us (15%)
  starting transfers between devices  27.6 us (15%)
  other arithmetic  17.6 us (10%)
  between operations  15.1 us (8%)
    reduce_scatter x1, waiting for transfers between devices, local(): ring_sum = lax.psum_scatter(chip_sum, 'z', scatter_dimension=0, tiled=True)  26.9 us
    ppermute x4, waiting for transfers between devices, gather_rows(): fwd = lax.ppermute(fwd, 'z', ahead)  21.6 us
    unnamed x40, local copies, waits for them, and re-layouts  11.4 us
    all_to_all x1, waiting for transfers between devices, local(): gathered = lax.all_to_all(input_term, 'tp', 0, 0, tiled=True)  11.1 us
    ppermute x3, starting transfers between devices, gather_rows(): bwd = lax.ppermute(bwd, 'z', behind)  9.38 us
    dot_general x3, matrix products, contract_last(): lax.dot_general(left, right, (((1,), (1,)), ((), ())), preferred_element_...  8.12 us
    all_to_all x1, starting transfers between devices, local(): gathered = lax.all_to_all(input_term, 'tp', 0, 0, tiled=True)  6.67 us
    convert_element_type x1, other arithmetic, head_pass(): (probs_wide * (grad_probs - row_dot) * factor).astype(jnp.bfloat16)  6.57 us
  transfers between devices with their start and end apart: 13, of which 9 were waited for; matrix products, arithmetic and copies ran while one was open for 18% of the time, Pallas kernels for 0%

profile of v11, /device:TPU:1, one launch (start us, length us, event | category | flops | bytes accessed | tf_op | source)
XLA Modules:
  0.0 183.3 jit_solution(10958040856382751276)
XLA Ops:
  7.2 0.9 constant_dynamic-update-slice_fusion.2
  8.1 0.8 constant_dynamic-update-slice_fusion.1
  8.9 0.8 constant_dynamic-update-slice_fusion
  9.7 2.1 %collective-permute-start = (bf16[128,768]{1,0:T(8,128)(2,1)S(1)}, bf16[128,768]{1,0:T(8,128)(2,1)S(1)}, u32[]{:S(2)}, u32[]{:S(2)}) collective-permute-start(bf16[128,768]{1,0:T(8,128)(2,1)S(1)} %constant_dynamic-update-slice_fusion), channel_id=1, source_target_pairs={{0,128},{128,0},{1,129},{129,1},{2,130},{130,2},{3,131},{131,3},{4... | collective-permute-start | bytes 589832 | tf_op jit(solution)/shard_map/ppermute | solution.py:68
  11.8 3.4 %collective-permute-done = bf16[128,768]{1,0:T(8,128)(2,1)S(1)} collective-permute-done((bf16[128,768]{1,0:T(8,128)(2,1)S(1)}, bf16[128,768]{1,0:T(8,128)(2,1)S(1)}, u32[]{:S(2)}, u32[]{:S(2)}) %collective-permute-start) | collective-permute-done | bytes 196640 | tf_op jit(solution)/shard_map/ppermute | solution.py:68
  15.2 2.9 %collective-permute-start.1 = (bf16[2,128,768]{2,1,0:T(8,128)(2,1)S(1)}, bf16[2,128,768]{2,1,0:T(8,128)(2,1)S(1)}, u32[]{:S(2)}, u32[]{:S(2)}) collective-permute-start(bf16[2,128,768]{2,1,0:T(8,128)(2,1)S(1)} %pad_maximum_fusion.1), channel_id=1, source_target_pairs={{0,16},{16,32},{32,48},{48,64},{64,80},{80,96},{96,112},{112,0},{1... | collective-permute-start | bytes 1179656 | tf_op jit(solution)/shard_map/ppermute | solution.py:77
  18.1 4.0 %collective-permute-start.2 = (bf16[2,128,768]{2,1,0:T(8,128)(2,1)S(1)}, bf16[2,128,768]{2,1,0:T(8,128)(2,1)S(1)}, u32[]{:S(2)}, u32[]{:S(2)}) collective-permute-start(bf16[2,128,768]{2,1,0:T(8,128)(2,1)S(1)} %pad_maximum_fusion.1), channel_id=1, source_target_pairs={{0,112},{16,0},{32,16},{48,32},{64,48},{80,64},{96,80},{112,96},{1... | collective-permute-start | bytes 1179656 | tf_op jit(solution)/shard_map/ppermute | solution.py:80
  22.2 2.0 %broadcast_in_dim.85 = bf16[8,2,128,768]{3,2,1,0:T(8,128)(2,1)} broadcast(bf16[]{:T(256)} %constant.121.clone.1), dimensions={} | broadcast | bytes 3145730 | tf_op jit(solution)/shard_map/broadcast_in_dim | solution.py:72
  24.1 0.8 bitcast_dynamic-update-slice_fusion.7
  25.0 5.1 %collective-permute-done.1 = bf16[2,128,768]{2,1,0:T(8,128)(2,1)S(1)} collective-permute-done((bf16[2,128,768]{2,1,0:T(8,128)(2,1)S(1)}, bf16[2,128,768]{2,1,0:T(8,128)(2,1)S(1)}, u32[]{:S(2)}, u32[]{:S(2)}) %collective-permute-start.1) | collective-permute-done | bytes 393248 | tf_op jit(solution)/shard_map/ppermute | solution.py:77
  30.1 2.7 %collective-permute-start.4 = (bf16[2,128,768]{2,1,0:T(8,128)(2,1)S(1)}, bf16[2,128,768]{2,1,0:T(8,128)(2,1)S(1)}, u32[]{:S(2)}, u32[]{:S(2)}) collective-permute-start(bf16[2,128,768]{2,1,0:T(8,128)(2,1)S(1)} %collective-permute-done.2), channel_id=1, source_target_pairs={{0,112},{16,0},{32,16},{48,32},{64,48},{80,64},{96,80},{112,96},{1... | collective-permute-start | bytes 1179656 | tf_op jit(solution)/shard_map/ppermute | solution.py:80
  32.7 0.8 bitcast_dynamic-update-slice_fusion.6
  33.5 0.8 bitcast_dynamic-update-slice_fusion.5
  34.3 5.5 %collective-permute-done.3 = bf16[2,128,768]{2,1,0:T(8,128)(2,1)S(1)} collective-permute-done((bf16[2,128,768]{2,1,0:T(8,128)(2,1)S(1)}, bf16[2,128,768]{2,1,0:T(8,128)(2,1)S(1)}, u32[]{:S(2)}, u32[]{:S(2)}) %collective-permute-start.3) | collective-permute-done | bytes 393248 | tf_op jit(solution)/shard_map/ppermute | solution.py:77
  39.8 2.7 %collective-permute-start.6 = (bf16[2,128,768]{2,1,0:T(8,128)(2,1)S(1)}, bf16[2,128,768]{2,1,0:T(8,128)(2,1)S(1)}, u32[]{:S(2)}, u32[]{:S(2)}) collective-permute-start(bf16[2,128,768]{2,1,0:T(8,128)(2,1)S(1)} %collective-permute-done.4), channel_id=1, source_target_pairs={{0,112},{16,0},{32,16},{48,32},{64,48},{80,64},{96,80},{112,96},{1... | collective-permute-start | bytes 1179656 | tf_op jit(solution)/shard_map/ppermute | solution.py:80
  42.5 0.8 bitcast_dynamic-update-slice_fusion.4
  43.3 0.8 bitcast_dynamic-update-slice_fusion.3
  44.1 4.7 %collective-permute-done.5 = bf16[2,128,768]{2,1,0:T(8,128)(2,1)S(1)} collective-permute-done((bf16[2,128,768]{2,1,0:T(8,128)(2,1)S(1)}, bf16[2,128,768]{2,1,0:T(8,128)(2,1)S(1)}, u32[]{:S(2)}, u32[]{:S(2)}) %collective-permute-start.5) | collective-permute-done | bytes 393248 | tf_op jit(solution)/shard_map/ppermute | solution.py:77
  48.8 0.8 bitcast_dynamic-update-slice_fusion.2
  49.5 0.8 bitcast_dynamic-update-slice_fusion.1
  50.3 6.3 %collective-permute-done.7 = bf16[2,128,768]{2,1,0:T(8,128)(2,1)S(1)} collective-permute-done((bf16[2,128,768]{2,1,0:T(8,128)(2,1)S(1)}, bf16[2,128,768]{2,1,0:T(8,128)(2,1)S(1)}, u32[]{:S(2)}, u32[]{:S(2)}) %collective-permute-start.7) | collective-permute-done | bytes 393248 | tf_op jit(solution)/shard_map/ppermute | solution.py:77
  56.6 0.8 bitcast_dynamic-update-slice_fusion
  57.4 5.0 %collective-permute-start.8 = (bf16[8,2,128,768]{3,2,1,0:T(8,128)(2,1)}, bf16[8,2,128,768]{3,2,1,0:T(8,128)(2,1)}, u32[]{:S(2)}, u32[]{:S(2)}) collective-permute-start(bf16[8,2,128,768]{3,2,1,0:T(8,128)(2,1)} %bitcast_dynamic-update-slice_fusion), channel_id=1, source_target_pairs={{0,8},{8,0},{1,9},{9,1},{2,10},{10,2},{3,11},{11,3},{4,12},{12,4},... | collective-permute-start | bytes 9437192 | tf_op jit(solution)/shard_map/ppermute | solution.py:82
  63.0 0.2 copy.40
  63.2 0.2 copy.41
  63.5 0.3 pad_add_fusion
  63.8 2.2 %broadcast_in_dim.83 = pred[4,384,1536]{1,0,2:T(4,128)(4,1)S(1)} broadcast(pred[384,1536]{0,1:T(8,128)(4,1)S(1)} %pad_add_fusion), dimensions={1,2} | broadcast | bytes 2949120 | tf_op jit(solution)/shard_map/while/body/eval_jaxpr/jit(_where)/broadcast_in_dim | solution.py:39
  66.1 2.6 %copy.47 = pred[192,8,4,384]{3,1,2,0:T(8,128)(4,1)} copy(pred[192,8,4,384]{3,2,1,0:T(4,128)(4,1)S(1)} %bitcast.93) | data formatting | bytes 4718592
  68.7 3.6 %copy.36 = bf16[384,4096]{0,1:T(8,128)(2,1)S(1)} copy(bf16[384,4096]{1,0:T(8,128)(2,1)} %param.8) | data formatting | bytes 6291456 | tf_op args[0]
  72.3 0.3 dynamic-slice_bitcast_fusion
  73.0 4.2 %fusion.25 = f32[384,768]{1,0:T(8,128)S(1)} fusion(bf16[384,2048]{0,1:T(8,128)(2,1)S(1)} %bitcast.104, bf16[2048,768]{1,0:T(8,128)(2,1)} %bitcast.17), kind=kOutput, calls=%fused_computation.61 | convolution fusion | flops 1207959552 | bytes 5898240 | tf_op jit(solution)/shard_map/dot_general | solution.py:105
  77.3 3.5 %fusion.5 = bf16[384,768]{1,0:T(8,128)(2,1)S(1)} fusion(f32[384,768]{1,0:T(8,128)S(1)} %fusion.25, bf16[384,2048]{0,1:T(8,128)(2,1)S(1)} %bitcast.94, bf16[2048,768]{1,0:T(8,128)(2,1)} %bitcast.16), kind=kOutput, calls=%fused_computation.24 | convolution fusion | flops 1208549376 | bytes 6488064 | tf_op jit(solution)/shard_map/dot_general | solution.py:104
  80.8 0.7 fusion.22
  81.7 2.9 %fusion.24 = (f32[1536]{0:T(1024)S(1)}, f32[1536,1536]{0,1:T(8,128)S(1)}) fusion(pred[1536,1536]{0,1:T(8,128)(4,1)S(1)} %bitcast.100, bf16[1536,128]{1,0:T(8,128)(2,1)S(1)} %bitcast.111, bf16[384,128]{1,0:T(8,128)(2,1)} %get-tuple-element.51, bf16[1152,128]{1,0:T(8,128)(2,1)} %bitcast.117), kind=kOutput, calls=%fused_computation.60 | convolution fusion | flops 611842560 | bytes 12589056 | tf_op jit(solution)/shard_map/while/body/eval_jaxpr/dot_general | solution.py:14
  84.6 1.3 fusion.4
  86.0 2.3 %fusion.1 = (f32[1536]{0:T(1024)S(1)}, bf16[1536,1536]{0,1:T(8,128)(2,1)S(1)}, f32[1536,1536]{1,0:T(8,128)S(1)}) fusion(f32[1536]{0:T(1024)S(1)} %fusion.4, f32[1536,1536]{0,1:T(8,128)S(1)} %get-tuple-element.58, f32[1536]{0:T(1024)S(1)} %get-tuple-element.57, bf16[1536,128]{1,0:T(8,128)(2,1)S(1)} %bitcast.109, bf16[384,128]{1,0:T(8,128)(2,1)S(1)} %copy-done.11, ...), kind=kOutput, calls=%fused_computation.4 | convolution fusion | flops 618920448 | bytes 24397824 | tf_op jit(solution)/shard_map/while/body/eval_jaxpr/dot_general | solution.py:14
  88.3 2.1 %copy-done.2 = bf16[1536,1536]{0,1:T(8,128)(2,1)} copy-done((bf16[1536,1536]{0,1:T(8,128)(2,1)}, bf16[1536,1536]{0,1:T(8,128)(2,1)S(1)}, u32[]{:S(2)}) %copy-start.2) | copy-done | bytes 4718616
  90.4 1.1 fusion.13
  91.5 6.6 %fusion.3 = bf16[1536,1536]{0,1:T(8,128)(2,1)} fusion(bf16[1536,1536]{0,1:T(8,128)(2,1)} %copy-done.2, f32[1536,1536]{1,0:T(8,128)S(1)} %get-tuple-element.59, f32[1536]{0:T(1024)S(1)} %get-tuple-element.33), kind=kLoop, calls=%fused_computation.6 | loop fusion | flops 11796480 | bytes 18880512 | tf_op jit(solution)/shard_map/while/body/eval_jaxpr/convert_element_type | solution.py:48
  98.1 1.8 fusion.10
  99.9 4.2 %convolution_convert_fusion.3 = bf16[1536,128]{1,0:T(8,128)(2,1)S(1)} fusion(bf16[1536,1536]{0,1:T(8,128)(2,1)} %fusion.3, bf16[384,128]{1,0:T(8,128)(2,1)} %get-tuple-element.51, bf16[1152,128]{1,0:T(8,128)(2,1)} %bitcast.118), kind=kOutput, calls=%fused_computation.19 | convolution fusion | flops 604962816 | bytes 5505024 | tf_op jit(solution)/shard_map/while/body/eval_jaxpr/dot_general | solution.py:49
  104.1 0.2 copy.42
  104.4 1.8 convolution_convert_fusion.1
  106.4 0.2 slice-done.1
  106.7 1.4 convolution_convert_fusion.2
  108.1 0.3 copy.43
  108.4 0.8 copy.52
  109.2 1.8 fusion.21
  111.0 0.9 collective-permute-done.9
  112.0 2.3 %add_convert_fusion = bf16[2048,768]{1,0:T(8,128)(2,1)} fusion(f32[2048,768]{1,0:T(8,128)S(1)} %fusion.21, bf16[2048,768]{1,0:T(8,128)(2,1)S(1)} %collective-permute-done.9), kind=kLoop, calls=%fused_computation.12 | loop fusion | flops 4718592 | bytes 12582912 | tf_op jit(solution)/shard_map/convert_element_type | solution.py:131
  114.4 3.3 %select_bitcast_fusion.1 = (bf16[8,2,1,128,768]{4,3,1,0,2:T(8,128)(2,1)S(1)}, bf16[8,2,1,128,768]{4,3,1,0,2:T(8,128)(2,1)S(1)}) fusion(bf16[8,2,128,768]{3,2,1,0:T(8,128)(2,1)} %bitcast_dynamic-update-slice_fusion, bf16[8,2,128,768]{3,2,1,0:T(8,128)(2,1)} %collective-permute-done.8, pred[]{:T(512)S(6)} %eq.17), kind=kLoop, calls=%fused_computation.17 | loop fusion | flops 3145728 | bytes 12582913 | tf_op jit(solution)/shard_map/stack | solution.py:85
  117.6 0.6 maximum_bitcast_fusion
  118.2 0.6 copy.44
  118.9 3.0 %convolution_convert_fusion = bf16[384,4096]{1,0:T(8,128)(2,1)S(1)} fusion(bf16[4096,768]{1,0:T(8,128)(2,1)S(1)} %bitcast.96, bf16[384,128]{0,1:T(8,128)(2,1)S(1)} %copy-done.9, bf16[384,128]{0,1:T(8,128)(2,1)S(1)} %fusion.10, bf16[384,512]{0,1:T(8,128)(2,1)S(1)} %bitcast.103), kind=kOutput, calls=%fused_computation.13 | convolution fusion | flops 2419261440 | bytes 10027008 | tf_op jit(solution)/shard_map/dot_general | solution.py:14
  121.8 2.0 %copy.51 = bf16[48,8,8,512]{3,2,0,1:T(8,128)(2,1)} copy(bf16[48,8,8,512]{3,2,1,0:T(8,128)(2,1)S(1)} %bitcast.99) | data formatting | bytes 6291456 | tf_op jit(solution)/shard_map/reshape | solution.py:138
  123.8 6.7 %all-to-all-start = ((bf16[8,384,512]{2,1,0:T(8,128)(2,1)}), bf16[8,384,512]{2,1,0:T(8,128)(2,1)S(1)}, u32[]{:S(2)}, u32[]{:S(2)}) async-start(bf16[8,384,512]{2,1,0:T(8,128)(2,1)} %bitcast.89), calls=%async_computation | async-start | bytes 6291456 | tf_op jit(solution)/shard_map/all_to_all | solution.py:139
  130.5 26.9 %reduce-scatter.2.cloned.1.call-done = bf16[256,768]{1,0:T(8,128)(2,1)} async-done(((bf16[2048,768]{1,0:T(8,128)(2,1)}), bf16[256,768]{1,0:T(8,128)(2,1)}) %reduce-scatter.2.cloned.1.call-update) | async-done | bytes 393232 | tf_op jit(solution)/shard_map/reduce_scatter | solution.py:132
  157.4 1.3 collective-permute-start.10
  158.7 11.1 %all-to-all-done = bf16[8,384,512]{2,1,0:T(8,128)(2,1)S(1)} async-done(((bf16[8,384,512]{2,1,0:T(8,128)(2,1)}), bf16[8,384,512]{2,1,0:T(8,128)(2,1)S(1)}, u32[]{:S(2)}, u32[]{:S(2)}) %all-to-all-start) | async-done | bytes 3145760 | tf_op jit(solution)/shard_map/all_to_all | solution.py:139
  169.8 1.3 reduce_sum.34
  171.1 2.9 %collective-permute-done.10 = bf16[2,128,768]{2,1,0:T(8,128)(2,1)} collective-permute-done((bf16[2,128,768]{2,1,0:T(8,128)(2,1)}, bf16[2,128,768]{2,1,0:T(8,128)(2,1)}, u32[]{:S(2)}, u32[]{:S(2)}) %collective-permute-start.10) | collective-permute-done | bytes 393248 | tf_op jit(solution)/shard_map/ppermute | solution.py:134
  174.1 1.0 multiply_bitcast_fusion
  175.0 0.7 fusion.23
  175.7 0.7 slice.42
  (53 shorter events, 1.0 us)
Async XLA Ops:
  7.2 150.2 %reduce-scatter.2.cloned.1.call-start = ((), (), s32[]{:S(2)}) async-start(), calls=%async_computation.2 | async-start | bytes 3538944 | tf_op jit(solution)/shard_map/reduce_scatter | solution.py:132
  9.7 5.5 %collective-permute-start = (bf16[128,768]{1,0:T(8,128)(2,1)S(1)}, bf16[128,768]{1,0:T(8,128)(2,1)S(1)}, u32[]{:S(2)}, u32[]{:S(2)}) collective-permute-start(bf16[128,768]{1,0:T(8,128)(2,1)S(1)} %constant_dynamic-update-slice_fusion), channel_id=1, source_target_pairs={{0,128},{128,0},{1,129},{129,1},{2,130},{130,2},{3,131},{131,3},{4... | collective-permute-start | bytes 589832 | tf_op jit(solution)/shard_map/ppermute | solution.py:68
  15.2 14.8 %collective-permute-start.1 = (bf16[2,128,768]{2,1,0:T(8,128)(2,1)S(1)}, bf16[2,128,768]{2,1,0:T(8,128)(2,1)S(1)}, u32[]{:S(2)}, u32[]{:S(2)}) collective-permute-start(bf16[2,128,768]{2,1,0:T(8,128)(2,1)S(1)} %pad_maximum_fusion.1), channel_id=1, source_target_pairs={{0,16},{16,32},{32,48},{48,64},{64,80},{80,96},{96,112},{112,0},{1... | collective-permute-start | bytes 1179656 | tf_op jit(solution)/shard_map/ppermute | solution.py:77
  18.1 11.9 %collective-permute-start.2 = (bf16[2,128,768]{2,1,0:T(8,128)(2,1)S(1)}, bf16[2,128,768]{2,1,0:T(8,128)(2,1)S(1)}, u32[]{:S(2)}, u32[]{:S(2)}) collective-permute-start(bf16[2,128,768]{2,1,0:T(8,128)(2,1)S(1)} %pad_maximum_fusion.1), channel_id=1, source_target_pairs={{0,112},{16,0},{32,16},{48,32},{64,48},{80,64},{96,80},{112,96},{1... | collective-permute-start | bytes 1179656 | tf_op jit(solution)/shard_map/ppermute | solution.py:80
  24.1 38.9 %copy-start.6 = (bf16[384,512]{1,0:T(8,128)(2,1)S(1)}, bf16[384,512]{1,0:T(8,128)(2,1)}, u32[]{:S(2)}) copy-start(bf16[384,512]{1,0:T(8,128)(2,1)} %param.15) | copy-start | bytes 1179652
  30.1 9.8 %collective-permute-start.3 = (bf16[2,128,768]{2,1,0:T(8,128)(2,1)S(1)}, bf16[2,128,768]{2,1,0:T(8,128)(2,1)S(1)}, u32[]{:S(2)}, u32[]{:S(2)}) collective-permute-start(bf16[2,128,768]{2,1,0:T(8,128)(2,1)S(1)} %collective-permute-done.1), channel_id=1, source_target_pairs={{0,16},{16,32},{32,48},{48,64},{64,80},{80,96},{96,112},{112,0},{1... | collective-permute-start | bytes 1179656 | tf_op jit(solution)/shard_map/ppermute | solution.py:77
  30.1 9.8 %collective-permute-start.4 = (bf16[2,128,768]{2,1,0:T(8,128)(2,1)S(1)}, bf16[2,128,768]{2,1,0:T(8,128)(2,1)S(1)}, u32[]{:S(2)}, u32[]{:S(2)}) collective-permute-start(bf16[2,128,768]{2,1,0:T(8,128)(2,1)S(1)} %collective-permute-done.2), channel_id=1, source_target_pairs={{0,112},{16,0},{32,16},{48,32},{64,48},{80,64},{96,80},{112,96},{1... | collective-permute-start | bytes 1179656 | tf_op jit(solution)/shard_map/ppermute | solution.py:80
  39.8 8.9 %collective-permute-start.5 = (bf16[2,128,768]{2,1,0:T(8,128)(2,1)S(1)}, bf16[2,128,768]{2,1,0:T(8,128)(2,1)S(1)}, u32[]{:S(2)}, u32[]{:S(2)}) collective-permute-start(bf16[2,128,768]{2,1,0:T(8,128)(2,1)S(1)} %collective-permute-done.3), channel_id=1, source_target_pairs={{0,16},{16,32},{32,48},{48,64},{64,80},{80,96},{96,112},{112,0},{1... | collective-permute-start | bytes 1179656 | tf_op jit(solution)/shard_map/ppermute | solution.py:77
  39.8 9.7 %collective-permute-start.6 = (bf16[2,128,768]{2,1,0:T(8,128)(2,1)S(1)}, bf16[2,128,768]{2,1,0:T(8,128)(2,1)S(1)}, u32[]{:S(2)}, u32[]{:S(2)}) collective-permute-start(bf16[2,128,768]{2,1,0:T(8,128)(2,1)S(1)} %collective-permute-done.4), channel_id=1, source_target_pairs={{0,112},{16,0},{32,16},{48,32},{64,48},{80,64},{96,80},{112,96},{1... | collective-permute-start | bytes 1179656 | tf_op jit(solution)/shard_map/ppermute | solution.py:80
  48.8 7.8 %collective-permute-start.7 = (bf16[2,128,768]{2,1,0:T(8,128)(2,1)S(1)}, bf16[2,128,768]{2,1,0:T(8,128)(2,1)S(1)}, u32[]{:S(2)}, u32[]{:S(2)}) collective-permute-start(bf16[2,128,768]{2,1,0:T(8,128)(2,1)S(1)} %collective-permute-done.5), channel_id=1, source_target_pairs={{0,16},{16,32},{32,48},{48,64},{64,80},{80,96},{96,112},{112,0},{1... | collective-permute-start | bytes 1179656 | tf_op jit(solution)/shard_map/ppermute | solution.py:77
  57.4 15.6 %collective-permute-start.8 = (bf16[8,2,128,768]{3,2,1,0:T(8,128)(2,1)}, bf16[8,2,128,768]{3,2,1,0:T(8,128)(2,1)}, u32[]{:S(2)}, u32[]{:S(2)}) collective-permute-start(bf16[8,2,128,768]{3,2,1,0:T(8,128)(2,1)} %bitcast_dynamic-update-slice_fusion), channel_id=1, source_target_pairs={{0,8},{8,0},{1,9},{9,1},{2,10},{10,2},{3,11},{11,3},{4,12},{12,4},... | collective-permute-start | bytes 9437192 | tf_op jit(solution)/shard_map/ppermute | solution.py:82
  72.8 4.5 %copy-start = (bf16[384,8,2,1,128]{0,4,2,1,3:T(8,128)(2,1)}, bf16[384,8,2,1,128]{0,4,2,1,3:T(8,128)(2,1)S(1)}, u32[]{:S(2)}) copy-start(bf16[384,8,2,1,128]{0,4,2,1,3:T(8,128)(2,1)S(1)} %copy.38) | copy-start | bytes 4718596
  73.0 4.3 %copy-start.4 = (bf16[384,8,2,1,128]{0,4,2,1,3:T(8,128)(2,1)}, bf16[384,8,2,1,128]{0,4,2,1,3:T(8,128)(2,1)S(1)}, u32[]{:S(2)}) copy-start(bf16[384,8,2,1,128]{0,4,2,1,3:T(8,128)(2,1)S(1)} %copy.37) | copy-start | bytes 4718596
  77.3 4.4 %copy-start.3 = (pred[192,8,4,384]{3,1,2,0:T(8,128)(4,1)S(1)}, pred[192,8,4,384]{3,1,2,0:T(8,128)(4,1)}, u32[]{:S(2)}) copy-start(pred[192,8,4,384]{3,1,2,0:T(8,128)(4,1)} %copy.47) | copy-start | bytes 7077892
  81.7 2.9 %copy-start.7 = (bf16[384,1,4,128]{3,0,2,1:T(8,128)(2,1)}, bf16[384,1,4,128]{3,0,2,1:T(8,128)(2,1)S(1)}, u32[]{:S(2)}) copy-start(bf16[384,1,4,128]{3,0,2,1:T(8,128)(2,1)S(1)} %copy.39) | copy-start | bytes 1179652
  84.6 1.4 copy-start.11
  84.6 1.3 copy-start.13
  88.3 2.1 %copy-start.2 = (bf16[1536,1536]{0,1:T(8,128)(2,1)}, bf16[1536,1536]{0,1:T(8,128)(2,1)S(1)}, u32[]{:S(2)}) copy-start(bf16[1536,1536]{0,1:T(8,128)(2,1)S(1)} %get-tuple-element.34) | copy-start | bytes 14155780
  91.5 6.6 %copy-start.8 = (bf16[384,1,4,128]{3,0,2,1:T(8,128)(2,1)S(1)}, bf16[384,1,4,128]{3,0,2,1:T(8,128)(2,1)}, u32[]{:S(2)}) copy-start(bf16[384,1,4,128]{3,0,2,1:T(8,128)(2,1)} %copy-done.7) | copy-start | bytes 1179652
  99.9 4.5 %copy-start.5 = (bf16[384,8,2,1,128]{0,4,2,1,3:T(8,128)(2,1)S(1)}, bf16[384,8,2,1,128]{0,4,2,1,3:T(8,128)(2,1)}, u32[]{:S(2)}) copy-start(bf16[384,8,2,1,128]{0,4,2,1,3:T(8,128)(2,1)} %copy-done.4) | copy-start | bytes 4718596
  99.9 4.5 %copy-start.9 = (bf16[384,128]{0,1:T(8,128)(2,1)S(1)}, bf16[384,128]{0,1:T(8,128)(2,1)}, u32[]{:S(2)}) copy-start(bf16[384,128]{0,1:T(8,128)(2,1)} %fusion.13) | copy-start | bytes 294916
  104.1 2.2 %slice-start = ((s8[4718592]{0:T(1024)(128)(4,1)}), s8[524288]{0:T(1024)(128)(4,1)S(1)}, s32[]{:S(2)}) async-start(s8[4718592]{0:T(1024)(128)(4,1)} %bitcast.97), calls=%async_computation.3 | async-start | bytes 1048576
  104.4 2.2 %slice-start.1 = ((s8[4718592]{0:T(1024)(128)(4,1)}), s8[4194304]{0:T(1024)(128)(4,1)S(1)}, s32[]{:S(2)}) async-start(s8[4718592]{0:T(1024)(128)(4,1)} %bitcast.97), calls=%async_computation.4 | async-start | bytes 8388608
  104.4 2.2 %copy-start.12 = (bf16[384,128]{1,0:T(8,128)(2,1)S(1)}, bf16[384,128]{1,0:T(8,128)(2,1)}, u32[]{:S(2)}) copy-start(bf16[384,128]{1,0:T(8,128)(2,1)} %get-tuple-element.52) | copy-start | bytes 294916
  104.4 2.3 %copy-start.14 = (bf16[1,1152,128]{2,1,0:T(8,128)(2,1)S(1)}, bf16[1,1152,128]{2,1,0:T(8,128)(2,1)}, u32[]{:S(2)}) copy-start(bf16[1,1152,128]{2,1,0:T(8,128)(2,1)} %param.14) | copy-start | bytes 884740
  106.2 3.0 %copy-start.1 = (bf16[384,8,2,1,128]{0,4,2,1,3:T(8,128)(2,1)S(1)}, bf16[384,8,2,1,128]{0,4,2,1,3:T(8,128)(2,1)}, u32[]{:S(2)}) copy-start(bf16[384,8,2,1,128]{0,4,2,1,3:T(8,128)(2,1)} %copy-done) | copy-start | bytes 4718596
  106.2 5.7 %collective-permute-start.9 = (bf16[2048,768]{1,0:T(8,128)(2,1)S(1)}, bf16[2048,768]{1,0:T(8,128)(2,1)S(1)}, u32[]{:S(2)}, u32[]{:S(2)}) collective-permute-start(bf16[2048,768]{1,0:T(8,128)(2,1)S(1)} %convolution_convert_fusion.1), channel_id=1, source_target_pairs={{0,8},{8,0},{1,9},{9,1},{2,10},{10,2},{3,11},{11,3},{4,12},{12,4},... | collective-permute-start | bytes 9437192 | tf_op jit(solution)/shard_map/ppermute | solution.py:128
  123.8 46.0 %all-to-all-start = ((bf16[8,384,512]{2,1,0:T(8,128)(2,1)}), bf16[8,384,512]{2,1,0:T(8,128)(2,1)S(1)}, u32[]{:S(2)}, u32[]{:S(2)}) async-start(bf16[8,384,512]{2,1,0:T(8,128)(2,1)} %bitcast.89), calls=%async_computation | async-start | bytes 6291456 | tf_op jit(solution)/shard_map/all_to_all | solution.py:139
  157.4 16.7 %copy-start.10 = (bf16[256,768]{1,0:T(8,128)(2,1)S(1)}, bf16[256,768]{1,0:T(8,128)(2,1)}, u32[]{:S(2)}) copy-start(bf16[256,768]{1,0:T(8,128)(2,1)} %reduce-scatter.2.cloned.1.call-done) | copy-start | bytes 1179652
  157.4 16.7 %collective-permute-start.10 = (bf16[2,128,768]{2,1,0:T(8,128)(2,1)}, bf16[2,128,768]{2,1,0:T(8,128)(2,1)}, u32[]{:S(2)}, u32[]{:S(2)}) collective-permute-start(bf16[2,128,768]{2,1,0:T(8,128)(2,1)} %bitcast.115), channel_id=1, source_target_pairs={{0,128},{128,0},{1,129},{129,1},{2,130},{130,2},{3,131},{131,3},{4... | collective-permute-start | bytes 1179656 | tf_op jit(solution)/shard_map/ppermute | solution.py:134
Sparse Core Ops, SparseCore 0:
  114.5 42.8 reduce-scatter.1
